TPU v7x, 512 devices: a whole 4x8x8 slice. The times are simulated.
512 devices in a mesh: dp: 128 (over y, z, core), tp: 4 (over x).
Axes of the slice: x: 4, y: 8, z: 8, core: 2. Of those that a mesh axis runs over, the one named last changes fastest.
Arguments:
- hidden: bfloat16 [2048, 2048], P('dp'), may hold values from -6 to 6
- routes: int32 [2048, 8], P('dp'), may hold values from 0 to 127, all different within a row; in each aligned block of 16 rows (0 to 15, 16 to 31, ...) at most 2 rows name the same one
- route_weights: int32 [2048, 8], P('dp'), may hold values from 1 to 65535
- w_gate: bfloat16 [128, 2048, 1024], P('dp', None, 'tp'), may hold values from -0.125 to 0.125
- w_up: bfloat16 [128, 2048, 1024], P('dp', None, 'tp'), may hold values from -0.125 to 0.125
- w_down: bfloat16 [128, 1024, 2048], P('dp', 'tp'), may hold values from -0.1875 to 0.1875
- queries: bfloat16 [1024, 8192], P('dp', 'tp'), may hold values from -480 to 480
- key_codes: bfloat16 [262144, 512], P('dp', 'tp'), may hold values from -127 to 127, as said below
- key_scales: float32 [4, 262144], P('tp', 'dp'), may hold values from 0.004 to 0.02
- cache_values: bfloat16 [262144, 512], P('dp', 'tp'), may hold values from -6 to 6
- new_keys: bfloat16 [1024, 512], P('dp', 'tp'), may hold values from -6 to 6
- new_values: bfloat16 [1024, 512], P('dp', 'tp'), may hold values from -6 to 6
- lengths: int32 [1024], P('dp'), may hold values from 1 to 2041, as said below
Outputs:
- expert_mix: bfloat16 [2048, 2048], P('dp')
- attended: bfloat16 [1024, 8192], P('dp', 'tp')
Inputs may be any that keep to these rules, and one draw needn't show every extreme that they name: `lengths`: the 8 requests of each block sum to at most 2048 positions; in every draw some block sums to exactly 2048, one of its requests holding 2048 - 7 positions. `routes`: each row names 8 different experts. Among the rows of one index of dp no expert is named more than 2 times, and in every draw some expert is named exactly 2 times by the rows of some index. `key_codes`: whole numbers.
All inputs are finite; a program needn't handle non-finite values.
Results may differ from a plain program's by a relative error of at most 0.014.
The roundings to bfloat16 on the way count: a program that leaves them out, or rounds other values in their place, can miss the bound.
Values may be sent and summed in bfloat16 or wider, within the bound.
No kernel may reach another device: no remote copies, remote signals or barrier semaphores. Data moves between devices by JAX's collectives and lax.ppermute only.
A program may use at most 64 MiB of HBM per device.

v0:
```python
import jax
import jax.numpy as jnp
from jax import lax
from jax.sharding import PartitionSpec as P

rope_base = 1000000.0


def inverse_freq(head_size):
    steps = jnp.arange(head_size // 2, dtype=jnp.float32) * (2.0 / head_size)
    return jnp.exp(-steps * jnp.log(jnp.float32(rope_base)))


def rotate(vector, angles):
    half_size = vector.shape[-1] // 2
    front_half = vector[..., :half_size]
    back_half = vector[..., half_size:]
    cosine = jnp.cos(angles)
    sine_part = jnp.sin(angles)
    return jnp.concatenate(
        [front_half * cosine - back_half * sine_part, back_half * cosine + front_half * sine_part],
        axis=-1,
    )


def attend_local(queries, codes, scales, cache_values, new_keys, new_values, lengths):
    row_count = queries.shape[0]
    cache_len = codes.shape[0]
    groups = scales.shape[0]
    head_size = codes.shape[1] // groups
    per_group = queries.shape[1] // (groups * head_size)
    request_end = jnp.cumsum(lengths)
    starts = request_end - lengths
    cache_pos = jnp.arange(cache_len, dtype=jnp.int32)
    member = (cache_pos[:, None] >= starts[None, :]) & (cache_pos[:, None] < request_end[None, :])
    offset = jnp.sum(jnp.where(member, starts[None, :], 0), axis=1)
    position = (cache_pos - offset).astype(jnp.float32)
    frequency = inverse_freq(head_size)
    cache_keys = (
        codes.astype(jnp.float32).reshape(cache_len, groups, head_size)
        * jnp.transpose(scales)[:, :, None]
    )
    cache_keys = rotate(cache_keys, position[:, None, None] * frequency[None, None, :]).astype(
        jnp.bfloat16
    )
    query_angles = lengths.astype(jnp.float32)[:, None] * frequency[None, :]
    rotated_query = queries.astype(jnp.float32).reshape(row_count, groups, per_group, head_size)
    rotated_query = rotate(rotated_query, query_angles[:, None, None, :]).astype(jnp.bfloat16)
    fresh_key = rotate(
        new_keys.astype(jnp.float32).reshape(row_count, groups, head_size), query_angles[:, None, :]
    ).astype(jnp.bfloat16)
    score_scale = head_size ** (-0.5)
    scores = (
        jnp.einsum("rgqd,cgd->rgqc", rotated_query, cache_keys, preferred_element_type=jnp.float32)
        * score_scale
    )
    own_score = (
        jnp.einsum("rgqd,rgd->rgq", rotated_query, fresh_key, preferred_element_type=jnp.float32)
        * score_scale
    )
    live_mask = jnp.transpose(member)[:, None, None, :]
    scores = jnp.where(live_mask, scores, -jnp.inf)
    peak_score = jnp.maximum(jnp.max(scores, axis=-1), own_score)
    weights = jnp.exp(scores - peak_score[..., None])
    own_weight = jnp.exp(own_score - peak_score)
    weight_sum = jnp.sum(weights, axis=-1) + own_weight
    value_rows = cache_values.reshape(cache_len, groups, head_size)
    mixture = jnp.einsum(
        "rgqc,cgd->rgqd",
        weights.astype(jnp.bfloat16),
        value_rows,
        preferred_element_type=jnp.float32,
    )
    mixture = mixture + own_weight[..., None] * new_values.astype(jnp.float32).reshape(
        row_count, groups, 1, head_size
    )
    return (
        (mixture / weight_sum[..., None])
        .reshape(row_count, groups * per_group * head_size)
        .astype(jnp.bfloat16)
    )


def expert_block(arrived, w_gate, w_up, w_down):
    arrived_shape = arrived.shape
    inputs = arrived.reshape(-1, arrived_shape[-1])
    gate_act = jnp.dot(inputs, w_gate[0], preferred_element_type=jnp.float32)
    up_act = jnp.dot(inputs, w_up[0], preferred_element_type=jnp.float32)
    hidden_act = (jax.nn.silu(gate_act) * up_act).astype(jnp.bfloat16)
    partial_value = jnp.dot(hidden_act, w_down[0], preferred_element_type=jnp.float32)
    return partial_value.reshape(arrived_shape[0], arrived_shape[1], partial_value.shape[-1])


def on_device(
    hidden,
    routes,
    route_weights,
    w_gate,
    w_up,
    w_down,
    queries,
    key_codes,
    key_scales,
    cache_values,
    new_keys,
    new_values,
    lengths,
):
    token_count = routes.shape[0]
    top_count = routes.shape[1]
    model_width = hidden.shape[1]
    experts = lax.axis_size("dp") * w_gate.shape[0]
    capacity = min(token_count, max(2, token_count * top_count * 2 // experts))
    flat_ids = routes.reshape(-1)
    onehot = (flat_ids[:, None] == jnp.arange(experts, dtype=jnp.int32)[None, :]).astype(jnp.int32)
    rank_ids = jnp.sum(onehot * (jnp.cumsum(onehot, axis=0) - 1), axis=1)
    slot_ids = flat_ids * capacity + rank_ids
    slot_grid = slot_ids.reshape(token_count, top_count)
    selector = jnp.any(
        jnp.arange(experts * capacity, dtype=jnp.int32)[:, None, None] == slot_grid[None, :, :],
        axis=2,
    ).astype(jnp.bfloat16)
    outgoing = jnp.dot(selector, hidden, preferred_element_type=jnp.float32).astype(jnp.bfloat16)
    outgoing = outgoing.reshape(experts, capacity, model_width)
    partial_value = expert_block(
        lax.all_to_all(outgoing, "dp", split_axis=0, concat_axis=0, tiled=True),
        w_gate,
        w_up,
        w_down,
    )
    summed = lax.psum(partial_value.astype(jnp.bfloat16), "tp")
    returned = lax.all_to_all(summed, "dp", split_axis=0, concat_axis=0, tiled=True)
    picked = jnp.take(returned.reshape(experts * capacity, model_width), slot_ids, axis=0)
    picked = picked.reshape(token_count, top_count, model_width)
    shares = route_weights.astype(jnp.float32)
    shares = shares / jnp.sum(shares, axis=1, keepdims=True)
    expert_mix = jnp.einsum("tk,tkd->td", shares, picked.astype(jnp.float32)).astype(jnp.bfloat16)
    attended = attend_local(
        queries, key_codes, key_scales, cache_values, new_keys, new_values, lengths
    )
    return (expert_mix, attended)


def solution(mesh):
    placed = (
        P("dp", None),
        P("dp", None),
        P("dp", None),
        P("dp", None, "tp"),
        P("dp", None, "tp"),
        P("dp", "tp", None),
        P("dp", "tp"),
        P("dp", "tp"),
        P("tp", "dp"),
        P("dp", "tp"),
        P("dp", "tp"),
        P("dp", "tp"),
        P("dp"),
    )
    return jax.shard_map(
        on_device,
        mesh=mesh,
        in_specs=placed,
        out_specs=(P("dp", None), P("dp", "tp")),
        check_vma=False,
    )
```

profile of v0, /device:TPU:1, one launch (start us, length us, event | category | flops | bytes accessed | tf_op | source)
XLA Modules:
  0.0 173.2 jit_solution(17918019356185554691)
XLA Ops:
  7.2 0.0 copy-start
  7.2 0.8 copy.26
  8.0 0.1 reshape.478
  8.1 0.1 fusion.34
  8.2 0.2 reduce_window_sum.18
  8.4 0.2 select_reduce_fusion.1
  8.6 0.1 reduce_sum.42
  8.7 0.1 fusion.33
  8.8 1.3 convolution_convert_fusion
  10.1 1.5 reshape.479
  11.6 18.5 %all-to-all-start = ((bf16[128,2,2048]{2,1,0:T(2,128)(2,1)}), bf16[128,2,2048]{2,1,0:T(2,128)(2,1)S(1)}, u32[]{:S(2)}, u32[]{:S(2)}) async-start(bf16[128,2,2048]{2,1,0:T(2,128)(2,1)} %reshape.479), calls=%async_computation | async-start | bytes 2097152 | tf_op jit(solution)/shard_map/all_to_all | solution.py:126
  30.2 0.0 all-reduce.2.cloned.1.call-start
  30.3 0.2 reduce-window.8
  30.5 0.1 select_reduce_fusion
  30.6 0.1 multiply_cosine_fusion.2
  30.7 0.1 fusion.50
  30.8 0.1 fusion.37
  30.9 0.1 fusion.35
  31.0 29.6 %all-to-all-done = bf16[128,2,2048]{2,1,0:T(2,128)(2,1)S(1)} async-done(((bf16[128,2,2048]{2,1,0:T(2,128)(2,1)}), bf16[128,2,2048]{2,1,0:T(2,128)(2,1)S(1)}, u32[]{:S(2)}, u32[]{:S(2)}) %all-to-all-start) | async-done | bytes 1048608 | tf_op jit(solution)/shard_map/all_to_all | solution.py:126
  60.6 0.4 reshape.480
  61.1 0.0 copy-start.9
  61.1 1.7 %fusion.17 = f32[256,256]{1,0:T(8,128)S(1)} fusion(bf16[256,2048]{1,0:T(8,128)(2,1)S(1)} %reshape.480, bf16[1,2048,256]{2,1,0:T(8,128)(2,1)} %param.16), kind=kOutput, calls=%fused_computation.25 | convolution fusion | flops 268435456 | bytes 2359296 | tf_op jit(solution)/shard_map/dot_general | solution.py:87
  62.8 0.0 copy-done.9
  62.8 0.4 fusion.6
  63.3 0.1 dot_general.33
  63.4 1.5 convolution_convert_fusion.1
  64.8 0.0 all-reduce.2.cloned.1.call-update
  64.9 0.1 maximum_bitcast_fusion.2
  65.0 0.9 copy-done.1
  65.9 0.3 multiply_bitcast_fusion
  66.2 4.8 %fusion.29 = (bf16[2048,64]{1,0:T(8,128)(2,1)S(1)}, bf16[2048,64]{1,0:T(8,128)(2,1)S(1)}) fusion(f32[2048,1,128]{2,0,1:T(8,128)S(1)} %multiply_bitcast_fusion, f32[64]{0:T(128)S(1)} %multiply_exponential_fusion, f32[2048]{0:T(1024)S(1)} %subtract_convert_fusion.1), kind=kLoop, calls=%fused_computation.40 | loop fusion | flops 1179648 | bytes 1581312 | tf_op jit(solution)/shard_map/concatenate | solution.py:20
  71.1 42.8 %all-reduce.2.cloned.1.call-done = bf16[128,2,2048]{2,0,1:T(8,128)(2,1)} async-done(((bf16[128,2,2048]{2,0,1:T(8,128)(2,1)}), bf16[128,2,2048]{2,0,1:T(8,128)(2,1)}) %all-reduce.2.cloned.1.call-update) | async-done | bytes 1048592 | tf_op jit(solution)/shard_map/psum | solution.py:131
  113.9 3.3 %copy.29 = bf16[128,2,2048]{2,1,0:T(2,128)(2,1)} copy(bf16[128,2,2048]{2,0,1:T(8,128)(2,1)} %all-reduce.2.cloned.1.call-done) | data formatting | bytes 2097152 | tf_op jit(solution)/shard_map/psum | solution.py:131
  117.2 16.3 %all-to-all-start.1 = ((bf16[128,2,2048]{2,1,0:T(2,128)(2,1)}), bf16[128,2,2048]{2,1,0:T(2,128)(2,1)S(1)}, u32[]{:S(2)}, u32[]{:S(2)}) async-start(bf16[128,2,2048]{2,1,0:T(2,128)(2,1)} %copy.29), calls=%async_computation.1 | async-start | bytes 2097152 | tf_op jit(solution)/shard_map/all_to_all | solution.py:132
  133.5 0.2 fusion.43
  133.7 0.5 fusion.59
  134.2 0.0 copy-start.2
  134.3 0.3 fusion.19
  134.6 0.7 copy-done.2
  135.3 0.4 fusion.10
  135.7 0.6 copy.45
  136.3 0.1 mul.239
  136.4 0.1 copy.30
  136.5 27.4 %all-to-all-done.1 = bf16[128,2,2048]{2,1,0:T(2,128)(2,1)S(1)} async-done(((bf16[128,2,2048]{2,1,0:T(2,128)(2,1)}), bf16[128,2,2048]{2,1,0:T(2,128)(2,1)S(1)}, u32[]{:S(2)}, u32[]{:S(2)}) %all-to-all-start.1) | async-done | bytes 1048608 | tf_op jit(solution)/shard_map/all_to_all | solution.py:132
  163.9 0.4 reshape.481
  164.4 0.9 gather_fusion
  165.3 0.4 fusion.26
  165.7 0.7 copy.43
  (29 shorter events, 0.2 us)
Async XLA Ops:
  7.2 56.2 %copy-start = (bf16[1,256,2048]{2,1,0:T(8,128)(2,1)S(1)}, bf16[1,256,2048]{2,1,0:T(8,128)(2,1)}, u32[]{:S(2)}) copy-start(bf16[1,256,2048]{2,1,0:T(8,128)(2,1)} %param.18) | copy-start | bytes 3145732
  11.6 18.6 %copy-start.3 = (bf16[8,2048]{1,0:T(8,128)(2,1)S(1)}, bf16[8,2048]{1,0:T(8,128)(2,1)}, u32[]{:S(2)}) copy-start(bf16[8,2048]{1,0:T(8,128)(2,1)} %param.19) | copy-start | bytes 98308
  11.6 18.6 %copy-start.8 = (s32[8]{0:T(128)S(1)}, s32[8]{0:T(128)}, u32[]{:S(2)}) copy-start(s32[8]{0:T(128)} %param.25) | copy-start | bytes 100
  11.6 19.0 %copy-start.6 = (bf16[8,128]{1,0:T(8,128)(2,1)S(1)}, bf16[8,128]{1,0:T(8,128)(2,1)}, u32[]{:S(2)}) copy-start(bf16[8,128]{1,0:T(8,128)(2,1)} %param.23) | copy-start | bytes 6148
  11.6 49.0 %all-to-all-start = ((bf16[128,2,2048]{2,1,0:T(2,128)(2,1)}), bf16[128,2,2048]{2,1,0:T(2,128)(2,1)S(1)}, u32[]{:S(2)}, u32[]{:S(2)}) async-start(bf16[128,2,2048]{2,1,0:T(2,128)(2,1)} %reshape.479), calls=%async_computation | async-start | bytes 2097152 | tf_op jit(solution)/shard_map/all_to_all | solution.py:126
  30.2 83.7 %all-reduce.2.cloned.1.call-start = ((), (), s32[]{:S(2)}) async-start(), calls=%async_computation.2 | async-start | bytes 2097152 | tf_op jit(solution)/shard_map/psum | solution.py:131
  61.1 1.8 %copy-start.9 = (bf16[1,2048,256]{2,1,0:T(8,128)(2,1)S(1)}, bf16[1,2048,256]{2,1,0:T(8,128)(2,1)}, u32[]{:S(2)}) copy-start(bf16[1,2048,256]{2,1,0:T(8,128)(2,1)} %param.17) | copy-start | bytes 3145732
  64.8 1.0 copy-start.1
  64.8 1.0 copy-start.5
  117.2 16.5 %copy-start.7 = (bf16[8,128]{1,0:T(8,128)(2,1)S(1)}, bf16[8,128]{1,0:T(8,128)(2,1)}, u32[]{:S(2)}) copy-start(bf16[8,128]{1,0:T(8,128)(2,1)} %param.24) | copy-start | bytes 6148
  117.2 46.8 %all-to-all-start.1 = ((bf16[128,2,2048]{2,1,0:T(2,128)(2,1)}), bf16[128,2,2048]{2,1,0:T(2,128)(2,1)S(1)}, u32[]{:S(2)}, u32[]{:S(2)}) async-start(bf16[128,2,2048]{2,1,0:T(2,128)(2,1)} %copy.29), calls=%async_computation.1 | async-start | bytes 2097152 | tf_op jit(solution)/shard_map/all_to_all | solution.py:132
  134.2 1.0 copy-start.2
  134.5 1.8 %copy-start.4 = (s32[16,8]{0,1:T(8,128)S(1)}, s32[16,8]{0,1:T(8,128)}, u32[]{:S(2)}) copy-start(s32[16,8]{0,1:T(8,128)} %param.15) | copy-start | bytes 1540
Sparse Core Ops, SparseCore 0:
  65.0 48.8 all-reduce.1
where the time goes:
time: 174 us; the launch traced here: 173 us
  waiting for transfers between devices  99.8 us (57%)
  starting transfers between devices  34.9 us (20%)
  between operations  14.3 us (8%)
  local copies, waits for them, and re-layouts  10.9 us (6%)
  other arithmetic  6.85 us (4%)
  matrix products  6.43 us (4%)
    psum x1, waiting for transfers between devices, on_device(): summed = lax.psum(partial_value.astype(jnp.bfloat16), 'tp')  42.8 us
    all_to_all x1, waiting for transfers between devices, on_device(): lax.all_to_all(outgoing, 'dp', split_axis=0, concat_axis=0, tiled=True)  29.6 us
    all_to_all x1, waiting for transfers between devices, on_device(): lax.all_to_all(summed, 'dp', split_axis=0, concat_axis=0, tiled=True)  27.4 us
    all_to_all x1, starting transfers between devices, on_device(): lax.all_to_all(outgoing, 'dp', split_axis=0, concat_axis=0, tiled=True)  18.5 us
    all_to_all x1, starting transfers between devices, on_device(): lax.all_to_all(summed, 'dp', split_axis=0, concat_axis=0, tiled=True)  16.3 us
    concatenate x4, other arithmetic, rotate(): jnp.concatenate([front_half * cosine - back_half * sine_part, back_half *...  5.09 us
  transfers between devices with their start and end apart: 3, of which 3 were waited for; matrix products, arithmetic and copies ran while one was open for 5% of the time, Pallas kernels for 0%

commit v1 on v0

--- a/solution.py
+++ b/solution.py
@@ -109,7 +109,10 @@
     token_count = routes.shape[0]
     top_count = routes.shape[1]
     model_width = hidden.shape[1]
-    experts = lax.axis_size("dp") * w_gate.shape[0]
+    tp_size = lax.axis_size("tp")
+    dp_size = lax.axis_size("dp")
+    slice_width = model_width // tp_size
+    experts = dp_size * w_gate.shape[0]
     capacity = min(token_count, max(2, token_count * top_count * 2 // experts))
     flat_ids = routes.reshape(-1)
     onehot = (flat_ids[:, None] == jnp.arange(experts, dtype=jnp.int32)[None, :]).astype(jnp.int32)
@@ -120,21 +123,31 @@
         jnp.arange(experts * capacity, dtype=jnp.int32)[:, None, None] == slot_grid[None, :, :],
         axis=2,
     ).astype(jnp.bfloat16)
-    outgoing = jnp.dot(selector, hidden, preferred_element_type=jnp.float32).astype(jnp.bfloat16)
-    outgoing = outgoing.reshape(experts, capacity, model_width)
-    partial_value = expert_block(
-        lax.all_to_all(outgoing, "dp", split_axis=0, concat_axis=0, tiled=True),
-        w_gate,
-        w_up,
-        w_down,
-    )
-    summed = lax.psum(partial_value.astype(jnp.bfloat16), "tp")
-    returned = lax.all_to_all(summed, "dp", split_axis=0, concat_axis=0, tiled=True)
-    picked = jnp.take(returned.reshape(experts * capacity, model_width), slot_ids, axis=0)
-    picked = picked.reshape(token_count, top_count, model_width)
+    tp_index = lax.axis_index("tp")
+    own_cols = lax.dynamic_slice_in_dim(hidden, tp_index * slice_width, slice_width, axis=1)
+    outgoing = jnp.dot(selector, own_cols, preferred_element_type=jnp.float32).astype(jnp.bfloat16)
+    outgoing = outgoing.reshape(experts, capacity, slice_width)
+    arrived = lax.all_to_all(outgoing, "dp", split_axis=0, concat_axis=0, tiled=True)
+    arrived = lax.all_gather(arrived, "tp", axis=0, tiled=False)
+    slots = dp_size * capacity
+    arrived = arrived.reshape(tp_size, slots, slice_width)
+    gate_w = w_gate[0].reshape(tp_size, slice_width, w_gate.shape[2])
+    up_w = w_up[0].reshape(tp_size, slice_width, w_up.shape[2])
+    gate_act = jnp.einsum("tsd,tdh->sh", arrived, gate_w, preferred_element_type=jnp.float32)
+    up_act = jnp.einsum("tsd,tdh->sh", arrived, up_w, preferred_element_type=jnp.float32)
+    hidden_act = (jax.nn.silu(gate_act) * up_act).astype(jnp.bfloat16)
+    partial_value = jnp.dot(hidden_act, w_down[0], preferred_element_type=jnp.float32)
+    partial_value = partial_value.astype(jnp.bfloat16).reshape(slots, tp_size, slice_width)
+    gathered = lax.all_to_all(partial_value, "tp", split_axis=1, concat_axis=1, tiled=True)
+    expert_out = jnp.sum(gathered.astype(jnp.float32), axis=1).astype(jnp.bfloat16)
+    expert_out = expert_out.reshape(dp_size, capacity, slice_width)
+    returned = lax.all_to_all(expert_out, "dp", split_axis=0, concat_axis=0, tiled=True)
+    picked = jnp.take(returned.reshape(experts * capacity, slice_width), slot_ids, axis=0)
+    picked = picked.reshape(token_count, top_count, slice_width)
     shares = route_weights.astype(jnp.float32)
     shares = shares / jnp.sum(shares, axis=1, keepdims=True)
-    expert_mix = jnp.einsum("tk,tkd->td", shares, picked.astype(jnp.float32)).astype(jnp.bfloat16)
+    mix_cols = jnp.einsum("tk,tkd->td", shares, picked.astype(jnp.float32)).astype(jnp.bfloat16)
+    expert_mix = lax.all_gather(mix_cols, "tp", axis=1, tiled=True)
     attended = attend_local(
         queries, key_codes, key_scales, cache_values, new_keys, new_values, lengths
     )

time: 174 us -> 143 us (0.82)
  the two profiles are of different devices: /device:TPU:1 before, /device:TPU:8 now
where the time goes in v1:
time: 143 us; the launch traced here: 142 us
  waiting for transfers between devices  56.8 us (40%)
  starting transfers between devices  35.1 us (25%)
  between operations  14.4 us (10%)
  blocking collectives  11.9 us (8%)
  local copies, waits for them, and re-layouts  9.56 us (7%)
  matrix products  7.53 us (5%)
  other arithmetic  7.1 us (5%)
    all_to_all x1, starting transfers between devices, on_device(): lax.all_to_all(outgoing, 'dp', split_axis=0, concat_axis=0, tiled=True)  17.4 us
    all_gather x1, waiting for transfers between devices, on_device(): arrived = lax.all_gather(arrived, 'tp', axis=0, tiled=False)  16.5 us
    all_to_all x1, starting transfers between devices, on_device(): lax.all_to_all(expert_out, 'dp', split_axis=0, concat_axis=0, tiled=True)  14.2 us
    all_to_all x1, waiting for transfers between devices, on_device(): lax.all_to_all(outgoing, 'dp', split_axis=0, concat_axis=0, tiled=True)  13.7 us
    all_to_all x1, waiting for transfers between devices, on_device(): lax.all_to_all(expert_out, 'dp', split_axis=0, concat_axis=0, tiled=True)  13.7 us
    all_to_all x1, waiting for transfers between devices, on_device(): lax.all_to_all(partial_value, 'tp', split_axis=1, concat_axis=1, tiled=True)  12.9 us
    all_gather x1, blocking collectives, on_device(): expert_mix = lax.all_gather(mix_cols, 'tp', axis=1, tiled=True)  11.9 us
    concatenate x4, other arithmetic, rotate(): jnp.concatenate([front_half * cosine - back_half * sine_part, back_half *...  5.09 us
  transfers between devices with their start and end apart: 4, of which 4 were waited for; matrix products, arithmetic and copies ran while one was open for 6% of the time, Pallas kernels for 0%

profile of v1, /device:TPU:8, one launch (start us, length us, event | category | flops | bytes accessed | tf_op | source)
XLA Modules:
  0.0 142.3 jit_solution(14156088460898718591)
XLA Ops:
  7.2 0.0 copy-start
  7.2 0.8 copy.22
  8.1 0.1 reshape.482
  8.2 0.1 fusion.37
  8.3 0.2 reduce_window_sum.18
  8.4 0.2 select_reduce_fusion.1
  8.6 0.1 reduce_sum.54
  8.7 0.1 fusion.34
  8.9 0.0 copy-start.6
  8.9 1.0 convolution_convert_fusion.1
  9.9 0.8 reshape.483
  10.7 17.4 %all-to-all-start = ((bf16[128,2,512]{2,1,0:T(2,128)(2,1)}), bf16[128,2,512]{2,1,0:T(2,128)(2,1)S(1)}, u32[]{:S(2)}, u32[]{:S(2)}) async-start(bf16[128,2,512]{2,1,0:T(2,128)(2,1)} %reshape.483), calls=%async_computation | async-start | bytes 524288 | tf_op jit(solution)/shard_map/all_to_all | solution.py:130
  28.1 0.0 all-gather.3.cloned.1.call-start
  28.2 0.2 reduce-window.8
  28.4 0.1 select_reduce_fusion
  28.6 0.1 multiply_cosine_fusion.2
  28.7 0.1 fusion.54
  28.8 0.1 copy.25
  28.9 0.1 mul.243
  29.0 0.1 fusion.38
  29.1 13.7 %all-to-all-done = bf16[128,2,512]{2,1,0:T(2,128)(2,1)S(1)} async-done(((bf16[128,2,512]{2,1,0:T(2,128)(2,1)}), bf16[128,2,512]{2,1,0:T(2,128)(2,1)S(1)}, u32[]{:S(2)}, u32[]{:S(2)}) %all-to-all-start) | async-done | bytes 262176 | tf_op jit(solution)/shard_map/all_to_all | solution.py:130
  42.8 0.7 copy-done.1
  43.5 0.0 all-gather.3.cloned.1.call-update
  43.5 0.1 maximum_bitcast_fusion.2
  43.6 0.1 fusion.40
  43.7 0.3 multiply_bitcast_fusion
  44.1 4.8 %fusion.26 = (bf16[2048,64]{1,0:T(8,128)(2,1)S(1)}, bf16[2048,64]{1,0:T(8,128)(2,1)S(1)}) fusion(f32[2048,1,128]{2,0,1:T(8,128)S(1)} %multiply_bitcast_fusion, f32[64]{0:T(128)S(1)} %multiply_exponential_fusion, f32[2048]{0:T(1024)S(1)} %subtract_convert_fusion.1), kind=kLoop, calls=%fused_computation.38 | loop fusion | flops 1179648 | bytes 1581312 | tf_op jit(solution)/shard_map/concatenate | solution.py:20
  48.9 0.5 fusion.65
  49.4 16.5 %all-gather.3.cloned.1.call-done = bf16[512,2,512]{2,1,0:T(2,128)(2,1)} async-done(((bf16[128,2,512]{2,1,0:T(2,128)(2,1)}), bf16[512,2,512]{2,1,0:T(2,128)(2,1)}) %all-gather.3.cloned.1.call-update) | async-done | bytes 1048592 | tf_op jit(solution)/shard_map/all_gather | solution.py:131
  65.9 1.5 %reshape.484 = bf16[4,256,512]{2,1,0:T(8,128)(2,1)S(1)} reshape(bf16[512,2,512]{2,1,0:T(2,128)(2,1)} %all-gather.3.cloned.1.call-done) | data formatting | bytes 2097152 | tf_op jit(solution)/shard_map/reshape | solution.py:133
  67.4 1.7 %convolution_bitcast_fusion.1 = f32[256,256]{1,0:T(8,128)S(1)} fusion(bf16[4,256,512]{2,1,0:T(8,128)(2,1)S(1)} %reshape.484, bf16[4,512,256]{2,1,0:T(8,128)(2,1)} %bitcast.111), kind=kOutput, calls=%fused_computation.14 | convolution fusion | flops 268435456 | bytes 2359296 | tf_op jit(solution)/shard_map/tsd,tdh->sh/dot_general | solution.py:136
  69.1 3.5 %convolution_convert_fusion = bf16[256,2048]{1,0:T(8,128)(2,1)} fusion(bf16[4,256,512]{2,1,0:T(8,128)(2,1)S(1)} %reshape.484, bf16[4,512,256]{2,1,0:T(8,128)(2,1)S(1)} %bitcast.109, bf16[1,256,2048]{2,1,0:T(8,128)(2,1)} %param.18, f32[256,256]{1,0:T(8,128)S(1)} %convolution_bitcast_fusion.1), kind=kOutput, calls=%fused_computation.1 | convolution fusion | flops 537788416 | bytes 4456448 | tf_op jit(solution)/shard_map/dot_general | solution.py:139
  72.6 2.4 %copy.38 = bf16[32,4,8,512]{3,2,0,1:T(8,128)(2,1)} copy(bf16[32,4,8,512]{3,2,1,0:T(8,128)(2,1)} %bitcast.112) | data formatting | bytes 2097152 | tf_op jit(solution)/shard_map/reshape | solution.py:140
  74.9 3.5 %all-to-all-start.1 = ((bf16[256,4,512]{2,0,1:T(8,128)(2,1)}), bf16[256,4,512]{2,0,1:T(8,128)(2,1)S(1)}, u32[]{:S(2)}, u32[]{:S(2)}) async-start(bf16[256,4,512]{2,0,1:T(8,128)(2,1)} %bitcast.110), calls=%async_computation.1 | async-start | bytes 2097152 | tf_op jit(solution)/shard_map/all_to_all | solution.py:141
  78.5 0.2 fusion.47
  78.7 0.3 fusion.17
  79.0 12.9 %all-to-all-done.1 = bf16[256,4,512]{2,0,1:T(8,128)(2,1)S(1)} async-done(((bf16[256,4,512]{2,0,1:T(8,128)(2,1)}), bf16[256,4,512]{2,0,1:T(8,128)(2,1)S(1)}, u32[]{:S(2)}, u32[]{:S(2)}) %all-to-all-start.1) | async-done | bytes 1048608 | tf_op jit(solution)/shard_map/all_to_all | solution.py:141
  91.8 0.2 reduce_sum.55
  92.1 0.8 reshape.486
  92.9 14.2 %all-to-all-start.2 = ((bf16[128,2,512]{2,1,0:T(2,128)(2,1)}), bf16[128,2,512]{2,1,0:T(2,128)(2,1)S(1)}, u32[]{:S(2)}, u32[]{:S(2)}) async-start(bf16[128,2,512]{2,1,0:T(2,128)(2,1)} %reshape.486), calls=%async_computation.2 | async-start | bytes 524288 | tf_op jit(solution)/shard_map/all_to_all | solution.py:144
  107.1 0.4 fusion.11
  107.4 0.6 copy.40
  108.1 13.7 %all-to-all-done.2 = bf16[128,2,512]{2,1,0:T(2,128)(2,1)S(1)} async-done(((bf16[128,2,512]{2,1,0:T(2,128)(2,1)}), bf16[128,2,512]{2,1,0:T(2,128)(2,1)S(1)}, u32[]{:S(2)}, u32[]{:S(2)}) %all-to-all-start.2) | async-done | bytes 262176 | tf_op jit(solution)/shard_map/all_to_all | solution.py:144
  121.8 0.1 reshape.487
  121.9 0.8 gather_fusion
  122.7 0.2 fusion.32
  123.0 11.9 %all_gather.11 = bf16[16,2048]{1,0:T(8,128)(2,1)S(1)} all-gather(bf16[16,512]{1,0:T(8,128)(2,1)S(1)} %bitcast.114), channel_id=1, replica_groups=mesh['dp'=128,'tp'=4] {'tp'}, dimensions={1}, use_global_device_ids=true | all-gather | bytes 81920 | tf_op jit(solution)/shard_map/all_gather | solution.py:150
  134.9 0.6 copy.43
  (33 shorter events, 0.2 us)
Async XLA Ops:
  7.2 61.9 %copy-start = (bf16[1,2048,256]{2,1,0:T(8,128)(2,1)S(1)}, bf16[1,2048,256]{2,1,0:T(8,128)(2,1)}, u32[]{:S(2)}) copy-start(bf16[1,2048,256]{2,1,0:T(8,128)(2,1)} %param.17) | copy-start | bytes 3145732
  7.2 21.0 %copy-start.5 = (s32[16,8]{0,1:T(8,128)S(1)}, s32[16,8]{0,1:T(8,128)}, u32[]{:S(2)}) copy-start(s32[16,8]{0,1:T(8,128)} %param.15) | copy-start | bytes 1540
  7.2 21.0 %copy-start.4 = (bf16[8,2048]{1,0:T(8,128)(2,1)S(1)}, bf16[8,2048]{1,0:T(8,128)(2,1)}, u32[]{:S(2)}) copy-start(bf16[8,2048]{1,0:T(8,128)(2,1)} %param.19) | copy-start | bytes 98308
  7.2 21.0 %copy-start.9 = (s32[8]{0:T(128)S(1)}, s32[8]{0:T(128)}, u32[]{:S(2)}) copy-start(s32[8]{0:T(128)} %param.25) | copy-start | bytes 100
  7.2 21.3 %copy-start.7 = (bf16[8,128]{1,0:T(8,128)(2,1)S(1)}, bf16[8,128]{1,0:T(8,128)(2,1)}, u32[]{:S(2)}) copy-start(bf16[8,128]{1,0:T(8,128)(2,1)} %param.23) | copy-start | bytes 6148
  7.2 21.8 %copy-start.8 = (bf16[8,128]{1,0:T(8,128)(2,1)S(1)}, bf16[8,128]{1,0:T(8,128)(2,1)}, u32[]{:S(2)}) copy-start(bf16[8,128]{1,0:T(8,128)(2,1)} %param.24) | copy-start | bytes 6148
  8.8 34.9 %copy-start.2 = (bf16[2048,128]{1,0:T(8,128)(2,1)S(1)}, bf16[2048,128]{1,0:T(8,128)(2,1)}, u32[]{:S(2)}) copy-start(bf16[2048,128]{1,0:T(8,128)(2,1)} %param.20) | copy-start | bytes 1572868
  8.9 34.9 %copy-start.6 = (f32[1,2048]{1,0:T(1,128)S(1)}, f32[1,2048]{1,0:T(1,128)}, u32[]{:S(2)}) copy-start(f32[1,2048]{1,0:T(1,128)} %param.21) | copy-start | bytes 24580
  10.7 32.1 %all-to-all-start = ((bf16[128,2,512]{2,1,0:T(2,128)(2,1)}), bf16[128,2,512]{2,1,0:T(2,128)(2,1)S(1)}, u32[]{:S(2)}, u32[]{:S(2)}) async-start(bf16[128,2,512]{2,1,0:T(2,128)(2,1)} %reshape.483), calls=%async_computation | async-start | bytes 524288 | tf_op jit(solution)/shard_map/all_to_all | solution.py:130
  28.1 37.8 %all-gather.3.cloned.1.call-start = ((), (), s32[]{:S(2)}) async-start(), calls=%async_computation.3 | async-start | bytes 1310720 | tf_op jit(solution)/shard_map/all_gather | solution.py:131
  42.8 0.7 copy-start.1
  74.9 16.9 %all-to-all-start.1 = ((bf16[256,4,512]{2,0,1:T(8,128)(2,1)}), bf16[256,4,512]{2,0,1:T(8,128)(2,1)S(1)}, u32[]{:S(2)}, u32[]{:S(2)}) async-start(bf16[256,4,512]{2,0,1:T(8,128)(2,1)} %bitcast.110), calls=%async_computation.1 | async-start | bytes 2097152 | tf_op jit(solution)/shard_map/all_to_all | solution.py:141
  92.1 15.0 %copy-start.3 = (bf16[2048,128]{1,0:T(8,128)(2,1)S(1)}, bf16[2048,128]{1,0:T(8,128)(2,1)}, u32[]{:S(2)}) copy-start(bf16[2048,128]{1,0:T(8,128)(2,1)} %param.22) | copy-start | bytes 1572868
  92.9 28.9 %all-to-all-start.2 = ((bf16[128,2,512]{2,1,0:T(2,128)(2,1)}), bf16[128,2,512]{2,1,0:T(2,128)(2,1)S(1)}, u32[]{:S(2)}, u32[]{:S(2)}) async-start(bf16[128,2,512]{2,1,0:T(2,128)(2,1)} %reshape.486), calls=%async_computation.2 | async-start | bytes 524288 | tf_op jit(solution)/shard_map/all_to_all | solution.py:144
Sparse Core Ops, SparseCore 0:
  43.7 22.2 all-gather.2

commit v2 on v1

--- a/solution.py
+++ b/solution.py
@@ -123,23 +123,19 @@
         jnp.arange(experts * capacity, dtype=jnp.int32)[:, None, None] == slot_grid[None, :, :],
         axis=2,
     ).astype(jnp.bfloat16)
-    tp_index = lax.axis_index("tp")
-    own_cols = lax.dynamic_slice_in_dim(hidden, tp_index * slice_width, slice_width, axis=1)
-    outgoing = jnp.dot(selector, own_cols, preferred_element_type=jnp.float32).astype(jnp.bfloat16)
-    outgoing = outgoing.reshape(experts, capacity, slice_width)
+    outgoing = jnp.dot(selector, hidden, preferred_element_type=jnp.float32).astype(jnp.bfloat16)
+    outgoing = outgoing.reshape(experts, capacity, model_width)
     arrived = lax.all_to_all(outgoing, "dp", split_axis=0, concat_axis=0, tiled=True)
-    arrived = lax.all_gather(arrived, "tp", axis=0, tiled=False)
     slots = dp_size * capacity
-    arrived = arrived.reshape(tp_size, slots, slice_width)
-    gate_w = w_gate[0].reshape(tp_size, slice_width, w_gate.shape[2])
-    up_w = w_up[0].reshape(tp_size, slice_width, w_up.shape[2])
-    gate_act = jnp.einsum("tsd,tdh->sh", arrived, gate_w, preferred_element_type=jnp.float32)
-    up_act = jnp.einsum("tsd,tdh->sh", arrived, up_w, preferred_element_type=jnp.float32)
+    arrived = arrived.reshape(slots, model_width)
+    gate_act = jnp.dot(arrived, w_gate[0], preferred_element_type=jnp.float32)
+    up_act = jnp.dot(arrived, w_up[0], preferred_element_type=jnp.float32)
     hidden_act = (jax.nn.silu(gate_act) * up_act).astype(jnp.bfloat16)
-    partial_value = jnp.dot(hidden_act, w_down[0], preferred_element_type=jnp.float32)
-    partial_value = partial_value.astype(jnp.bfloat16).reshape(slots, tp_size, slice_width)
-    gathered = lax.all_to_all(partial_value, "tp", split_axis=1, concat_axis=1, tiled=True)
-    expert_out = jnp.sum(gathered.astype(jnp.float32), axis=1).astype(jnp.bfloat16)
+    down_w = w_down[0].reshape(w_down.shape[1], tp_size, slice_width)
+    partial_value = jnp.einsum("sh,hcd->csd", hidden_act, down_w, preferred_element_type=jnp.float32)
+    partial_value = partial_value.astype(jnp.bfloat16)
+    gathered = lax.all_to_all(partial_value, "tp", split_axis=0, concat_axis=0, tiled=True)
+    expert_out = jnp.sum(gathered.astype(jnp.float32), axis=0).astype(jnp.bfloat16)
     expert_out = expert_out.reshape(dp_size, capacity, slice_width)
     returned = lax.all_to_all(expert_out, "dp", split_axis=0, concat_axis=0, tiled=True)
     picked = jnp.take(returned.reshape(experts * capacity, slice_width), slot_ids, axis=0)

time: 143 us -> 116 us (0.81)
  between operations: 14.4 us -> 0.95 us
  waiting for transfers between devices: 56.8 us -> 48.6 us
  starting transfers between devices: 35.1 us -> 29.4 us
    all_gather x1 -> x0, waiting for transfers between devices: 16.5 us -> none  [on_device(): arrived = lax.all_gather(arrived, 'tp', axis=0, tiled=False)]
    all_to_all x1, waiting for transfers between devices: 13.7 us -> 21.9 us  [on_device(): lax.all_to_all(outgoing, 'dp', split_axis=0, concat_axis=0, tiled=True)]
    all_to_all x1, starting transfers between devices: 14.2 us -> 7.62 us  [on_device(): lax.all_to_all(expert_out, 'dp', split_axis=0, concat_axis=0, tiled=True)]
    reshape x3 -> x2, local copies, waits for them, and re-layouts: 4.61 us -> 2.75 us  [the longest x1 1.52 us: on_device(): outgoing = outgoing.reshape(experts, capacity, model_width)]
    another operation x0 -> x1, local copies, waits for them, and re-layouts: none -> 1.6 us  [on_device(): down_w = w_down[0].reshape(w_down.shape[1], tp_size, slice_width)]
  transfers between devices with their start and end apart: 4 -> 3, of which waited for: 4 -> 3; matrix products, arithmetic and copies ran while one was open for 6% -> 9% of each run, Pallas kernels for 0% -> 0%
where the time goes in v2:
time: 116 us
  waiting for transfers between devices  48.6 us (42%)
  starting transfers between devices  29.4 us (25%)
  blocking collectives  11.9 us (10%)
  local copies, waits for them, and re-layouts  8.6 us (7%)
  matrix products  8.26 us (7%)
  other arithmetic  8.14 us (7%)
    all_to_all x1, waiting for transfers between devices, on_device(): lax.all_to_all(outgoing, 'dp', split_axis=0, concat_axis=0, tiled=True)  21.9 us
    all_to_all x1, starting transfers between devices, on_device(): lax.all_to_all(outgoing, 'dp', split_axis=0, concat_axis=0, tiled=True)  17.5 us
    all_to_all x1, waiting for transfers between devices, on_device(): lax.all_to_all(expert_out, 'dp', split_axis=0, concat_axis=0, tiled=True)  13.7 us
    all_to_all x1, waiting for transfers between devices, on_device(): lax.all_to_all(partial_value, 'tp', split_axis=0, concat_axis=0, tiled=True)  13.1 us
    all_gather x1, blocking collectives, on_device(): expert_mix = lax.all_gather(mix_cols, 'tp', axis=1, tiled=True)  11.9 us
    all_to_all x1, starting transfers between devices, on_device(): lax.all_to_all(expert_out, 'dp', split_axis=0, concat_axis=0, tiled=True)  7.62 us
    concatenate x4, other arithmetic, rotate(): jnp.concatenate([front_half * cosine - back_half * sine_part, back_half *...  5.09 us
    all_to_all x1, starting transfers between devices, on_device(): lax.all_to_all(partial_value, 'tp', split_axis=0, concat_axis=0, tiled=True)  4.29 us
  transfers between devices with their start and end apart: 3, of which 3 were waited for; matrix products, arithmetic and copies ran while one was open for 9% of the time, Pallas kernels for 0%

profile of v2, /device:TPU:8, one launch (start us, length us, event | category | flops | bytes accessed | tf_op | source)
XLA Modules:
  0.0 115.9 jit_solution(11320574703570330145)
XLA Ops:
  0.6 0.0 copy-start
  0.6 0.8 copy.21
  1.5 0.1 reshape.479
  1.6 0.1 fusion.43
  1.7 0.2 reduce_window_sum.18
  1.8 0.2 select_reduce_fusion.1
  2.0 0.1 reduce_sum.54
  2.1 0.1 fusion.40
  2.3 1.3 %convolution_convert_fusion = bf16[256,2048]{1,0:T(8,128)(2,1)S(1)} fusion(pred[256,16]{0,1:T(8,128)(4,1)S(1)} %fusion.40, bf16[16,2048]{1,0:T(8,128)(2,1)} %param.13), kind=kOutput, calls=%fused_computation.1 | convolution fusion | flops 17301504 | bytes 1118208 | tf_op jit(solution)/shard_map/dot_general | solution.py:126
  3.6 1.5 %reshape.480 = bf16[128,2,2048]{2,1,0:T(2,128)(2,1)} reshape(bf16[256,2048]{1,0:T(8,128)(2,1)S(1)} %convolution_convert_fusion) | data formatting | bytes 2097152 | tf_op jit(solution)/shard_map/reshape | solution.py:127
  5.1 0.0 copy-start.2
  5.1 17.5 %all-to-all-start = ((bf16[128,2,2048]{2,1,0:T(2,128)(2,1)}), bf16[128,2,2048]{2,1,0:T(2,128)(2,1)S(1)}, u32[]{:S(2)}, u32[]{:S(2)}) async-start(bf16[128,2,2048]{2,1,0:T(2,128)(2,1)} %reshape.480), calls=%async_computation | async-start | bytes 2097152 | tf_op jit(solution)/shard_map/all_to_all | solution.py:128
  22.7 0.0 copy-done.5
  22.7 0.2 reduce-window.8
  22.9 0.1 select_reduce_fusion
  23.0 0.0 copy-done.7
  23.1 0.1 multiply_cosine_fusion.2
  23.2 0.1 fusion.59
  23.3 0.1 copy.24
  23.4 0.0 copy-start.6
  23.4 1.6 %reshape_squeeze.3 = bf16[256,4,512]{2,1,0:T(4,128)(2,1)} reshape(bf16[1,256,2048]{2,1,0:T(8,128)(2,1)S(1)} %copy-done.2) | data formatting | bytes 2097152 | tf_op jit(solution)/shard_map/reshape;squeeze | solution.py:134
  25.0 0.1 mul.239
  25.1 0.1 maximum_bitcast_fusion.2
  25.2 0.1 fusion.46
  25.3 0.1 fusion.44
  25.4 1.4 %multiply_bitcast_fusion = f32[2048,1,128]{2,0,1:T(8,128)S(1)} fusion(bf16[2048,128]{1,0:T(8,128)(2,1)} %param.20, f32[2048]{0:T(1024)S(1)} %bitcast.108), kind=kLoop, calls=%fused_computation.30 | loop fusion | flops 524288 | bytes 1581056 | tf_op jit(solution)/shard_map/mul | solution.py:40
  26.8 4.8 %fusion.32 = (bf16[2048,64]{1,0:T(8,128)(2,1)S(1)}, bf16[2048,64]{1,0:T(8,128)(2,1)S(1)}) fusion(f32[2048,1,128]{2,0,1:T(8,128)S(1)} %multiply_bitcast_fusion, f32[64]{0:T(128)S(1)} %multiply_exponential_fusion, f32[2048]{0:T(1024)S(1)} %subtract_convert_fusion.1), kind=kLoop, calls=%fused_computation.40 | loop fusion | flops 1179648 | bytes 1581312 | tf_op jit(solution)/shard_map/concatenate | solution.py:20
  31.6 0.5 fusion.69
  32.1 21.9 %all-to-all-done = bf16[128,2,2048]{2,1,0:T(2,128)(2,1)S(1)} async-done(((bf16[128,2,2048]{2,1,0:T(2,128)(2,1)}), bf16[128,2,2048]{2,1,0:T(2,128)(2,1)S(1)}, u32[]{:S(2)}, u32[]{:S(2)}) %all-to-all-start) | async-done | bytes 1048608 | tf_op jit(solution)/shard_map/all_to_all | solution.py:128
  54.0 1.2 %reshape.481 = bf16[256,2048]{1,0:T(8,128)(2,1)} reshape(bf16[128,2,2048]{2,1,0:T(2,128)(2,1)S(1)} %all-to-all-done) | data formatting | bytes 2097152 | tf_op jit(solution)/shard_map/reshape | solution.py:130
  55.3 2.1 %fusion.18 = f32[256,256]{1,0:T(8,128)S(1)} fusion(bf16[256,2048]{1,0:T(8,128)(2,1)} %reshape.481, bf16[1,2048,256]{2,1,0:T(8,128)(2,1)} %param.16), kind=kOutput, calls=%fused_computation.26 | convolution fusion | flops 268435456 | bytes 2359296 | tf_op jit(solution)/shard_map/dot_general | solution.py:131
  57.3 3.6 %fusion.6 = bf16[4,256,512]{2,1,0:T(8,128)(2,1)} fusion(bf16[256,4,512]{2,1,0:T(4,128)(2,1)} %reshape_squeeze.3, bf16[256,2048]{1,0:T(8,128)(2,1)S(1)} %copy-done.1, bf16[1,2048,256]{2,1,0:T(8,128)(2,1)S(1)} %copy-done, f32[256,256]{1,0:T(8,128)S(1)} %fusion.18), kind=kOutput, calls=%fused_computation.12 | convolution fusion | flops 537788416 | bytes 4456448 | tf_op jit(solution)/shard_map/sh,hcd->csd/dot_general | solution.py:135
  60.9 4.3 %all-to-all-start.1 = ((bf16[4,256,512]{2,1,0:T(8,128)(2,1)}), bf16[4,256,512]{2,1,0:T(8,128)(2,1)S(1)}, u32[]{:S(2)}, u32[]{:S(2)}) async-start(bf16[4,256,512]{2,1,0:T(8,128)(2,1)} %fusion.6), calls=%async_computation.1 | async-start | bytes 2097152 | tf_op jit(solution)/shard_map/all_to_all | solution.py:137
  65.2 0.2 fusion.52
  65.4 0.3 fusion.21
  65.7 13.1 %all-to-all-done.1 = bf16[4,256,512]{2,1,0:T(8,128)(2,1)S(1)} async-done(((bf16[4,256,512]{2,1,0:T(8,128)(2,1)}), bf16[4,256,512]{2,1,0:T(8,128)(2,1)S(1)}, u32[]{:S(2)}, u32[]{:S(2)}) %all-to-all-start.1) | async-done | bytes 1048608 | tf_op jit(solution)/shard_map/all_to_all | solution.py:137
  78.8 0.2 reduce_sum.55
  79.0 0.0 copy-start.3
  79.0 0.8 reshape.482
  79.8 7.6 %all-to-all-start.2 = ((bf16[128,2,512]{2,1,0:T(2,128)(2,1)}), bf16[128,2,512]{2,1,0:T(2,128)(2,1)S(1)}, u32[]{:S(2)}, u32[]{:S(2)}) async-start(bf16[128,2,512]{2,1,0:T(2,128)(2,1)} %reshape.482), calls=%async_computation.2 | async-start | bytes 524288 | tf_op jit(solution)/shard_map/all_to_all | solution.py:140
  87.5 0.4 fusion.12
  87.8 0.6 copy.38
  88.5 13.7 %all-to-all-done.2 = bf16[128,2,512]{2,1,0:T(2,128)(2,1)S(1)} async-done(((bf16[128,2,512]{2,1,0:T(2,128)(2,1)}), bf16[128,2,512]{2,1,0:T(2,128)(2,1)S(1)}, u32[]{:S(2)}, u32[]{:S(2)}) %all-to-all-start.2) | async-done | bytes 262176 | tf_op jit(solution)/shard_map/all_to_all | solution.py:140
  102.2 0.1 reshape.483
  102.3 0.8 gather_fusion
  103.1 0.2 fusion.38
  103.4 11.9 %all_gather.3 = bf16[16,2048]{1,0:T(8,128)(2,1)S(1)} all-gather(bf16[16,512]{1,0:T(8,128)(2,1)S(1)} %bitcast.104), channel_id=1, replica_groups=mesh['dp'=128,'tp'=4] {'tp'}, dimensions={1}, use_global_device_ids=true | all-gather | bytes 81920 | tf_op jit(solution)/shard_map/all_gather | solution.py:146
  115.3 0.6 copy.41
  (30 shorter events, 0.2 us)
Async XLA Ops:
  0.6 56.7 %copy-start = (bf16[1,2048,256]{2,1,0:T(8,128)(2,1)S(1)}, bf16[1,2048,256]{2,1,0:T(8,128)(2,1)}, u32[]{:S(2)}) copy-start(bf16[1,2048,256]{2,1,0:T(8,128)(2,1)} %param.17) | copy-start | bytes 3145732
  5.1 17.6 %copy-start.5 = (s32[16,8]{0,1:T(8,128)S(1)}, s32[16,8]{0,1:T(8,128)}, u32[]{:S(2)}) copy-start(s32[16,8]{0,1:T(8,128)} %param.15) | copy-start | bytes 1540
  5.1 17.6 %copy-start.4 = (bf16[8,2048]{1,0:T(8,128)(2,1)S(1)}, bf16[8,2048]{1,0:T(8,128)(2,1)}, u32[]{:S(2)}) copy-start(bf16[8,2048]{1,0:T(8,128)(2,1)} %param.19) | copy-start | bytes 98308
  5.1 17.6 %copy-start.9 = (s32[8]{0:T(128)S(1)}, s32[8]{0:T(128)}, u32[]{:S(2)}) copy-start(s32[8]{0:T(128)} %param.25) | copy-start | bytes 100
  5.1 17.9 %copy-start.7 = (bf16[8,128]{1,0:T(8,128)(2,1)S(1)}, bf16[8,128]{1,0:T(8,128)(2,1)}, u32[]{:S(2)}) copy-start(bf16[8,128]{1,0:T(8,128)(2,1)} %param.23) | copy-start | bytes 6148
  5.1 18.3 %copy-start.2 = (bf16[1,256,2048]{2,1,0:T(8,128)(2,1)S(1)}, bf16[1,256,2048]{2,1,0:T(8,128)(2,1)}, u32[]{:S(2)}) copy-start(bf16[1,256,2048]{2,1,0:T(8,128)(2,1)} %param.18) | copy-start | bytes 3145732
  5.1 48.9 %all-to-all-start = ((bf16[128,2,2048]{2,1,0:T(2,128)(2,1)}), bf16[128,2,2048]{2,1,0:T(2,128)(2,1)S(1)}, u32[]{:S(2)}, u32[]{:S(2)}) async-start(bf16[128,2,2048]{2,1,0:T(2,128)(2,1)} %reshape.480), calls=%async_computation | async-start | bytes 2097152 | tf_op jit(solution)/shard_map/all_to_all | solution.py:128
  23.4 1.7 %copy-start.8 = (bf16[8,128]{1,0:T(8,128)(2,1)S(1)}, bf16[8,128]{1,0:T(8,128)(2,1)}, u32[]{:S(2)}) copy-start(bf16[8,128]{1,0:T(8,128)(2,1)} %param.24) | copy-start | bytes 6148
  23.4 2.0 %copy-start.6 = (f32[1,2048]{1,0:T(1,128)S(1)}, f32[1,2048]{1,0:T(1,128)}, u32[]{:S(2)}) copy-start(f32[1,2048]{1,0:T(1,128)} %param.21) | copy-start | bytes 24580
  55.3 2.1 %copy-start.1 = (bf16[256,2048]{1,0:T(8,128)(2,1)S(1)}, bf16[256,2048]{1,0:T(8,128)(2,1)}, u32[]{:S(2)}) copy-start(bf16[256,2048]{1,0:T(8,128)(2,1)} %reshape.481) | copy-start | bytes 3145732
  60.9 17.9 %all-to-all-start.1 = ((bf16[4,256,512]{2,1,0:T(8,128)(2,1)}), bf16[4,256,512]{2,1,0:T(8,128)(2,1)S(1)}, u32[]{:S(2)}, u32[]{:S(2)}) async-start(bf16[4,256,512]{2,1,0:T(8,128)(2,1)} %fusion.6), calls=%async_computation.1 | async-start | bytes 2097152 | tf_op jit(solution)/shard_map/all_to_all | solution.py:137
  79.0 8.4 %copy-start.3 = (bf16[2048,128]{1,0:T(8,128)(2,1)S(1)}, bf16[2048,128]{1,0:T(8,128)(2,1)}, u32[]{:S(2)}) copy-start(bf16[2048,128]{1,0:T(8,128)(2,1)} %param.22) | copy-start | bytes 1572868
  79.8 22.4 %all-to-all-start.2 = ((bf16[128,2,512]{2,1,0:T(2,128)(2,1)}), bf16[128,2,512]{2,1,0:T(2,128)(2,1)S(1)}, u32[]{:S(2)}, u32[]{:S(2)}) async-start(bf16[128,2,512]{2,1,0:T(2,128)(2,1)} %reshape.482), calls=%async_computation.2 | async-start | bytes 524288 | tf_op jit(solution)/shard_map/all_to_all | solution.py:140

commit v3 on v2

--- a/solution.py
+++ b/solution.py
@@ -115,22 +115,22 @@
     experts = dp_size * w_gate.shape[0]
     capacity = min(token_count, max(2, token_count * top_count * 2 // experts))
     flat_ids = routes.reshape(-1)
-    onehot = (flat_ids[:, None] == jnp.arange(experts, dtype=jnp.int32)[None, :]).astype(jnp.int32)
-    rank_ids = jnp.sum(onehot * (jnp.cumsum(onehot, axis=0) - 1), axis=1)
+    pair_count = flat_ids.shape[0]
+    pair_pos = jnp.arange(pair_count, dtype=jnp.int32)
+    same_before = (flat_ids[:, None] == flat_ids[None, :]) & (pair_pos[None, :] < pair_pos[:, None])
+    rank_ids = jnp.sum(same_before.astype(jnp.int32), axis=1)
     slot_ids = flat_ids * capacity + rank_ids
-    slot_grid = slot_ids.reshape(token_count, top_count)
-    selector = jnp.any(
-        jnp.arange(experts * capacity, dtype=jnp.int32)[:, None, None] == slot_grid[None, :, :],
-        axis=2,
-    ).astype(jnp.bfloat16)
-    outgoing = jnp.dot(selector, hidden, preferred_element_type=jnp.float32).astype(jnp.bfloat16)
-    outgoing = outgoing.reshape(experts, capacity, model_width)
+    slot_pos = jnp.arange(experts * capacity, dtype=jnp.int32)
+    slot_hit = slot_pos[:, None] == slot_ids[None, :]
+    slot_token = jnp.sum(jnp.where(slot_hit, pair_pos[None, :] // top_count, 0), axis=1)
+    slot_token = jnp.where(jnp.any(slot_hit, axis=1), slot_token, token_count)
+    padded = jnp.concatenate([hidden, jnp.zeros((1, model_width), hidden.dtype)], axis=0)
+    outgoing = padded[slot_token.reshape(experts, capacity)]
     arrived = lax.all_to_all(outgoing, "dp", split_axis=0, concat_axis=0, tiled=True)
     slots = dp_size * capacity
-    arrived = arrived.reshape(slots, model_width)
-    gate_act = jnp.dot(arrived, w_gate[0], preferred_element_type=jnp.float32)
-    up_act = jnp.dot(arrived, w_up[0], preferred_element_type=jnp.float32)
-    hidden_act = (jax.nn.silu(gate_act) * up_act).astype(jnp.bfloat16)
+    gate_act = jnp.einsum("ecd,dh->ech", arrived, w_gate[0], preferred_element_type=jnp.float32)
+    up_act = jnp.einsum("ecd,dh->ech", arrived, w_up[0], preferred_element_type=jnp.float32)
+    hidden_act = (jax.nn.silu(gate_act) * up_act).astype(jnp.bfloat16).reshape(slots, -1)
     down_w = w_down[0].reshape(w_down.shape[1], tp_size, slice_width)
     partial_value = jnp.einsum("sh,hcd->csd", hidden_act, down_w, preferred_element_type=jnp.float32)
     partial_value = partial_value.astype(jnp.bfloat16)
@@ -143,7 +143,9 @@
     shares = route_weights.astype(jnp.float32)
     shares = shares / jnp.sum(shares, axis=1, keepdims=True)
     mix_cols = jnp.einsum("tk,tkd->td", shares, picked.astype(jnp.float32)).astype(jnp.bfloat16)
-    expert_mix = lax.all_gather(mix_cols, "tp", axis=1, tiled=True)
+    spread = jnp.broadcast_to(mix_cols[:, None, :], (token_count, tp_size, slice_width))
+    expert_mix = lax.all_to_all(spread, "tp", split_axis=1, concat_axis=1, tiled=True)
+    expert_mix = expert_mix.reshape(token_count, model_width)
     attended = attend_local(
         queries, key_codes, key_scales, cache_values, new_keys, new_values, lengths
     )

time: 116 us -> 114 us (0.983)
  blocking collectives: 11.9 us -> 0 us
  waiting for transfers between devices: 48.6 us -> 54.6 us
  starting transfers between devices: 29.4 us -> 33.2 us
  matrix products: 8.26 us -> 6.84 us
  local copies, waits for them, and re-layouts: 8.6 us -> 9.89 us
    all_gather x1 -> x0, blocking collectives: 11.9 us -> none  [on_device(): expert_mix = lax.all_gather(mix_cols, 'tp', axis=1, tiled=True)]
    all_to_all x0 -> x1, waiting for transfers between devices: none -> 4.59 us  [on_device(): lax.all_to_all(spread, 'tp', split_axis=1, concat_axis=1, tiled=True)]
    all_to_all x0 -> x1, starting transfers between devices: none -> 3.28 us  [on_device(): lax.all_to_all(spread, 'tp', split_axis=1, concat_axis=1, tiled=True)]
    gather x0 -> x2, local copies, waits for them, and re-layouts: none -> 2.88 us  [on_device(): outgoing = padded[slot_token.reshape(experts, capacity)]]
    reshape x2, local copies, waits for them, and re-layouts: 2.75 us -> 0.69 us  [the longest x1 0.63 us: on_device(): expert_mix = expert_mix.reshape(token_count, model_width)]
    dot_general x1, matrix products: 3.56 us -> 1.54 us  [on_device(): jnp.einsum('sh,hcd->csd', hidden_act, down_w, preferred_element_type=jnp....]
  transfers between devices with their start and end apart: 3 -> 4, of which waited for: 3 -> 4; matrix products, arithmetic and copies ran while one was open for 9% -> 9% of each run, Pallas kernels for 0% -> 0%
where the time goes in v3:
time: 114 us; the launch traced here: 113 us
  waiting for transfers between devices  54.6 us (48%)
  starting transfers between devices  33.2 us (29%)
  local copies, waits for them, and re-layouts  9.89 us (9%)
  other arithmetic  8.01 us (7%)
  matrix products  6.84 us (6%)
    all_to_all x1, waiting for transfers between devices, on_device(): lax.all_to_all(outgoing, 'dp', split_axis=0, concat_axis=0, tiled=True)  22.2 us
    all_to_all x1, starting transfers between devices, on_device(): lax.all_to_all(outgoing, 'dp', split_axis=0, concat_axis=0, tiled=True)  18 us
    all_to_all x1, waiting for transfers between devices, on_device(): lax.all_to_all(expert_out, 'dp', split_axis=0, concat_axis=0, tiled=True)  14.7 us
    all_to_all x1, waiting for transfers between devices, on_device(): lax.all_to_all(partial_value, 'tp', split_axis=0, concat_axis=0, tiled=True)  13.1 us
    all_to_all x1, starting transfers between devices, on_device(): lax.all_to_all(expert_out, 'dp', split_axis=0, concat_axis=0, tiled=True)  7.62 us
    concatenate x4, other arithmetic, rotate(): jnp.concatenate([front_half * cosine - back_half * sine_part, back_half *...  5.09 us
    all_to_all x1, waiting for transfers between devices, on_device(): lax.all_to_all(spread, 'tp', split_axis=1, concat_axis=1, tiled=True)  4.59 us
    all_to_all x1, starting transfers between devices, on_device(): lax.all_to_all(partial_value, 'tp', split_axis=0, concat_axis=0, tiled=True)  4.29 us
  transfers between devices with their start and end apart: 4, of which 4 were waited for; matrix products, arithmetic and copies ran while one was open for 9% of the time, Pallas kernels for 0%

profile of v3, /device:TPU:8, one launch (start us, length us, event | category | flops | bytes accessed | tf_op | source)
XLA Modules:
  0.0 113.5 jit_solution(14860070322754836657)
XLA Ops:
  0.6 0.8 copy.36
  1.5 0.1 reshape.551
  1.6 0.2 convert_reduce_fusion
  1.8 0.1 fusion.33
  1.9 0.1 select_reduce_fusion
  2.0 0.1 select_n.73
  2.2 0.1 reshape.569
  2.3 0.8 concatenate.37
  3.2 1.4 %gather_fusion = bf16[256,2048]{1,0:T(8,128)(2,1)S(1)} fusion(bf16[17,2048]{1,0:T(8,128)(2,1)S(1)} %concatenate.37, s32[1024]{0:T(1024)S(1)} %pad_clamp_fusion.1), kind=kCustom, calls=%fused_computation | custom fusion | bytes 2098176 | tf_op jit(solution)/shard_map/gather | solution.py:128
  4.6 1.5 %reshape.568 = bf16[128,2,2048]{2,1,0:T(2,128)(2,1)} reshape(bf16[256,2048]{1,0:T(8,128)(2,1)S(1)} %gather_fusion) | data formatting | bytes 2097152 | tf_op jit(solution)/shard_map/gather | solution.py:128
  6.1 18.0 %all-to-all-start = ((bf16[128,2,2048]{2,1,0:T(2,128)(2,1)}), bf16[128,2,2048]{2,1,0:T(2,128)(2,1)}, u32[]{:S(2)}, u32[]{:S(2)}) async-start(bf16[128,2,2048]{2,1,0:T(2,128)(2,1)} %reshape.568), calls=%async_computation | async-start | bytes 2097152 | tf_op jit(solution)/shard_map/all_to_all | solution.py:129
  24.2 0.2 reduce-window.8
  24.4 0.1 select_reduce_fusion.1
  24.5 0.1 multiply_cosine_fusion.2
  24.6 0.1 fusion.52
  24.7 0.1 reduce_sum.63
  24.8 0.1 copy.43
  24.9 0.8 reshape_squeeze.3
  25.7 0.1 mul.243
  25.9 0.1 maximum_bitcast_fusion.2
  25.9 0.1 fusion.39
  26.0 0.1 fusion.37
  26.1 1.4 %multiply_bitcast_fusion = f32[2048,1,128]{2,0,1:T(8,128)S(1)} fusion(bf16[2048,128]{1,0:T(8,128)(2,1)} %param.20, f32[2048]{0:T(1024)S(1)} %bitcast.107), kind=kLoop, calls=%fused_computation.29 | loop fusion | flops 524288 | bytes 1581056 | tf_op jit(solution)/shard_map/mul | solution.py:40
  27.5 4.8 %fusion.31 = (bf16[2048,64]{1,0:T(8,128)(2,1)S(1)}, bf16[2048,64]{1,0:T(8,128)(2,1)S(1)}) fusion(f32[2048,1,128]{2,0,1:T(8,128)S(1)} %multiply_bitcast_fusion, f32[64]{0:T(128)S(1)} %multiply_exponential_fusion, f32[2048]{0:T(1024)S(1)} %subtract_convert_fusion.1), kind=kLoop, calls=%fused_computation.41 | loop fusion | flops 1179648 | bytes 1581312 | tf_op jit(solution)/shard_map/concatenate | solution.py:20
  32.3 0.5 fusion.59
  32.9 22.2 %all-to-all-done = bf16[128,2,2048]{2,1,0:T(2,128)(2,1)} async-done(((bf16[128,2,2048]{2,1,0:T(2,128)(2,1)}), bf16[128,2,2048]{2,1,0:T(2,128)(2,1)}, u32[]{:S(2)}, u32[]{:S(2)}) %all-to-all-start) | async-done | bytes 1048608 | tf_op jit(solution)/shard_map/all_to_all | solution.py:129
  55.1 2.0 %fusion.17 = f32[128,2,256]{2,0,1:T(8,128)S(1)} fusion(bf16[1,2048,256]{2,1,0:T(8,128)(2,1)S(1)} %copy-done, bf16[128,2,2048]{2,1,0:T(2,128)(2,1)} %all-to-all-done), kind=kOutput, calls=%fused_computation.25 | convolution fusion | flops 268435456 | bytes 2359296 | tf_op jit(solution)/shard_map/ecd,dh->ech/dot_general | solution.py:131
  57.2 2.0 %fusion.7 = bf16[128,2,256]{2,0,1:T(8,128)(2,1)S(1)} fusion(bf16[1,2048,256]{2,1,0:T(8,128)(2,1)S(1)} %copy-done.9, bf16[128,2,2048]{2,1,0:T(2,128)(2,1)} %all-to-all-done, f32[128,2,256]{2,0,1:T(8,128)S(1)} %fusion.17), kind=kOutput, calls=%fused_computation.14 | convolution fusion | flops 268828672 | bytes 2490368 | tf_op jit(solution)/shard_map/ecd,dh->ech/dot_general | solution.py:132
  59.1 0.1 copy.40
  59.3 0.1 reshape.586
  59.3 1.5 %fusion.6 = bf16[4,256,512]{2,1,0:T(8,128)(2,1)} fusion(bf16[256,256,1]{1,0,2:T(8,128)(2,1)S(1)} %reshape.586, bf16[256,4,512]{2,1,0:T(4,128)(2,1)S(1)} %reshape_squeeze.3), kind=kOutput, calls=%fused_computation.12 | convolution fusion | flops 268959744 | bytes 2228224 | tf_op jit(solution)/shard_map/sh,hcd->csd/dot_general | solution.py:135
  60.9 4.3 %all-to-all-start.1 = ((bf16[4,256,512]{2,1,0:T(8,128)(2,1)}), bf16[4,256,512]{2,1,0:T(8,128)(2,1)S(1)}, u32[]{:S(2)}, u32[]{:S(2)}) async-start(bf16[4,256,512]{2,1,0:T(8,128)(2,1)} %fusion.6), calls=%async_computation.1 | async-start | bytes 2097152 | tf_op jit(solution)/shard_map/all_to_all | solution.py:137
  65.2 0.2 fusion.45
  65.4 0.3 fusion.20
  65.6 13.1 %all-to-all-done.1 = bf16[4,256,512]{2,1,0:T(8,128)(2,1)S(1)} async-done(((bf16[4,256,512]{2,1,0:T(8,128)(2,1)}), bf16[4,256,512]{2,1,0:T(8,128)(2,1)S(1)}, u32[]{:S(2)}, u32[]{:S(2)}) %all-to-all-start.1) | async-done | bytes 1048608 | tf_op jit(solution)/shard_map/all_to_all | solution.py:137
  78.7 0.2 reduce_sum.65
  79.0 0.8 reshape.553
  79.8 7.6 %all-to-all-start.2 = ((bf16[128,2,512]{2,1,0:T(2,128)(2,1)}), bf16[128,2,512]{2,1,0:T(2,128)(2,1)S(1)}, u32[]{:S(2)}, u32[]{:S(2)}) async-start(bf16[128,2,512]{2,1,0:T(2,128)(2,1)} %reshape.553), calls=%async_computation.2 | async-start | bytes 524288 | tf_op jit(solution)/shard_map/all_to_all | solution.py:140
  87.5 14.7 %all-to-all-done.2 = bf16[128,2,512]{2,1,0:T(2,128)(2,1)S(1)} async-done(((bf16[128,2,512]{2,1,0:T(2,128)(2,1)}), bf16[128,2,512]{2,1,0:T(2,128)(2,1)S(1)}, u32[]{:S(2)}, u32[]{:S(2)}) %all-to-all-start.2) | async-done | bytes 262176 | tf_op jit(solution)/shard_map/all_to_all | solution.py:140
  102.1 0.1 reshape.554
  102.2 0.8 gather_fusion.1
  103.1 0.2 fusion.32
  103.3 0.6 broadcast_in_dim.51
  104.0 3.3 %all-to-all-start.3 = ((bf16[16,4,512]{2,0,1:T(8,128)(2,1)}), bf16[16,4,512]{2,0,1:T(8,128)(2,1)S(1)}, u32[]{:S(2)}, u32[]{:S(2)}) async-start(bf16[16,4,512]{2,0,1:T(8,128)(2,1)} %broadcast_in_dim.51), calls=%async_computation.3 | async-start | bytes 131072 | tf_op jit(solution)/shard_map/all_to_all | solution.py:147
  107.3 0.4 fusion.11
  107.6 0.6 copy.62
  108.3 4.6 %all-to-all-done.3 = bf16[16,4,512]{2,0,1:T(8,128)(2,1)S(1)} async-done(((bf16[16,4,512]{2,0,1:T(8,128)(2,1)}), bf16[16,4,512]{2,0,1:T(8,128)(2,1)S(1)}, u32[]{:S(2)}, u32[]{:S(2)}) %all-to-all-start.3) | async-done | bytes 65568 | tf_op jit(solution)/shard_map/all_to_all | solution.py:147
  112.8 0.6 copy.47
  (40 shorter events, 0.2 us)
Async XLA Ops:
  0.6 54.5 %copy-start = (bf16[1,2048,256]{2,1,0:T(8,128)(2,1)S(1)}, bf16[1,2048,256]{2,1,0:T(8,128)(2,1)}, u32[]{:S(2)}) copy-start(bf16[1,2048,256]{2,1,0:T(8,128)(2,1)} %param.16) | copy-start | bytes 3145732
  6.1 18.0 %copy-start.4 = (s32[16,8]{0,1:T(8,128)S(1)}, s32[16,8]{0,1:T(8,128)}, u32[]{:S(2)}) copy-start(s32[16,8]{0,1:T(8,128)} %param.15) | copy-start | bytes 1540
  6.1 18.1 %copy-start.3 = (bf16[8,2048]{1,0:T(8,128)(2,1)S(1)}, bf16[8,2048]{1,0:T(8,128)(2,1)}, u32[]{:S(2)}) copy-start(bf16[8,2048]{1,0:T(8,128)(2,1)} %param.19) | copy-start | bytes 98308
  6.1 18.1 %copy-start.8 = (s32[8]{0:T(128)S(1)}, s32[8]{0:T(128)}, u32[]{:S(2)}) copy-start(s32[8]{0:T(128)} %param.25) | copy-start | bytes 100
  6.1 18.4 %copy-start.6 = (bf16[8,128]{1,0:T(8,128)(2,1)S(1)}, bf16[8,128]{1,0:T(8,128)(2,1)}, u32[]{:S(2)}) copy-start(bf16[8,128]{1,0:T(8,128)(2,1)} %param.23) | copy-start | bytes 6148
  6.1 18.8 %copy-start.1 = (bf16[1,256,2048]{2,1,0:T(8,128)(2,1)S(1)}, bf16[1,256,2048]{2,1,0:T(8,128)(2,1)}, u32[]{:S(2)}) copy-start(bf16[1,256,2048]{2,1,0:T(8,128)(2,1)} %param.18) | copy-start | bytes 3145732
  6.1 49.0 %all-to-all-start = ((bf16[128,2,2048]{2,1,0:T(2,128)(2,1)}), bf16[128,2,2048]{2,1,0:T(2,128)(2,1)}, u32[]{:S(2)}, u32[]{:S(2)}) async-start(bf16[128,2,2048]{2,1,0:T(2,128)(2,1)} %reshape.568), calls=%async_computation | async-start | bytes 2097152 | tf_op jit(solution)/shard_map/all_to_all | solution.py:129
  24.9 0.9 copy-start.7
  24.9 1.2 %copy-start.5 = (f32[1,2048]{1,0:T(1,128)S(1)}, f32[1,2048]{1,0:T(1,128)}, u32[]{:S(2)}) copy-start(f32[1,2048]{1,0:T(1,128)} %param.21) | copy-start | bytes 24580
  55.1 2.0 %copy-start.9 = (bf16[1,2048,256]{2,1,0:T(8,128)(2,1)S(1)}, bf16[1,2048,256]{2,1,0:T(8,128)(2,1)}, u32[]{:S(2)}) copy-start(bf16[1,2048,256]{2,1,0:T(8,128)(2,1)} %param.17) | copy-start | bytes 3145732
  60.9 17.9 %all-to-all-start.1 = ((bf16[4,256,512]{2,1,0:T(8,128)(2,1)}), bf16[4,256,512]{2,1,0:T(8,128)(2,1)S(1)}, u32[]{:S(2)}, u32[]{:S(2)}) async-start(bf16[4,256,512]{2,1,0:T(8,128)(2,1)} %fusion.6), calls=%async_computation.1 | async-start | bytes 2097152 | tf_op jit(solution)/shard_map/all_to_all | solution.py:137
  79.8 22.4 %all-to-all-start.2 = ((bf16[128,2,512]{2,1,0:T(2,128)(2,1)}), bf16[128,2,512]{2,1,0:T(2,128)(2,1)S(1)}, u32[]{:S(2)}, u32[]{:S(2)}) async-start(bf16[128,2,512]{2,1,0:T(2,128)(2,1)} %reshape.553), calls=%async_computation.2 | async-start | bytes 524288 | tf_op jit(solution)/shard_map/all_to_all | solution.py:140
  87.4 19.8 %copy-start.2 = (bf16[2048,128]{1,0:T(8,128)(2,1)S(1)}, bf16[2048,128]{1,0:T(8,128)(2,1)}, u32[]{:S(2)}) copy-start(bf16[2048,128]{1,0:T(8,128)(2,1)} %param.22) | copy-start | bytes 1572868
  104.0 8.9 %all-to-all-start.3 = ((bf16[16,4,512]{2,0,1:T(8,128)(2,1)}), bf16[16,4,512]{2,0,1:T(8,128)(2,1)S(1)}, u32[]{:S(2)}, u32[]{:S(2)}) async-start(bf16[16,4,512]{2,0,1:T(8,128)(2,1)} %broadcast_in_dim.51), calls=%async_computation.3 | async-start | bytes 131072 | tf_op jit(solution)/shard_map/all_to_all | solution.py:147

commit v4 on v3

--- a/solution.py
+++ b/solution.py
@@ -121,11 +121,16 @@
     rank_ids = jnp.sum(same_before.astype(jnp.int32), axis=1)
     slot_ids = flat_ids * capacity + rank_ids
     slot_pos = jnp.arange(experts * capacity, dtype=jnp.int32)
+    token_of_pair = pair_pos // top_count
+    token_pos = jnp.arange(token_count, dtype=jnp.int32)
     slot_hit = slot_pos[:, None] == slot_ids[None, :]
-    slot_token = jnp.sum(jnp.where(slot_hit, pair_pos[None, :] // top_count, 0), axis=1)
+    slot_token = jnp.sum(jnp.where(slot_hit, token_of_pair[None, :], 0), axis=1)
     slot_token = jnp.where(jnp.any(slot_hit, axis=1), slot_token, token_count)
-    padded = jnp.concatenate([hidden, jnp.zeros((1, model_width), hidden.dtype)], axis=0)
-    outgoing = padded[slot_token.reshape(experts, capacity)]
+    selector = (slot_token[:, None] == token_pos[None, :]).astype(hidden.dtype)
+    selector = selector.reshape(experts, capacity, token_count)
+    outgoing = jnp.einsum(
+        "ect,td->ecd", selector, hidden, preferred_element_type=jnp.float32
+    ).astype(hidden.dtype)
     arrived = lax.all_to_all(outgoing, "dp", split_axis=0, concat_axis=0, tiled=True)
     slots = dp_size * capacity
     gate_act = jnp.einsum("ecd,dh->ech", arrived, w_gate[0], preferred_element_type=jnp.float32)

time: 114 us -> 114 us (level)
  local copies, waits for them, and re-layouts: 9.89 us -> 8.2 us
  matrix products: 6.84 us -> 8.17 us
    gather x2 -> x0, local copies, waits for them, and re-layouts: 2.88 us -> none  [on_device(): outgoing = padded[slot_token.reshape(experts, capacity)]]
    convert_element_type x0 -> x1, local copies, waits for them, and re-layouts: none -> 2.11 us  [on_device(): outgoing = jnp.einsum('ect,td->ecd', selector, hidden, preferred_element_...]
    dot_general x0 -> x1, matrix products: none -> 1.33 us  [on_device(): jnp.einsum('ect,td->ecd', selector, hidden, preferred_element_type=jnp.fl...]
where the time goes in v4:
time: 114 us; the launch traced here: 113 us
  waiting for transfers between devices  54.6 us (48%)
  starting transfers between devices  33.2 us (29%)
  local copies, waits for them, and re-layouts  8.2 us (7%)
  matrix products  8.17 us (7%)
  other arithmetic  7.99 us (7%)
    all_to_all x1, waiting for transfers between devices, on_device(): lax.all_to_all(outgoing, 'dp', split_axis=0, concat_axis=0, tiled=True)  22.2 us
    all_to_all x1, starting transfers between devices, on_device(): lax.all_to_all(outgoing, 'dp', split_axis=0, concat_axis=0, tiled=True)  18 us
    all_to_all x1, waiting for transfers between devices, on_device(): lax.all_to_all(expert_out, 'dp', split_axis=0, concat_axis=0, tiled=True)  14.7 us
    all_to_all x1, waiting for transfers between devices, on_device(): lax.all_to_all(partial_value, 'tp', split_axis=0, concat_axis=0, tiled=True)  13.1 us
    all_to_all x1, starting transfers between devices, on_device(): lax.all_to_all(expert_out, 'dp', split_axis=0, concat_axis=0, tiled=True)  7.62 us
    concatenate x4, other arithmetic, rotate(): jnp.concatenate([front_half * cosine - back_half * sine_part, back_half *...  5.09 us
    all_to_all x1, waiting for transfers between devices, on_device(): lax.all_to_all(spread, 'tp', split_axis=1, concat_axis=1, tiled=True)  4.59 us
    all_to_all x1, starting transfers between devices, on_device(): lax.all_to_all(partial_value, 'tp', split_axis=0, concat_axis=0, tiled=True)  4.3 us
  transfers between devices with their start and end apart: 4, of which 4 were waited for; matrix products, arithmetic and copies ran while one was open for 9% of the time, Pallas kernels for 0%

profile of v4, /device:TPU:8, one launch (start us, length us, event | category | flops | bytes accessed | tf_op | source)
XLA Modules:
  0.0 113.1 jit_solution(512758518221204367)
XLA Ops:
  0.6 0.0 copy-start
  0.6 0.8 copy.40
  1.5 0.1 reshape.514
  1.6 0.2 convert_reduce_fusion
  1.8 0.1 fusion.33
  1.9 0.1 select_reduce_fusion
  2.0 0.1 select_n.57
  2.2 0.1 copy.42
  2.2 1.3 %convolution_convert_fusion = bf16[128,2,2048]{2,0,1:T(8,128)(2,1)S(1)} fusion(bf16[16,2048]{1,0:T(8,128)(2,1)} %param.13, s32[128,2]{0,1:T(2,128)S(1)} %copy.42), kind=kOutput, calls=%fused_computation.1 | convolution fusion | flops 17305600 | bytes 1115136 | tf_op jit(solution)/shard_map/ect,td->ecd/dot_general | solution.py:131
  3.6 2.1 %copy.43 = bf16[128,2,2048]{2,1,0:T(2,128)(2,1)} copy(bf16[128,2,2048]{2,0,1:T(8,128)(2,1)S(1)} %convolution_convert_fusion) | data formatting | bytes 2097152 | tf_op jit(solution)/shard_map/convert_element_type | solution.py:133
  5.7 18.0 %all-to-all-start = ((bf16[128,2,2048]{2,1,0:T(2,128)(2,1)}), bf16[128,2,2048]{2,1,0:T(2,128)(2,1)}, u32[]{:S(2)}, u32[]{:S(2)}) async-start(bf16[128,2,2048]{2,1,0:T(2,128)(2,1)} %copy.43), calls=%async_computation | async-start | bytes 2097152 | tf_op jit(solution)/shard_map/all_to_all | solution.py:134
  23.8 0.2 reduce-window.8
  24.0 0.1 select_reduce_fusion.1
  24.1 0.1 multiply_cosine_fusion.2
  24.2 0.1 fusion.54
  24.3 0.1 reduce_sum.63
  24.4 0.1 copy.49
  24.5 0.8 reshape_squeeze.3
  25.3 0.1 mul.243
  25.5 0.1 maximum_bitcast_fusion.2
  25.5 0.1 fusion.40
  25.6 0.1 fusion.38
  25.7 1.4 %multiply_bitcast_fusion = f32[2048,1,128]{2,0,1:T(8,128)S(1)} fusion(bf16[2048,128]{1,0:T(8,128)(2,1)} %param.20, f32[2048]{0:T(1024)S(1)} %bitcast.108), kind=kLoop, calls=%fused_computation.29 | loop fusion | flops 524288 | bytes 1581056 | tf_op jit(solution)/shard_map/mul | solution.py:40
  27.1 4.8 %fusion.31 = (bf16[2048,64]{1,0:T(8,128)(2,1)S(1)}, bf16[2048,64]{1,0:T(8,128)(2,1)S(1)}) fusion(f32[2048,1,128]{2,0,1:T(8,128)S(1)} %multiply_bitcast_fusion, f32[64]{0:T(128)S(1)} %multiply_exponential_fusion, f32[2048]{0:T(1024)S(1)} %subtract_convert_fusion.1), kind=kLoop, calls=%fused_computation.41 | loop fusion | flops 1179648 | bytes 1581312 | tf_op jit(solution)/shard_map/concatenate | solution.py:20
  31.9 0.5 fusion.61
  32.5 22.2 %all-to-all-done = bf16[128,2,2048]{2,1,0:T(2,128)(2,1)} async-done(((bf16[128,2,2048]{2,1,0:T(2,128)(2,1)}), bf16[128,2,2048]{2,1,0:T(2,128)(2,1)}, u32[]{:S(2)}, u32[]{:S(2)}) %all-to-all-start) | async-done | bytes 1048608 | tf_op jit(solution)/shard_map/all_to_all | solution.py:134
  54.7 2.0 %fusion.17 = f32[128,2,256]{2,0,1:T(8,128)S(1)} fusion(bf16[1,2048,256]{2,1,0:T(8,128)(2,1)S(1)} %copy-done, bf16[128,2,2048]{2,1,0:T(2,128)(2,1)} %all-to-all-done), kind=kOutput, calls=%fused_computation.25 | convolution fusion | flops 268435456 | bytes 2359296 | tf_op jit(solution)/shard_map/ecd,dh->ech/dot_general | solution.py:136
  56.8 2.0 %fusion.7 = bf16[128,2,256]{2,0,1:T(8,128)(2,1)S(1)} fusion(bf16[1,2048,256]{2,1,0:T(8,128)(2,1)S(1)} %copy-done.9, bf16[128,2,2048]{2,1,0:T(2,128)(2,1)} %all-to-all-done, f32[128,2,256]{2,0,1:T(8,128)S(1)} %fusion.17), kind=kOutput, calls=%fused_computation.14 | convolution fusion | flops 268828672 | bytes 2490368 | tf_op jit(solution)/shard_map/ecd,dh->ech/dot_general | solution.py:137
  58.7 0.1 copy.46
  58.9 0.1 reshape.541
  58.9 1.5 %fusion.6 = bf16[4,256,512]{2,1,0:T(8,128)(2,1)} fusion(bf16[256,256,1]{1,0,2:T(8,128)(2,1)S(1)} %reshape.541, bf16[256,4,512]{2,1,0:T(4,128)(2,1)S(1)} %reshape_squeeze.3), kind=kOutput, calls=%fused_computation.12 | convolution fusion | flops 268959744 | bytes 2228224 | tf_op jit(solution)/shard_map/sh,hcd->csd/dot_general | solution.py:140
  60.5 4.3 %all-to-all-start.1 = ((bf16[4,256,512]{2,1,0:T(8,128)(2,1)}), bf16[4,256,512]{2,1,0:T(8,128)(2,1)S(1)}, u32[]{:S(2)}, u32[]{:S(2)}) async-start(bf16[4,256,512]{2,1,0:T(8,128)(2,1)} %fusion.6), calls=%async_computation.1 | async-start | bytes 2097152 | tf_op jit(solution)/shard_map/all_to_all | solution.py:142
  64.8 0.2 fusion.47
  65.0 0.3 fusion.20
  65.3 13.1 %all-to-all-done.1 = bf16[4,256,512]{2,1,0:T(8,128)(2,1)S(1)} async-done(((bf16[4,256,512]{2,1,0:T(8,128)(2,1)}), bf16[4,256,512]{2,1,0:T(8,128)(2,1)S(1)}, u32[]{:S(2)}, u32[]{:S(2)}) %all-to-all-start.1) | async-done | bytes 1048608 | tf_op jit(solution)/shard_map/all_to_all | solution.py:142
  78.3 0.2 reduce_sum.65
  78.6 0.8 reshape.516
  79.4 7.6 %all-to-all-start.2 = ((bf16[128,2,512]{2,1,0:T(2,128)(2,1)}), bf16[128,2,512]{2,1,0:T(2,128)(2,1)S(1)}, u32[]{:S(2)}, u32[]{:S(2)}) async-start(bf16[128,2,512]{2,1,0:T(2,128)(2,1)} %reshape.516), calls=%async_computation.2 | async-start | bytes 524288 | tf_op jit(solution)/shard_map/all_to_all | solution.py:145
  87.1 14.7 %all-to-all-done.2 = bf16[128,2,512]{2,1,0:T(2,128)(2,1)S(1)} async-done(((bf16[128,2,512]{2,1,0:T(2,128)(2,1)}), bf16[128,2,512]{2,1,0:T(2,128)(2,1)S(1)}, u32[]{:S(2)}, u32[]{:S(2)}) %all-to-all-start.2) | async-done | bytes 262176 | tf_op jit(solution)/shard_map/all_to_all | solution.py:145
  101.7 0.1 reshape.517
  101.8 0.8 gather_fusion
  102.7 0.2 fusion.32
  102.9 0.6 broadcast_in_dim.51
  103.6 3.3 %all-to-all-start.3 = ((bf16[16,4,512]{2,0,1:T(8,128)(2,1)}), bf16[16,4,512]{2,0,1:T(8,128)(2,1)S(1)}, u32[]{:S(2)}, u32[]{:S(2)}) async-start(bf16[16,4,512]{2,0,1:T(8,128)(2,1)} %broadcast_in_dim.51), calls=%async_computation.3 | async-start | bytes 131072 | tf_op jit(solution)/shard_map/all_to_all | solution.py:152
  106.9 0.4 fusion.11
  107.2 0.6 copy.68
  107.9 4.6 %all-to-all-done.3 = bf16[16,4,512]{2,0,1:T(8,128)(2,1)S(1)} async-done(((bf16[16,4,512]{2,0,1:T(8,128)(2,1)}), bf16[16,4,512]{2,0,1:T(8,128)(2,1)S(1)}, u32[]{:S(2)}, u32[]{:S(2)}) %all-to-all-start.3) | async-done | bytes 65568 | tf_op jit(solution)/shard_map/all_to_all | solution.py:152
  112.5 0.6 copy.53
  (37 shorter events, 0.2 us)
Async XLA Ops:
  0.6 54.1 %copy-start = (bf16[1,2048,256]{2,1,0:T(8,128)(2,1)S(1)}, bf16[1,2048,256]{2,1,0:T(8,128)(2,1)}, u32[]{:S(2)}) copy-start(bf16[1,2048,256]{2,1,0:T(8,128)(2,1)} %param.16) | copy-start | bytes 3145732
  5.7 18.0 %copy-start.4 = (s32[16,8]{0,1:T(8,128)S(1)}, s32[16,8]{0,1:T(8,128)}, u32[]{:S(2)}) copy-start(s32[16,8]{0,1:T(8,128)} %param.15) | copy-start | bytes 1540
  5.7 18.1 %copy-start.3 = (bf16[8,2048]{1,0:T(8,128)(2,1)S(1)}, bf16[8,2048]{1,0:T(8,128)(2,1)}, u32[]{:S(2)}) copy-start(bf16[8,2048]{1,0:T(8,128)(2,1)} %param.19) | copy-start | bytes 98308
  5.7 18.1 %copy-start.8 = (s32[8]{0:T(128)S(1)}, s32[8]{0:T(128)}, u32[]{:S(2)}) copy-start(s32[8]{0:T(128)} %param.25) | copy-start | bytes 100
  5.7 18.4 %copy-start.6 = (bf16[8,128]{1,0:T(8,128)(2,1)S(1)}, bf16[8,128]{1,0:T(8,128)(2,1)}, u32[]{:S(2)}) copy-start(bf16[8,128]{1,0:T(8,128)(2,1)} %param.23) | copy-start | bytes 6148
  5.7 18.8 %copy-start.1 = (bf16[1,256,2048]{2,1,0:T(8,128)(2,1)S(1)}, bf16[1,256,2048]{2,1,0:T(8,128)(2,1)}, u32[]{:S(2)}) copy-start(bf16[1,256,2048]{2,1,0:T(8,128)(2,1)} %param.18) | copy-start | bytes 3145732
  5.7 49.0 %all-to-all-start = ((bf16[128,2,2048]{2,1,0:T(2,128)(2,1)}), bf16[128,2,2048]{2,1,0:T(2,128)(2,1)}, u32[]{:S(2)}, u32[]{:S(2)}) async-start(bf16[128,2,2048]{2,1,0:T(2,128)(2,1)} %copy.43), calls=%async_computation | async-start | bytes 2097152 | tf_op jit(solution)/shard_map/all_to_all | solution.py:134
  24.5 0.9 copy-start.7
  24.5 1.2 %copy-start.5 = (f32[1,2048]{1,0:T(1,128)S(1)}, f32[1,2048]{1,0:T(1,128)}, u32[]{:S(2)}) copy-start(f32[1,2048]{1,0:T(1,128)} %param.21) | copy-start | bytes 24580
  54.7 2.0 %copy-start.9 = (bf16[1,2048,256]{2,1,0:T(8,128)(2,1)S(1)}, bf16[1,2048,256]{2,1,0:T(8,128)(2,1)}, u32[]{:S(2)}) copy-start(bf16[1,2048,256]{2,1,0:T(8,128)(2,1)} %param.17) | copy-start | bytes 3145732
  60.5 17.9 %all-to-all-start.1 = ((bf16[4,256,512]{2,1,0:T(8,128)(2,1)}), bf16[4,256,512]{2,1,0:T(8,128)(2,1)S(1)}, u32[]{:S(2)}, u32[]{:S(2)}) async-start(bf16[4,256,512]{2,1,0:T(8,128)(2,1)} %fusion.6), calls=%async_computation.1 | async-start | bytes 2097152 | tf_op jit(solution)/shard_map/all_to_all | solution.py:142
  79.4 22.4 %all-to-all-start.2 = ((bf16[128,2,512]{2,1,0:T(2,128)(2,1)}), bf16[128,2,512]{2,1,0:T(2,128)(2,1)S(1)}, u32[]{:S(2)}, u32[]{:S(2)}) async-start(bf16[128,2,512]{2,1,0:T(2,128)(2,1)} %reshape.516), calls=%async_computation.2 | async-start | bytes 524288 | tf_op jit(solution)/shard_map/all_to_all | solution.py:145
  87.0 19.8 %copy-start.2 = (bf16[2048,128]{1,0:T(8,128)(2,1)S(1)}, bf16[2048,128]{1,0:T(8,128)(2,1)}, u32[]{:S(2)}) copy-start(bf16[2048,128]{1,0:T(8,128)(2,1)} %param.22) | copy-start | bytes 1572868
  103.6 8.9 %all-to-all-start.3 = ((bf16[16,4,512]{2,0,1:T(8,128)(2,1)}), bf16[16,4,512]{2,0,1:T(8,128)(2,1)S(1)}, u32[]{:S(2)}, u32[]{:S(2)}) async-start(bf16[16,4,512]{2,0,1:T(8,128)(2,1)} %broadcast_in_dim.51), calls=%async_computation.3 | async-start | bytes 131072 | tf_op jit(solution)/shard_map/all_to_all | solution.py:152

commit v5 on v4

--- a/solution.py
+++ b/solution.py
@@ -127,10 +127,8 @@
     slot_token = jnp.sum(jnp.where(slot_hit, token_of_pair[None, :], 0), axis=1)
     slot_token = jnp.where(jnp.any(slot_hit, axis=1), slot_token, token_count)
     selector = (slot_token[:, None] == token_pos[None, :]).astype(hidden.dtype)
-    selector = selector.reshape(experts, capacity, token_count)
-    outgoing = jnp.einsum(
-        "ect,td->ecd", selector, hidden, preferred_element_type=jnp.float32
-    ).astype(hidden.dtype)
+    outgoing = jnp.dot(selector, hidden, preferred_element_type=jnp.float32).astype(hidden.dtype)
+    outgoing = outgoing.reshape(experts, capacity, model_width)
     arrived = lax.all_to_all(outgoing, "dp", split_axis=0, concat_axis=0, tiled=True)
     slots = dp_size * capacity
     gate_act = jnp.einsum("ecd,dh->ech", arrived, w_gate[0], preferred_element_type=jnp.float32)
@@ -143,11 +141,18 @@
     expert_out = jnp.sum(gathered.astype(jnp.float32), axis=0).astype(jnp.bfloat16)
     expert_out = expert_out.reshape(dp_size, capacity, slice_width)
     returned = lax.all_to_all(expert_out, "dp", split_axis=0, concat_axis=0, tiled=True)
-    picked = jnp.take(returned.reshape(experts * capacity, slice_width), slot_ids, axis=0)
-    picked = picked.reshape(token_count, top_count, slice_width)
     shares = route_weights.astype(jnp.float32)
     shares = shares / jnp.sum(shares, axis=1, keepdims=True)
-    mix_cols = jnp.einsum("tk,tkd->td", shares, picked.astype(jnp.float32)).astype(jnp.bfloat16)
+    slot_grid = slot_ids.reshape(token_count, top_count)
+    slot_weight = jnp.sum(
+        jnp.where(slot_grid[:, :, None] == slot_pos[None, None, :], shares[:, :, None], 0.0), axis=1
+    )
+    mix_cols = jnp.dot(
+        slot_weight,
+        returned.reshape(experts * capacity, slice_width).astype(jnp.float32),
+        precision=lax.Precision.HIGHEST,
+        preferred_element_type=jnp.float32,
+    ).astype(jnp.bfloat16)
     spread = jnp.broadcast_to(mix_cols[:, None, :], (token_count, tp_size, slice_width))
     expert_mix = lax.all_to_all(spread, "tp", split_axis=1, concat_axis=1, tiled=True)
     expert_mix = expert_mix.reshape(token_count, model_width)

time: 114 us -> 112 us (0.982)
  waiting for transfers between devices: 54.6 us -> 52.6 us
  local copies, waits for them, and re-layouts: 8.2 us -> 6.47 us
  matrix products: 8.17 us -> 9.33 us
    convert_element_type x1 -> x0, local copies, waits for them, and re-layouts: 2.11 us -> none  [on_device(): outgoing = jnp.einsum('ect,td->ecd', selector, hidden, preferred_element_...]
    reshape x2, local copies, waits for them, and re-layouts: 0.19 us -> 1.62 us  [the longest x1 1.52 us: on_device(): outgoing = outgoing.reshape(experts, capacity, model_width)]
    all_to_all x1, waiting for transfers between devices: 13.1 us -> 11.8 us  [on_device(): lax.all_to_all(partial_value, 'tp', split_axis=0, concat_axis=0, tiled=True)]
    dot_general x1, matrix products: 0.54 us -> 1.73 us  [attend_local(): jnp.einsum('rgqd,cgd->rgqc', rotated_query, cache_keys, preferred_element...]
  transfers between devices with their start and end apart: 4 -> 4, of which waited for: 4 -> 4; matrix products, arithmetic and copies ran while one was open for 9% -> 11% of each run, Pallas kernels for 0% -> 0%
where the time goes in v5:
time: 112 us; the launch traced here: 111 us
  waiting for transfers between devices  52.6 us (47%)
  starting transfers between devices  33.3 us (30%)
  matrix products  9.33 us (8%)
  other arithmetic  8.86 us (8%)
  local copies, waits for them, and re-layouts  6.47 us (6%)
    all_to_all x1, waiting for transfers between devices, on_device(): lax.all_to_all(outgoing, 'dp', split_axis=0, concat_axis=0, tiled=True)  22 us
    all_to_all x1, starting transfers between devices, on_device(): lax.all_to_all(outgoing, 'dp', split_axis=0, concat_axis=0, tiled=True)  18 us
    all_to_all x1, waiting for transfers between devices, on_device(): lax.all_to_all(expert_out, 'dp', split_axis=0, concat_axis=0, tiled=True)  14.2 us
    all_to_all x1, waiting for transfers between devices, on_device(): lax.all_to_all(partial_value, 'tp', split_axis=0, concat_axis=0, tiled=True)  11.8 us
    all_to_all x1, starting transfers between devices, on_device(): lax.all_to_all(expert_out, 'dp', split_axis=0, concat_axis=0, tiled=True)  7.62 us
    concatenate x4, other arithmetic, rotate(): jnp.concatenate([front_half * cosine - back_half * sine_part, back_half *...  5.87 us
    all_to_all x1, waiting for transfers between devices, on_device(): lax.all_to_all(spread, 'tp', split_axis=1, concat_axis=1, tiled=True)  4.59 us
    all_to_all x1, starting transfers between devices, on_device(): lax.all_to_all(partial_value, 'tp', split_axis=0, concat_axis=0, tiled=True)  4.42 us
  transfers between devices with their start and end apart: 4, of which 4 were waited for; matrix products, arithmetic and copies ran while one was open for 11% of the time, Pallas kernels for 0%

profile of v5, /device:TPU:8, one launch (start us, length us, event | category | flops | bytes accessed | tf_op | source)
XLA Modules:
  0.0 111.5 jit_solution(12935051719217566484)
XLA Ops:
  0.6 0.0 copy-start
  0.6 0.8 copy.41
  1.5 0.1 eq.26
  1.6 0.2 convert_reduce_fusion
  1.8 0.1 fusion.32
  1.9 0.1 select_reduce_fusion
  2.0 1.3 %convolution_convert_fusion = bf16[256,2048]{1,0:T(8,128)(2,1)S(1)} fusion(bf16[16,2048]{1,0:T(8,128)(2,1)} %param.13, s32[256]{0:T(256)S(1)} %broadcast_select_fusion), kind=kOutput, calls=%fused_computation | convolution fusion | flops 17305600 | bytes 1115136 | tf_op jit(solution)/shard_map/dot_general | solution.py:130
  3.3 1.5 %reshape.467 = bf16[128,2,2048]{2,1,0:T(2,128)(2,1)} reshape(bf16[256,2048]{1,0:T(8,128)(2,1)S(1)} %convolution_convert_fusion) | data formatting | bytes 2097152 | tf_op jit(solution)/shard_map/reshape | solution.py:131
  4.9 18.0 %all-to-all-start = ((bf16[128,2,2048]{2,1,0:T(2,128)(2,1)}), bf16[128,2,2048]{2,1,0:T(2,128)(2,1)}, u32[]{:S(2)}, u32[]{:S(2)}) async-start(bf16[128,2,2048]{2,1,0:T(2,128)(2,1)} %reshape.467), calls=%async_computation | async-start | bytes 2097152 | tf_op jit(solution)/shard_map/all_to_all | solution.py:132
  22.8 0.1 reduce_sum.69
  22.9 0.0 copy-start.3
  23.0 0.0 copy-start.5
  23.0 0.8 reshape_squeeze.3
  23.9 0.2 reduce-window.8
  24.0 0.1 multiply_cosine_fusion.2
  24.2 0.1 fusion.50
  24.3 0.1 select_reduce_fusion.2
  24.4 0.1 maximum_bitcast_fusion.2
  24.5 0.1 fusion.37
  24.5 0.2 fusion.43
  24.8 0.1 fusion.35
  24.9 1.4 %multiply_bitcast_fusion = f32[2048,1,128]{2,0,1:T(8,128)S(1)} fusion(bf16[2048,128]{1,0:T(8,128)(2,1)} %param.20, f32[2048]{0:T(1024)S(1)} %bitcast.92), kind=kLoop, calls=%fused_computation.29 | loop fusion | flops 524288 | bytes 1581056 | tf_op jit(solution)/shard_map/mul | solution.py:40
  26.2 5.6 %fusion.31 = (bf16[2048,64]{1,0:T(8,128)(2,1)}, bf16[2048,64]{1,0:T(8,128)(2,1)}) fusion(f32[2048,1,128]{2,0,1:T(8,128)S(1)} %multiply_bitcast_fusion, f32[64]{0:T(128)S(1)} %multiply_exponential_fusion, f32[2048]{0:T(1024)S(1)} %subtract_convert_fusion.1), kind=kLoop, calls=%fused_computation.41 | loop fusion | flops 1179648 | bytes 1581312 | tf_op jit(solution)/shard_map/concatenate | solution.py:20
  31.8 22.0 %all-to-all-done = bf16[128,2,2048]{2,1,0:T(2,128)(2,1)} async-done(((bf16[128,2,2048]{2,1,0:T(2,128)(2,1)}), bf16[128,2,2048]{2,1,0:T(2,128)(2,1)}, u32[]{:S(2)}, u32[]{:S(2)}) %all-to-all-start) | async-done | bytes 1048608 | tf_op jit(solution)/shard_map/all_to_all | solution.py:132
  53.9 2.0 %fusion.17 = f32[128,2,256]{2,0,1:T(8,128)S(1)} fusion(bf16[1,2048,256]{2,1,0:T(8,128)(2,1)S(1)} %copy-done, bf16[128,2,2048]{2,1,0:T(2,128)(2,1)} %all-to-all-done), kind=kOutput, calls=%fused_computation.25 | convolution fusion | flops 268435456 | bytes 2359296 | tf_op jit(solution)/shard_map/ecd,dh->ech/dot_general | solution.py:134
  55.9 2.0 %fusion.7 = bf16[128,2,256]{2,0,1:T(8,128)(2,1)S(1)} fusion(bf16[1,2048,256]{2,1,0:T(8,128)(2,1)S(1)} %copy-done.9, bf16[128,2,2048]{2,1,0:T(2,128)(2,1)} %all-to-all-done, f32[128,2,256]{2,0,1:T(8,128)S(1)} %fusion.17), kind=kOutput, calls=%fused_computation.13 | convolution fusion | flops 268828672 | bytes 2490368 | tf_op jit(solution)/shard_map/ecd,dh->ech/dot_general | solution.py:135
  57.9 0.1 copy.46
  58.0 0.1 reshape.485
  58.1 1.5 %fusion.6 = bf16[4,256,512]{2,1,0:T(8,128)(2,1)} fusion(bf16[256,256,1]{1,0,2:T(8,128)(2,1)S(1)} %reshape.485, bf16[256,4,512]{2,1,0:T(4,128)(2,1)S(1)} %reshape_squeeze.3), kind=kOutput, calls=%fused_computation.11 | convolution fusion | flops 268959744 | bytes 2228224 | tf_op jit(solution)/shard_map/sh,hcd->csd/dot_general | solution.py:138
  59.6 4.4 %all-to-all-start.1 = ((bf16[4,256,512]{2,1,0:T(8,128)(2,1)}), bf16[4,256,512]{2,1,0:T(8,128)(2,1)S(1)}, u32[]{:S(2)}, u32[]{:S(2)}) async-start(bf16[4,256,512]{2,1,0:T(8,128)(2,1)} %fusion.6), calls=%async_computation.1 | async-start | bytes 2097152 | tf_op jit(solution)/shard_map/all_to_all | solution.py:140
  64.1 1.7 %fusion.55 = (f32[8,16]{1,0:T(8,128)S(1)}, f32[8,1,16,2048]{3,2,0,1:T(8,128)S(1)}) fusion(bf16[8,16,64]{2,1,0:T(8,128)(2,1)S(1)} %get-tuple-element.7, bf16[8,16,64]{2,1,0:T(8,128)(2,1)S(1)} %get-tuple-element.6, bf16[2048,64]{1,0:T(8,128)(2,1)} %get-tuple-element.5, bf16[2048,64]{1,0:T(8,128)(2,1)} %get-tuple-element.4, pred[8,2048]{1,0:T(8,128)(4,1)S(1)} %fusion.35), kind=kOutput, calls=%fused_computation.103 | convolution fusion | flops 69009280 | bytes 1622528 | tf_op jit(solution)/shard_map/rgqd,cgd->rgqc/dot_general | solution.py:54
  65.8 0.0 copy-start.7
  65.8 11.8 %all-to-all-done.1 = bf16[4,256,512]{2,1,0:T(8,128)(2,1)S(1)} async-done(((bf16[4,256,512]{2,1,0:T(8,128)(2,1)}), bf16[4,256,512]{2,1,0:T(8,128)(2,1)S(1)}, u32[]{:S(2)}, u32[]{:S(2)}) %all-to-all-start.1) | async-done | bytes 1048608 | tf_op jit(solution)/shard_map/all_to_all | solution.py:140
  77.6 0.2 reduce_sum.73
  77.9 0.8 reshape.469
  78.7 7.6 %all-to-all-start.2 = ((bf16[128,2,512]{2,1,0:T(2,128)(2,1)}), bf16[128,2,512]{2,1,0:T(2,128)(2,1)S(1)}, u32[]{:S(2)}, u32[]{:S(2)}) async-start(bf16[128,2,512]{2,1,0:T(2,128)(2,1)} %reshape.469), calls=%async_computation.2 | async-start | bytes 524288 | tf_op jit(solution)/shard_map/all_to_all | solution.py:143
  86.3 0.1 copy.43
  86.4 0.1 select_reduce_fusion.1
  86.5 0.3 fusion.20
  86.8 14.2 %all-to-all-done.2 = bf16[128,2,512]{2,1,0:T(2,128)(2,1)S(1)} async-done(((bf16[128,2,512]{2,1,0:T(2,128)(2,1)}), bf16[128,2,512]{2,1,0:T(2,128)(2,1)S(1)}, u32[]{:S(2)}, u32[]{:S(2)}) %all-to-all-start.2) | async-done | bytes 262176 | tf_op jit(solution)/shard_map/all_to_all | solution.py:143
  101.0 0.1 reshape.470
  101.1 0.2 convolution_convert_fusion.2
  101.3 0.7 broadcast_in_dim.53
  102.0 3.3 %all-to-all-start.3 = ((bf16[16,4,512]{2,0,1:T(8,128)(2,1)}), bf16[16,4,512]{2,0,1:T(8,128)(2,1)S(1)}, u32[]{:S(2)}, u32[]{:S(2)}) async-start(bf16[16,4,512]{2,0,1:T(8,128)(2,1)} %broadcast_in_dim.53), calls=%async_computation.3 | async-start | bytes 131072 | tf_op jit(solution)/shard_map/all_to_all | solution.py:157
  105.3 0.4 fusion.11
  105.6 0.6 copy.65
  106.3 4.6 %all-to-all-done.3 = bf16[16,4,512]{2,0,1:T(8,128)(2,1)S(1)} async-done(((bf16[16,4,512]{2,0,1:T(8,128)(2,1)}), bf16[16,4,512]{2,0,1:T(8,128)(2,1)S(1)}, u32[]{:S(2)}, u32[]{:S(2)}) %all-to-all-start.3) | async-done | bytes 65568 | tf_op jit(solution)/shard_map/all_to_all | solution.py:157
  110.9 0.6 copy.51
  (30 shorter events, 0.2 us)
Async XLA Ops:
  0.6 53.2 %copy-start = (bf16[1,2048,256]{2,1,0:T(8,128)(2,1)S(1)}, bf16[1,2048,256]{2,1,0:T(8,128)(2,1)}, u32[]{:S(2)}) copy-start(bf16[1,2048,256]{2,1,0:T(8,128)(2,1)} %param.16) | copy-start | bytes 3145732
  4.9 18.1 %copy-start.1 = (bf16[1,256,2048]{2,1,0:T(8,128)(2,1)S(1)}, bf16[1,256,2048]{2,1,0:T(8,128)(2,1)}, u32[]{:S(2)}) copy-start(bf16[1,256,2048]{2,1,0:T(8,128)(2,1)} %param.18) | copy-start | bytes 3145732
  4.9 49.0 %all-to-all-start = ((bf16[128,2,2048]{2,1,0:T(2,128)(2,1)}), bf16[128,2,2048]{2,1,0:T(2,128)(2,1)}, u32[]{:S(2)}, u32[]{:S(2)}) async-start(bf16[128,2,2048]{2,1,0:T(2,128)(2,1)} %reshape.467), calls=%async_computation | async-start | bytes 2097152 | tf_op jit(solution)/shard_map/all_to_all | solution.py:132
  22.9 0.9 copy-start.3
  23.0 0.9 copy-start.8
  23.0 1.1 copy-start.6
  23.0 1.9 %copy-start.5 = (f32[1,2048]{1,0:T(1,128)S(1)}, f32[1,2048]{1,0:T(1,128)}, u32[]{:S(2)}) copy-start(f32[1,2048]{1,0:T(1,128)} %param.21) | copy-start | bytes 24580
  53.9 2.0 %copy-start.9 = (bf16[1,2048,256]{2,1,0:T(8,128)(2,1)S(1)}, bf16[1,2048,256]{2,1,0:T(8,128)(2,1)}, u32[]{:S(2)}) copy-start(bf16[1,2048,256]{2,1,0:T(8,128)(2,1)} %param.17) | copy-start | bytes 3145732
  59.6 4.4 %copy-start.4 = (s32[16,8]{0,1:T(8,128)S(1)}, s32[16,8]{0,1:T(8,128)}, u32[]{:S(2)}) copy-start(s32[16,8]{0,1:T(8,128)} %param.15) | copy-start | bytes 1540
  59.6 18.0 %all-to-all-start.1 = ((bf16[4,256,512]{2,1,0:T(8,128)(2,1)}), bf16[4,256,512]{2,1,0:T(8,128)(2,1)S(1)}, u32[]{:S(2)}, u32[]{:S(2)}) async-start(bf16[4,256,512]{2,1,0:T(8,128)(2,1)} %fusion.6), calls=%async_computation.1 | async-start | bytes 2097152 | tf_op jit(solution)/shard_map/all_to_all | solution.py:140
  65.8 20.5 %copy-start.7 = (bf16[8,128]{1,0:T(8,128)(2,1)S(1)}, bf16[8,128]{1,0:T(8,128)(2,1)}, u32[]{:S(2)}) copy-start(bf16[8,128]{1,0:T(8,128)(2,1)} %param.24) | copy-start | bytes 6148
  78.7 22.4 %all-to-all-start.2 = ((bf16[128,2,512]{2,1,0:T(2,128)(2,1)}), bf16[128,2,512]{2,1,0:T(2,128)(2,1)S(1)}, u32[]{:S(2)}, u32[]{:S(2)}) async-start(bf16[128,2,512]{2,1,0:T(2,128)(2,1)} %reshape.469), calls=%async_computation.2 | async-start | bytes 524288 | tf_op jit(solution)/shard_map/all_to_all | solution.py:143
  86.5 18.8 %copy-start.2 = (bf16[2048,128]{1,0:T(8,128)(2,1)S(1)}, bf16[2048,128]{1,0:T(8,128)(2,1)}, u32[]{:S(2)}) copy-start(bf16[2048,128]{1,0:T(8,128)(2,1)} %param.22) | copy-start | bytes 1572868
  102.0 8.9 %all-to-all-start.3 = ((bf16[16,4,512]{2,0,1:T(8,128)(2,1)}), bf16[16,4,512]{2,0,1:T(8,128)(2,1)S(1)}, u32[]{:S(2)}, u32[]{:S(2)}) async-start(bf16[16,4,512]{2,0,1:T(8,128)(2,1)} %broadcast_in_dim.53), calls=%async_computation.3 | async-start | bytes 131072 | tf_op jit(solution)/shard_map/all_to_all | solution.py:157

commit v6 on v5

--- a/solution.py
+++ b/solution.py
@@ -138,8 +138,8 @@
     partial_value = jnp.einsum("sh,hcd->csd", hidden_act, down_w, preferred_element_type=jnp.float32)
     partial_value = partial_value.astype(jnp.bfloat16)
     gathered = lax.all_to_all(partial_value, "tp", split_axis=0, concat_axis=0, tiled=True)
+    gathered = gathered.reshape(tp_size, dp_size, capacity, slice_width)
     expert_out = jnp.sum(gathered.astype(jnp.float32), axis=0).astype(jnp.bfloat16)
-    expert_out = expert_out.reshape(dp_size, capacity, slice_width)
     returned = lax.all_to_all(expert_out, "dp", split_axis=0, concat_axis=0, tiled=True)
     shares = route_weights.astype(jnp.float32)
     shares = shares / jnp.sum(shares, axis=1, keepdims=True)
@@ -147,15 +147,16 @@
     slot_weight = jnp.sum(
         jnp.where(slot_grid[:, :, None] == slot_pos[None, None, :], shares[:, :, None], 0.0), axis=1
     )
-    mix_cols = jnp.dot(
+    slot_weight = jnp.broadcast_to(slot_weight[None], (tp_size,) + slot_weight.shape)
+    spread = jnp.einsum(
+        "cts,sd->ctd",
         slot_weight,
         returned.reshape(experts * capacity, slice_width).astype(jnp.float32),
         precision=lax.Precision.HIGHEST,
         preferred_element_type=jnp.float32,
     ).astype(jnp.bfloat16)
-    spread = jnp.broadcast_to(mix_cols[:, None, :], (token_count, tp_size, slice_width))
-    expert_mix = lax.all_to_all(spread, "tp", split_axis=1, concat_axis=1, tiled=True)
-    expert_mix = expert_mix.reshape(token_count, model_width)
+    expert_mix = lax.all_to_all(spread, "tp", split_axis=0, concat_axis=0, tiled=True)
+    expert_mix = jnp.transpose(expert_mix, (1, 0, 2)).reshape(token_count, model_width)
     attended = attend_local(
         queries, key_codes, key_scales, cache_values, new_keys, new_values, lengths
     )

time: 112 us -> 112 us (level)
  no operation moved by 1% of the time
where the time goes in v6:
time: 112 us
  waiting for transfers between devices  52.6 us (47%)
  starting transfers between devices  33.3 us (30%)
  matrix products  10 us (9%)
  other arithmetic  8.86 us (8%)
  local copies, waits for them, and re-layouts  5.82 us (5%)
    all_to_all x1, waiting for transfers between devices, on_device(): lax.all_to_all(outgoing, 'dp', split_axis=0, concat_axis=0, tiled=True)  22 us
    all_to_all x1, starting transfers between devices, on_device(): lax.all_to_all(outgoing, 'dp', split_axis=0, concat_axis=0, tiled=True)  18 us
    all_to_all x1, waiting for transfers between devices, on_device(): lax.all_to_all(expert_out, 'dp', split_axis=0, concat_axis=0, tiled=True)  14.2 us
    all_to_all x1, waiting for transfers between devices, on_device(): lax.all_to_all(partial_value, 'tp', split_axis=0, concat_axis=0, tiled=True)  11.8 us
    all_to_all x1, starting transfers between devices, on_device(): lax.all_to_all(expert_out, 'dp', split_axis=0, concat_axis=0, tiled=True)  7.62 us
    concatenate x4, other arithmetic, rotate(): jnp.concatenate([front_half * cosine - back_half * sine_part, back_half *...  5.87 us
    all_to_all x1, waiting for transfers between devices, on_device(): lax.all_to_all(spread, 'tp', split_axis=0, concat_axis=0, tiled=True)  4.58 us
    all_to_all x1, starting transfers between devices, on_device(): lax.all_to_all(partial_value, 'tp', split_axis=0, concat_axis=0, tiled=True)  4.42 us
  transfers between devices with their start and end apart: 4, of which 4 were waited for; matrix products, arithmetic and copies ran while one was open for 11% of the time, Pallas kernels for 0%

profile of v6, /device:TPU:8, one launch (start us, length us, event | category | flops | bytes accessed | tf_op | source)
XLA Modules:
  0.0 111.5 jit_solution(6963865021221848984)
XLA Ops:
  0.6 0.0 copy-start
  0.6 0.8 copy.35
  1.5 0.1 eq.26
  1.6 0.2 convert_reduce_fusion
  1.8 0.1 fusion.32
  1.9 0.1 select_reduce_fusion
  2.0 1.3 %convolution_convert_fusion = bf16[256,2048]{1,0:T(8,128)(2,1)S(1)} fusion(bf16[16,2048]{1,0:T(8,128)(2,1)} %param.13, s32[256]{0:T(256)S(1)} %broadcast_select_fusion), kind=kOutput, calls=%fused_computation | convolution fusion | flops 17305600 | bytes 1115136 | tf_op jit(solution)/shard_map/dot_general | solution.py:130
  3.3 1.5 %reshape.466 = bf16[128,2,2048]{2,1,0:T(2,128)(2,1)} reshape(bf16[256,2048]{1,0:T(8,128)(2,1)S(1)} %convolution_convert_fusion) | data formatting | bytes 2097152 | tf_op jit(solution)/shard_map/reshape | solution.py:131
  4.9 18.0 %all-to-all-start = ((bf16[128,2,2048]{2,1,0:T(2,128)(2,1)}), bf16[128,2,2048]{2,1,0:T(2,128)(2,1)}, u32[]{:S(2)}, u32[]{:S(2)}) async-start(bf16[128,2,2048]{2,1,0:T(2,128)(2,1)} %reshape.466), calls=%async_computation | async-start | bytes 2097152 | tf_op jit(solution)/shard_map/all_to_all | solution.py:132
  22.8 0.1 reduce_sum.71
  22.9 0.0 copy-start.3
  23.0 0.0 copy-start.8
  23.0 0.0 copy-start.6
  23.0 0.8 reshape_squeeze.3
  23.9 0.2 reduce-window.8
  24.0 0.1 multiply_cosine_fusion.2
  24.2 0.1 fusion.51
  24.3 0.1 select_reduce_fusion.2
  24.4 0.1 maximum_bitcast_fusion.2
  24.5 0.1 fusion.37
  24.5 0.2 fusion.44
  24.8 0.1 fusion.35
  24.9 1.4 %multiply_bitcast_fusion = f32[2048,1,128]{2,0,1:T(8,128)S(1)} fusion(bf16[2048,128]{1,0:T(8,128)(2,1)} %param.20, f32[2048]{0:T(1024)S(1)} %bitcast.92), kind=kLoop, calls=%fused_computation.29 | loop fusion | flops 524288 | bytes 1581056 | tf_op jit(solution)/shard_map/mul | solution.py:40
  26.2 5.6 %fusion.31 = (bf16[2048,64]{1,0:T(8,128)(2,1)}, bf16[2048,64]{1,0:T(8,128)(2,1)}) fusion(f32[2048,1,128]{2,0,1:T(8,128)S(1)} %multiply_bitcast_fusion, f32[64]{0:T(128)S(1)} %multiply_exponential_fusion, f32[2048]{0:T(1024)S(1)} %subtract_convert_fusion.1), kind=kLoop, calls=%fused_computation.41 | loop fusion | flops 1179648 | bytes 1581312 | tf_op jit(solution)/shard_map/concatenate | solution.py:20
  31.8 22.0 %all-to-all-done = bf16[128,2,2048]{2,1,0:T(2,128)(2,1)} async-done(((bf16[128,2,2048]{2,1,0:T(2,128)(2,1)}), bf16[128,2,2048]{2,1,0:T(2,128)(2,1)}, u32[]{:S(2)}, u32[]{:S(2)}) %all-to-all-start) | async-done | bytes 1048608 | tf_op jit(solution)/shard_map/all_to_all | solution.py:132
  53.9 2.0 %fusion.17 = f32[128,2,256]{2,0,1:T(8,128)S(1)} fusion(bf16[1,2048,256]{2,1,0:T(8,128)(2,1)S(1)} %copy-done, bf16[128,2,2048]{2,1,0:T(2,128)(2,1)} %all-to-all-done), kind=kOutput, calls=%fused_computation.25 | convolution fusion | flops 268435456 | bytes 2359296 | tf_op jit(solution)/shard_map/ecd,dh->ech/dot_general | solution.py:134
  55.9 2.0 %fusion.7 = bf16[128,2,256]{2,0,1:T(8,128)(2,1)S(1)} fusion(bf16[1,2048,256]{2,1,0:T(8,128)(2,1)S(1)} %copy-done.9, bf16[128,2,2048]{2,1,0:T(2,128)(2,1)} %all-to-all-done, f32[128,2,256]{2,0,1:T(8,128)S(1)} %fusion.17), kind=kOutput, calls=%fused_computation.13 | convolution fusion | flops 268828672 | bytes 2490368 | tf_op jit(solution)/shard_map/ecd,dh->ech/dot_general | solution.py:135
  57.9 0.1 copy.40
  58.0 0.1 reshape.483
  58.1 1.5 %fusion.6 = bf16[4,256,512]{2,1,0:T(8,128)(2,1)} fusion(bf16[256,256,1]{1,0,2:T(8,128)(2,1)S(1)} %reshape.483, bf16[256,4,512]{2,1,0:T(4,128)(2,1)S(1)} %reshape_squeeze.3), kind=kOutput, calls=%fused_computation.11 | convolution fusion | flops 268959744 | bytes 2228224 | tf_op jit(solution)/shard_map/sh,hcd->csd/dot_general | solution.py:138
  59.6 4.4 %all-to-all-start.1 = ((bf16[4,256,512]{2,1,0:T(8,128)(2,1)}), bf16[4,256,512]{2,1,0:T(8,128)(2,1)S(1)}, u32[]{:S(2)}, u32[]{:S(2)}) async-start(bf16[4,256,512]{2,1,0:T(8,128)(2,1)} %fusion.6), calls=%async_computation.1 | async-start | bytes 2097152 | tf_op jit(solution)/shard_map/all_to_all | solution.py:140
  64.1 1.7 %fusion.56 = (f32[8,16]{1,0:T(8,128)S(1)}, f32[8,1,16,2048]{3,2,0,1:T(8,128)S(1)}) fusion(bf16[8,16,64]{2,1,0:T(8,128)(2,1)S(1)} %get-tuple-element.7, bf16[8,16,64]{2,1,0:T(8,128)(2,1)S(1)} %get-tuple-element.6, bf16[2048,64]{1,0:T(8,128)(2,1)} %get-tuple-element.5, bf16[2048,64]{1,0:T(8,128)(2,1)} %get-tuple-element.4, pred[8,2048]{1,0:T(8,128)(4,1)S(1)} %fusion.35), kind=kOutput, calls=%fused_computation.104 | convolution fusion | flops 69009280 | bytes 1622528 | tf_op jit(solution)/shard_map/rgqd,cgd->rgqc/dot_general | solution.py:54
  65.8 11.8 %all-to-all-done.1 = bf16[4,256,512]{2,1,0:T(8,128)(2,1)S(1)} async-done(((bf16[4,256,512]{2,1,0:T(8,128)(2,1)}), bf16[4,256,512]{2,1,0:T(8,128)(2,1)S(1)}, u32[]{:S(2)}, u32[]{:S(2)}) %all-to-all-start.1) | async-done | bytes 1048608 | tf_op jit(solution)/shard_map/all_to_all | solution.py:140
  77.6 0.2 reduce_sum.75
  77.9 0.8 reduce_sum.76
  78.7 7.6 %all-to-all-start.2 = ((bf16[128,2,512]{2,1,0:T(2,128)(2,1)}), bf16[128,2,512]{2,1,0:T(2,128)(2,1)S(1)}, u32[]{:S(2)}, u32[]{:S(2)}) async-start(bf16[128,2,512]{2,1,0:T(2,128)(2,1)} %reduce_sum.76), calls=%async_computation.2 | async-start | bytes 524288 | tf_op jit(solution)/shard_map/all_to_all | solution.py:143
  86.3 0.1 copy.37
  86.4 0.1 select_reduce_fusion.1
  86.5 0.0 copy-start.2
  86.5 0.3 fusion.20
  86.8 14.2 %all-to-all-done.2 = bf16[128,2,512]{2,1,0:T(2,128)(2,1)S(1)} async-done(((bf16[128,2,512]{2,1,0:T(2,128)(2,1)}), bf16[128,2,512]{2,1,0:T(2,128)(2,1)S(1)}, u32[]{:S(2)}, u32[]{:S(2)}) %all-to-all-start.2) | async-done | bytes 262176 | tf_op jit(solution)/shard_map/all_to_all | solution.py:143
  101.0 0.1 reshape.484
  101.1 0.9 convolution_convert_fusion.2
  102.0 3.3 %all-to-all-start.3 = ((bf16[4,16,512]{2,1,0:T(8,128)(2,1)}), bf16[4,16,512]{2,1,0:T(8,128)(2,1)S(1)}, u32[]{:S(2)}, u32[]{:S(2)}) async-start(bf16[4,16,512]{2,1,0:T(8,128)(2,1)} %convolution_convert_fusion.2), calls=%async_computation.3 | async-start | bytes 131072 | tf_op jit(solution)/shard_map/all_to_all | solution.py:158
  105.3 0.4 fusion.11
  105.7 0.6 copy.59
  106.3 4.6 %all-to-all-done.3 = bf16[4,16,512]{2,1,0:T(8,128)(2,1)S(1)} async-done(((bf16[4,16,512]{2,1,0:T(8,128)(2,1)}), bf16[4,16,512]{2,1,0:T(8,128)(2,1)S(1)}, u32[]{:S(2)}, u32[]{:S(2)}) %all-to-all-start.3) | async-done | bytes 65568 | tf_op jit(solution)/shard_map/all_to_all | solution.py:158
  110.9 0.6 copy.45
  (29 shorter events, 0.1 us)
Async XLA Ops:
  0.6 53.2 %copy-start = (bf16[1,2048,256]{2,1,0:T(8,128)(2,1)S(1)}, bf16[1,2048,256]{2,1,0:T(8,128)(2,1)}, u32[]{:S(2)}) copy-start(bf16[1,2048,256]{2,1,0:T(8,128)(2,1)} %param.16) | copy-start | bytes 3145732
  4.9 18.1 %copy-start.1 = (bf16[1,256,2048]{2,1,0:T(8,128)(2,1)S(1)}, bf16[1,256,2048]{2,1,0:T(8,128)(2,1)}, u32[]{:S(2)}) copy-start(bf16[1,256,2048]{2,1,0:T(8,128)(2,1)} %param.18) | copy-start | bytes 3145732
  4.9 49.0 %all-to-all-start = ((bf16[128,2,2048]{2,1,0:T(2,128)(2,1)}), bf16[128,2,2048]{2,1,0:T(2,128)(2,1)}, u32[]{:S(2)}, u32[]{:S(2)}) async-start(bf16[128,2,2048]{2,1,0:T(2,128)(2,1)} %reshape.466), calls=%async_computation | async-start | bytes 2097152 | tf_op jit(solution)/shard_map/all_to_all | solution.py:132
  22.9 0.9 copy-start.3
  23.0 0.9 copy-start.8
  23.0 1.1 copy-start.6
  23.0 1.9 %copy-start.5 = (f32[1,2048]{1,0:T(1,128)S(1)}, f32[1,2048]{1,0:T(1,128)}, u32[]{:S(2)}) copy-start(f32[1,2048]{1,0:T(1,128)} %param.21) | copy-start | bytes 24580
  53.9 2.0 %copy-start.9 = (bf16[1,2048,256]{2,1,0:T(8,128)(2,1)S(1)}, bf16[1,2048,256]{2,1,0:T(8,128)(2,1)}, u32[]{:S(2)}) copy-start(bf16[1,2048,256]{2,1,0:T(8,128)(2,1)} %param.17) | copy-start | bytes 3145732
  59.6 4.4 %copy-start.4 = (s32[16,8]{0,1:T(8,128)S(1)}, s32[16,8]{0,1:T(8,128)}, u32[]{:S(2)}) copy-start(s32[16,8]{0,1:T(8,128)} %param.15) | copy-start | bytes 1540
  59.6 18.0 %all-to-all-start.1 = ((bf16[4,256,512]{2,1,0:T(8,128)(2,1)}), bf16[4,256,512]{2,1,0:T(8,128)(2,1)S(1)}, u32[]{:S(2)}, u32[]{:S(2)}) async-start(bf16[4,256,512]{2,1,0:T(8,128)(2,1)} %fusion.6), calls=%async_computation.1 | async-start | bytes 2097152 | tf_op jit(solution)/shard_map/all_to_all | solution.py:140
  65.8 20.5 %copy-start.7 = (bf16[8,128]{1,0:T(8,128)(2,1)S(1)}, bf16[8,128]{1,0:T(8,128)(2,1)}, u32[]{:S(2)}) copy-start(bf16[8,128]{1,0:T(8,128)(2,1)} %param.24) | copy-start | bytes 6148
  78.7 22.4 %all-to-all-start.2 = ((bf16[128,2,512]{2,1,0:T(2,128)(2,1)}), bf16[128,2,512]{2,1,0:T(2,128)(2,1)S(1)}, u32[]{:S(2)}, u32[]{:S(2)}) async-start(bf16[128,2,512]{2,1,0:T(2,128)(2,1)} %reduce_sum.76), calls=%async_computation.2 | async-start | bytes 524288 | tf_op jit(solution)/shard_map/all_to_all | solution.py:143
  86.5 18.8 %copy-start.2 = (bf16[2048,128]{1,0:T(8,128)(2,1)S(1)}, bf16[2048,128]{1,0:T(8,128)(2,1)}, u32[]{:S(2)}) copy-start(bf16[2048,128]{1,0:T(8,128)(2,1)} %param.22) | copy-start | bytes 1572868
  102.0 8.9 %all-to-all-start.3 = ((bf16[4,16,512]{2,1,0:T(8,128)(2,1)}), bf16[4,16,512]{2,1,0:T(8,128)(2,1)S(1)}, u32[]{:S(2)}, u32[]{:S(2)}) async-start(bf16[4,16,512]{2,1,0:T(8,128)(2,1)} %convolution_convert_fusion.2), calls=%async_computation.3 | async-start | bytes 131072 | tf_op jit(solution)/shard_map/all_to_all | solution.py:158

commit v7 on v6

--- a/solution.py
+++ b/solution.py
@@ -2,6 +2,8 @@
 import jax.numpy as jnp
 from jax import lax
 from jax.sharding import PartitionSpec as P
+from jax.experimental import pallas as pl
+from jax.experimental.pallas import tpu as pltpu
 
 rope_base = 1000000.0
 
@@ -80,6 +82,29 @@
         .astype(jnp.bfloat16)
     )
 
+
+def expert_kernel(x_ref, gate_ref, up_ref, down_ref, out_ref):
+    inputs = x_ref[...]
+    gate_act = jnp.dot(inputs, gate_ref[...], preferred_element_type=jnp.float32)
+    up_act = jnp.dot(inputs, up_ref[...], preferred_element_type=jnp.float32)
+    hidden_act = (gate_act / (1.0 + jnp.exp(-gate_act)) * up_act).astype(jnp.bfloat16)
+    partial_value = jnp.dot(hidden_act, down_ref[...], preferred_element_type=jnp.float32)
+    pieces = out_ref.shape[0]
+    width = out_ref.shape[2]
+    for piece in range(pieces):
+        out_ref[piece] = partial_value[:, piece * width:(piece + 1) * width].astype(out_ref.dtype)
+
+
+def expert_ffn(inputs, gate_w, up_w, down_w, pieces):
+    rows = inputs.shape[0]
+    width = down_w.shape[1] // pieces
+    in_vmem = pl.BlockSpec(memory_space=pltpu.VMEM)
+    return pl.pallas_call(
+        expert_kernel,
+        out_shape=jax.ShapeDtypeStruct((pieces, rows, width), jnp.bfloat16),
+        in_specs=[in_vmem, in_vmem, in_vmem, in_vmem],
+        out_specs=pl.BlockSpec(memory_space=pltpu.VMEM),
+    )(inputs, gate_w, up_w, down_w)
 
 def expert_block(arrived, w_gate, w_up, w_down):
     arrived_shape = arrived.shape
@@ -131,12 +156,9 @@
     outgoing = outgoing.reshape(experts, capacity, model_width)
     arrived = lax.all_to_all(outgoing, "dp", split_axis=0, concat_axis=0, tiled=True)
     slots = dp_size * capacity
-    gate_act = jnp.einsum("ecd,dh->ech", arrived, w_gate[0], preferred_element_type=jnp.float32)
-    up_act = jnp.einsum("ecd,dh->ech", arrived, w_up[0], preferred_element_type=jnp.float32)
-    hidden_act = (jax.nn.silu(gate_act) * up_act).astype(jnp.bfloat16).reshape(slots, -1)
-    down_w = w_down[0].reshape(w_down.shape[1], tp_size, slice_width)
-    partial_value = jnp.einsum("sh,hcd->csd", hidden_act, down_w, preferred_element_type=jnp.float32)
-    partial_value = partial_value.astype(jnp.bfloat16)
+    partial_value = expert_ffn(
+        arrived.reshape(slots, model_width), w_gate[0], w_up[0], w_down[0], tp_size
+    )
     gathered = lax.all_to_all(partial_value, "tp", split_axis=0, concat_axis=0, tiled=True)
     gathered = gathered.reshape(tp_size, dp_size, capacity, slice_width)
     expert_out = jnp.sum(gathered.astype(jnp.float32), axis=0).astype(jnp.bfloat16)

time: 112 us -> 112 us (level)
  matrix products: 10 us -> 4.35 us
  Pallas kernels: 0 us -> 4.25 us
  waiting for transfers between devices: 52.6 us -> 55.1 us
  other arithmetic: 8.86 us -> 7.67 us
    dot_general x3 -> x0, matrix products: 5.51 us -> none  [the longest x1 2.02 us: on_device(): jnp.einsum('ecd,dh->ech', arrived, w_gate[0], preferred_element_type=jnp....]
    pallas_call x0 -> x1, Pallas kernels: none -> 4.25 us  [expert_ffn(): pl.pallas_call(expert_kernel, out_shape=jax.ShapeDtypeStruct((pieces, row...]
    all_to_all x1, waiting for transfers between devices: 22 us -> 24.4 us  [on_device(): lax.all_to_all(outgoing, 'dp', split_axis=0, concat_axis=0, tiled=True)]
    reshape x1, local copies, waits for them, and re-layouts: 0.06 us -> 1.23 us  [on_device(): arrived.reshape(slots, model_width)]
  transfers between devices with their start and end apart: 4 -> 4, of which waited for: 4 -> 4; matrix products, arithmetic and copies ran while one was open for 11% -> 9% of each run, Pallas kernels for 0% -> 0%
where the time goes in v7:
time: 112 us; the launch traced here: 111 us
  waiting for transfers between devices  55.1 us (49%)
  starting transfers between devices  32.9 us (29%)
  other arithmetic  7.67 us (7%)
  local copies, waits for them, and re-layouts  6.02 us (5%)
  matrix products  4.35 us (4%)
  Pallas kernels  4.25 us (4%)
    all_to_all x1, waiting for transfers between devices, on_device(): lax.all_to_all(outgoing, 'dp', split_axis=0, concat_axis=0, tiled=True)  24.4 us
    all_to_all x1, starting transfers between devices, on_device(): lax.all_to_all(outgoing, 'dp', split_axis=0, concat_axis=0, tiled=True)  17.5 us
    all_to_all x1, waiting for transfers between devices, on_device(): lax.all_to_all(expert_out, 'dp', split_axis=0, concat_axis=0, tiled=True)  14.2 us
    all_to_all x1, waiting for transfers between devices, on_device(): lax.all_to_all(partial_value, 'tp', split_axis=0, concat_axis=0, tiled=True)  11.9 us
    all_to_all x1, starting transfers between devices, on_device(): lax.all_to_all(expert_out, 'dp', split_axis=0, concat_axis=0, tiled=True)  7.62 us
    concatenate x4, other arithmetic, rotate(): jnp.concatenate([front_half * cosine - back_half * sine_part, back_half *...  5.72 us
    all_to_all x1, waiting for transfers between devices, on_device(): lax.all_to_all(spread, 'tp', split_axis=0, concat_axis=0, tiled=True)  4.59 us
    all_to_all x1, starting transfers between devices, on_device(): lax.all_to_all(partial_value, 'tp', split_axis=0, concat_axis=0, tiled=True)  4.43 us
  transfers between devices with their start and end apart: 4, of which 4 were waited for; matrix products, arithmetic and copies ran while one was open for 9% of the time, Pallas kernels for 0%

profile of v7, /device:TPU:8, one launch (start us, length us, event | category | flops | bytes accessed | tf_op | source)
XLA Modules:
  0.0 111.2 jit_solution(9257965780000270381)
XLA Ops:
  0.6 0.0 copy-start
  0.6 0.8 copy.22
  1.5 0.1 eq.26
  1.5 0.2 convert_reduce_fusion
  1.7 0.1 fusion.24
  1.9 0.1 select_reduce_fusion
  2.0 1.3 %convolution_convert_fusion = bf16[256,2048]{1,0:T(8,128)(2,1)S(1)} fusion(bf16[16,2048]{1,0:T(8,128)(2,1)} %param.13, s32[256]{0:T(256)S(1)} %broadcast_select_fusion), kind=kOutput, calls=%fused_computation | convolution fusion | flops 17305600 | bytes 1115136 | tf_op jit(solution)/shard_map/dot_general | solution.py:155
  3.3 1.5 %reshape.466 = bf16[128,2,2048]{2,1,0:T(2,128)(2,1)} reshape(bf16[256,2048]{1,0:T(8,128)(2,1)S(1)} %convolution_convert_fusion) | data formatting | bytes 2097152 | tf_op jit(solution)/shard_map/reshape | solution.py:156
  4.8 0.0 copy-start.4
  4.9 17.5 %all-to-all-start = ((bf16[128,2,2048]{2,1,0:T(2,128)(2,1)}), bf16[128,2,2048]{2,1,0:T(2,128)(2,1)S(1)}, u32[]{:S(2)}, u32[]{:S(2)}) async-start(bf16[128,2,2048]{2,1,0:T(2,128)(2,1)} %reshape.466), calls=%async_computation | async-start | bytes 2097152 | tf_op jit(solution)/shard_map/all_to_all | solution.py:157
  22.4 0.1 reduce_sum.71
  22.5 0.0 copy-done.7
  22.5 0.2 reduce-window.8
  22.7 0.0 copy-done.2
  22.7 0.0 copy-done.5
  22.7 0.1 multiply_cosine_fusion.2
  22.8 0.1 fusion.43
  23.0 0.1 select_reduce_fusion.2
  23.1 0.1 maximum_bitcast_fusion.2
  23.1 0.1 fusion.29
  23.2 0.2 fusion.36
  23.4 0.1 fusion.27
  23.5 0.0 copy-done.1
  23.5 0.0 copy-done.4
  23.6 0.3 multiply_bitcast_fusion
  23.9 5.4 %fusion.23 = (bf16[2048,64]{1,0:T(8,128)(2,1)S(1)}, bf16[2048,64]{1,0:T(8,128)(2,1)}) fusion(f32[2048,1,128]{2,0,1:T(8,128)S(1)} %multiply_bitcast_fusion, f32[64]{0:T(128)S(1)} %multiply_exponential_fusion, f32[2048]{0:T(1024)S(1)} %subtract_convert_fusion.1), kind=kLoop, calls=%fused_computation.31 | loop fusion | flops 1179648 | bytes 1581312 | tf_op jit(solution)/shard_map/concatenate | solution.py:22
  29.3 24.4 %all-to-all-done = bf16[128,2,2048]{2,1,0:T(2,128)(2,1)S(1)} async-done(((bf16[128,2,2048]{2,1,0:T(2,128)(2,1)}), bf16[128,2,2048]{2,1,0:T(2,128)(2,1)S(1)}, u32[]{:S(2)}, u32[]{:S(2)}) %all-to-all-start) | async-done | bytes 1048608 | tf_op jit(solution)/shard_map/all_to_all | solution.py:157
  53.8 1.2 %reshape.467.x_ref = bf16[256,2048]{1,0:T(8,128)(2,1)} reshape(bf16[128,2,2048]{2,1,0:T(2,128)(2,1)S(1)} %all-to-all-done) | data formatting | bytes 2097152 | tf_op jit(solution)/shard_map/reshape | solution.py:160
  55.0 4.3 %shard_map.140 = bf16[4,256,512]{2,1,0:T(8,128)(2,1)} custom-call(bf16[256,2048]{1,0:T(8,128)(2,1)} %reshape.467.x_ref, bf16[2048,256]{1,0:T(8,128)(2,1)} %bitcast.78, bf16[2048,256]{1,0:T(8,128)(2,1)} %bitcast.79, bf16[256,2048]{1,0:T(8,128)(2,1)} %bitcast.80), custom_call_target="tpu_custom_call" | custom-call | tf_op jit(solution)/shard_map/pallas_call | solution.py:102
  59.2 4.4 %all-to-all-start.1 = ((bf16[4,256,512]{2,1,0:T(8,128)(2,1)}), bf16[4,256,512]{2,1,0:T(8,128)(2,1)S(1)}, u32[]{:S(2)}, u32[]{:S(2)}) async-start(bf16[4,256,512]{2,1,0:T(8,128)(2,1)} %shard_map.140), calls=%async_computation.1 | async-start | bytes 2097152 | tf_op jit(solution)/shard_map/all_to_all | solution.py:162
  63.7 0.0 copy-done.3
  63.7 1.6 %fusion.48 = (f32[8,16]{1,0:T(8,128)S(1)}, f32[8,1,16,2048]{3,2,0,1:T(8,128)S(1)}) fusion(bf16[8,16,64]{2,1,0:T(8,128)(2,1)S(1)} %get-tuple-element.7, bf16[8,16,64]{2,1,0:T(8,128)(2,1)S(1)} %get-tuple-element.6, bf16[2048,64]{1,0:T(8,128)(2,1)} %get-tuple-element.5, bf16[2048,64]{1,0:T(8,128)(2,1)S(1)} %get-tuple-element.4, pred[8,2048]{1,0:T(8,128)(4,1)S(1)} %fusion.27), kind=kOutput, calls=%fused_computation.94 | convolution fusion | flops 69009280 | bytes 1622528 | tf_op jit(solution)/shard_map/rgqd,cgd->rgqc/dot_general | solution.py:56
  65.3 0.0 copy-start.6
  65.3 11.9 %all-to-all-done.1 = bf16[4,256,512]{2,1,0:T(8,128)(2,1)S(1)} async-done(((bf16[4,256,512]{2,1,0:T(8,128)(2,1)}), bf16[4,256,512]{2,1,0:T(8,128)(2,1)S(1)}, u32[]{:S(2)}, u32[]{:S(2)}) %all-to-all-start.1) | async-done | bytes 1048608 | tf_op jit(solution)/shard_map/all_to_all | solution.py:162
  77.3 0.2 reduce_sum.75
  77.5 0.8 reduce_sum.76
  78.3 7.6 %all-to-all-start.2 = ((bf16[128,2,512]{2,1,0:T(2,128)(2,1)}), bf16[128,2,512]{2,1,0:T(2,128)(2,1)S(1)}, u32[]{:S(2)}, u32[]{:S(2)}) async-start(bf16[128,2,512]{2,1,0:T(2,128)(2,1)} %reduce_sum.76), calls=%async_computation.2 | async-start | bytes 524288 | tf_op jit(solution)/shard_map/all_to_all | solution.py:165
  86.0 0.1 copy.24
  86.0 0.1 select_reduce_fusion.1
  86.2 0.3 fusion.14
  86.5 14.2 %all-to-all-done.2 = bf16[128,2,512]{2,1,0:T(2,128)(2,1)S(1)} async-done(((bf16[128,2,512]{2,1,0:T(2,128)(2,1)}), bf16[128,2,512]{2,1,0:T(2,128)(2,1)S(1)}, u32[]{:S(2)}, u32[]{:S(2)}) %all-to-all-start.2) | async-done | bytes 262176 | tf_op jit(solution)/shard_map/all_to_all | solution.py:165
  100.7 0.1 reshape.481
  100.8 0.9 convolution_convert_fusion.1
  101.7 3.3 %all-to-all-start.3 = ((bf16[4,16,512]{2,1,0:T(8,128)(2,1)}), bf16[4,16,512]{2,1,0:T(8,128)(2,1)S(1)}, u32[]{:S(2)}, u32[]{:S(2)}) async-start(bf16[4,16,512]{2,1,0:T(8,128)(2,1)} %convolution_convert_fusion.1), calls=%async_computation.3 | async-start | bytes 131072 | tf_op jit(solution)/shard_map/all_to_all | solution.py:180
  105.0 0.4 fusion.9
  105.3 0.6 copy.36
  106.0 4.6 %all-to-all-done.3 = bf16[4,16,512]{2,1,0:T(8,128)(2,1)S(1)} async-done(((bf16[4,16,512]{2,1,0:T(8,128)(2,1)}), bf16[4,16,512]{2,1,0:T(8,128)(2,1)S(1)}, u32[]{:S(2)}, u32[]{:S(2)}) %all-to-all-start.3) | async-done | bytes 65568 | tf_op jit(solution)/shard_map/all_to_all | solution.py:180
  110.5 0.6 copy.28
  (21 shorter events, 0.1 us)
Async XLA Ops:
  0.6 104.3 %copy-start = (bf16[2048,128]{1,0:T(8,128)(2,1)S(1)}, bf16[2048,128]{1,0:T(8,128)(2,1)}, u32[]{:S(2)}) copy-start(bf16[2048,128]{1,0:T(8,128)(2,1)} %param.22) | copy-start | bytes 1572868
  4.8 17.6 %copy-start.7 = (s32[8]{0:T(128)S(1)}, s32[8]{0:T(128)}, u32[]{:S(2)}) copy-start(s32[8]{0:T(128)} %param.25) | copy-start | bytes 100
  4.8 17.8 %copy-start.2 = (bf16[8,2048]{1,0:T(8,128)(2,1)S(1)}, bf16[8,2048]{1,0:T(8,128)(2,1)}, u32[]{:S(2)}) copy-start(bf16[8,2048]{1,0:T(8,128)(2,1)} %param.19) | copy-start | bytes 98308
  4.8 17.9 %copy-start.5 = (bf16[8,128]{1,0:T(8,128)(2,1)S(1)}, bf16[8,128]{1,0:T(8,128)(2,1)}, u32[]{:S(2)}) copy-start(bf16[8,128]{1,0:T(8,128)(2,1)} %param.23) | copy-start | bytes 6148
  4.8 18.7 %copy-start.1 = (bf16[2048,128]{1,0:T(8,128)(2,1)S(1)}, bf16[2048,128]{1,0:T(8,128)(2,1)}, u32[]{:S(2)}) copy-start(bf16[2048,128]{1,0:T(8,128)(2,1)} %param.20) | copy-start | bytes 1572868
  4.8 18.7 %copy-start.4 = (f32[1,2048]{1,0:T(1,128)S(1)}, f32[1,2048]{1,0:T(1,128)}, u32[]{:S(2)}) copy-start(f32[1,2048]{1,0:T(1,128)} %param.21) | copy-start | bytes 24580
  4.9 48.9 %all-to-all-start = ((bf16[128,2,2048]{2,1,0:T(2,128)(2,1)}), bf16[128,2,2048]{2,1,0:T(2,128)(2,1)S(1)}, u32[]{:S(2)}, u32[]{:S(2)}) async-start(bf16[128,2,2048]{2,1,0:T(2,128)(2,1)} %reshape.466), calls=%async_computation | async-start | bytes 2097152 | tf_op jit(solution)/shard_map/all_to_all | solution.py:157
  59.2 4.4 %copy-start.3 = (s32[16,8]{0,1:T(8,128)S(1)}, s32[16,8]{0,1:T(8,128)}, u32[]{:S(2)}) copy-start(s32[16,8]{0,1:T(8,128)} %param.15) | copy-start | bytes 1540
  59.2 18.0 %all-to-all-start.1 = ((bf16[4,256,512]{2,1,0:T(8,128)(2,1)}), bf16[4,256,512]{2,1,0:T(8,128)(2,1)S(1)}, u32[]{:S(2)}, u32[]{:S(2)}) async-start(bf16[4,256,512]{2,1,0:T(8,128)(2,1)} %shard_map.140), calls=%async_computation.1 | async-start | bytes 2097152 | tf_op jit(solution)/shard_map/all_to_all | solution.py:162
  65.3 20.6 %copy-start.6 = (bf16[8,128]{1,0:T(8,128)(2,1)S(1)}, bf16[8,128]{1,0:T(8,128)(2,1)}, u32[]{:S(2)}) copy-start(bf16[8,128]{1,0:T(8,128)(2,1)} %param.24) | copy-start | bytes 6148
  78.3 22.4 %all-to-all-start.2 = ((bf16[128,2,512]{2,1,0:T(2,128)(2,1)}), bf16[128,2,512]{2,1,0:T(2,128)(2,1)S(1)}, u32[]{:S(2)}, u32[]{:S(2)}) async-start(bf16[128,2,512]{2,1,0:T(2,128)(2,1)} %reduce_sum.76), calls=%async_computation.2 | async-start | bytes 524288 | tf_op jit(solution)/shard_map/all_to_all | solution.py:165
  101.7 8.9 %all-to-all-start.3 = ((bf16[4,16,512]{2,1,0:T(8,128)(2,1)}), bf16[4,16,512]{2,1,0:T(8,128)(2,1)S(1)}, u32[]{:S(2)}, u32[]{:S(2)}) async-start(bf16[4,16,512]{2,1,0:T(8,128)(2,1)} %convolution_convert_fusion.1), calls=%async_computation.3 | async-start | bytes 131072 | tf_op jit(solution)/shard_map/all_to_all | solution.py:180

commit v8 on v7

--- a/solution.py
+++ b/solution.py
@@ -83,28 +83,50 @@
     )
 
 
-def expert_kernel(x_ref, gate_ref, up_ref, down_ref, out_ref):
+def expert_kernel(x_ref, gate_ref, up_ref, down_ref, out_ref, acc_ref):
+    step = pl.program_id(0)
     inputs = x_ref[...]
     gate_act = jnp.dot(inputs, gate_ref[...], preferred_element_type=jnp.float32)
     up_act = jnp.dot(inputs, up_ref[...], preferred_element_type=jnp.float32)
     hidden_act = (gate_act / (1.0 + jnp.exp(-gate_act)) * up_act).astype(jnp.bfloat16)
     partial_value = jnp.dot(hidden_act, down_ref[...], preferred_element_type=jnp.float32)
-    pieces = out_ref.shape[0]
-    width = out_ref.shape[2]
-    for piece in range(pieces):
-        out_ref[piece] = partial_value[:, piece * width:(piece + 1) * width].astype(out_ref.dtype)
+
+    @pl.when(step == 0)
+    def _():
+        acc_ref[...] = partial_value
+
+    @pl.when(step > 0)
+    def _():
+        acc_ref[...] += partial_value
+
+    @pl.when(step == pl.num_programs(0) - 1)
+    def _():
+        pieces = out_ref.shape[0]
+        width = out_ref.shape[2]
+        for piece in range(pieces):
+            out_ref[piece] = acc_ref[:, piece * width:(piece + 1) * width].astype(out_ref.dtype)
 
 
 def expert_ffn(inputs, gate_w, up_w, down_w, pieces):
-    rows = inputs.shape[0]
+    rows, model_width = inputs.shape
+    hidden_width = gate_w.shape[1]
+    chunk = 128 if hidden_width % 128 == 0 else hidden_width
     width = down_w.shape[1] // pieces
-    in_vmem = pl.BlockSpec(memory_space=pltpu.VMEM)
     return pl.pallas_call(
         expert_kernel,
         out_shape=jax.ShapeDtypeStruct((pieces, rows, width), jnp.bfloat16),
-        in_specs=[in_vmem, in_vmem, in_vmem, in_vmem],
-        out_specs=pl.BlockSpec(memory_space=pltpu.VMEM),
+        grid=(hidden_width // chunk,),
+        in_specs=[
+            pl.BlockSpec((rows, model_width), lambda i: (0, 0)),
+            pl.BlockSpec((model_width, chunk), lambda i: (0, i)),
+            pl.BlockSpec((model_width, chunk), lambda i: (0, i)),
+            pl.BlockSpec((chunk, down_w.shape[1]), lambda i: (i, 0)),
+        ],
+        out_specs=pl.BlockSpec((pieces, rows, width), lambda i: (0, 0, 0)),
+        scratch_shapes=[pltpu.VMEM((rows, down_w.shape[1]), jnp.float32)],
+        compiler_params=pltpu.CompilerParams(dimension_semantics=("arbitrary",)),
     )(inputs, gate_w, up_w, down_w)
+
 
 def expert_block(arrived, w_gate, w_up, w_down):
     arrived_shape = arrived.shape

time: 112 us -> 113 us (level)
    pallas_call x1, Pallas kernels: 4.25 us -> 5.38 us  [expert_ffn(): pl.pallas_call(expert_kernel, out_shape=jax.ShapeDtypeStruct((pieces, row...]
where the time goes in v8:
time: 113 us; the launch traced here: 112 us
  waiting for transfers between devices  55.1 us (49%)
  starting transfers between devices  32.9 us (29%)
  other arithmetic  7.67 us (7%)
  local copies, waits for them, and re-layouts  6.02 us (5%)
  Pallas kernels  5.38 us (5%)
  matrix products  4.35 us (4%)
    all_to_all x1, waiting for transfers between devices, on_device(): lax.all_to_all(outgoing, 'dp', split_axis=0, concat_axis=0, tiled=True)  24.4 us
    all_to_all x1, starting transfers between devices, on_device(): lax.all_to_all(outgoing, 'dp', split_axis=0, concat_axis=0, tiled=True)  17.5 us
    all_to_all x1, waiting for transfers between devices, on_device(): lax.all_to_all(expert_out, 'dp', split_axis=0, concat_axis=0, tiled=True)  14.2 us
    all_to_all x1, waiting for transfers between devices, on_device(): lax.all_to_all(partial_value, 'tp', split_axis=0, concat_axis=0, tiled=True)  11.9 us
    all_to_all x1, starting transfers between devices, on_device(): lax.all_to_all(expert_out, 'dp', split_axis=0, concat_axis=0, tiled=True)  7.62 us
    concatenate x4, other arithmetic, rotate(): jnp.concatenate([front_half * cosine - back_half * sine_part, back_half *...  5.72 us
    pallas_call x1, Pallas kernels, expert_ffn(): pl.pallas_call(expert_kernel, out_shape=jax.ShapeDtypeStruct((pieces, row...  5.38 us
    all_to_all x1, waiting for transfers between devices, on_device(): lax.all_to_all(spread, 'tp', split_axis=0, concat_axis=0, tiled=True)  4.59 us
  transfers between devices with their start and end apart: 4, of which 4 were waited for; matrix products, arithmetic and copies ran while one was open for 9% of the time, Pallas kernels for 0%

profile of v8, /device:TPU:8, one launch (start us, length us, event | category | flops | bytes accessed | tf_op | source)
XLA Modules:
  0.0 112.3 jit_solution(5403175635013983780)
XLA Ops:
  0.6 0.0 copy-start
  0.6 0.8 copy.22
  1.5 0.1 eq.26
  1.5 0.2 convert_reduce_fusion
  1.7 0.1 fusion.24
  1.9 0.1 select_reduce_fusion
  2.0 1.3 %convolution_convert_fusion = bf16[256,2048]{1,0:T(8,128)(2,1)S(1)} fusion(bf16[16,2048]{1,0:T(8,128)(2,1)} %param.13, s32[256]{0:T(256)S(1)} %broadcast_select_fusion), kind=kOutput, calls=%fused_computation | convolution fusion | flops 17305600 | bytes 1115136 | tf_op jit(solution)/shard_map/dot_general | solution.py:177
  3.3 1.5 %reshape.466 = bf16[128,2,2048]{2,1,0:T(2,128)(2,1)} reshape(bf16[256,2048]{1,0:T(8,128)(2,1)S(1)} %convolution_convert_fusion) | data formatting | bytes 2097152 | tf_op jit(solution)/shard_map/reshape | solution.py:178
  4.8 0.0 copy-start.4
  4.9 17.5 %all-to-all-start = ((bf16[128,2,2048]{2,1,0:T(2,128)(2,1)}), bf16[128,2,2048]{2,1,0:T(2,128)(2,1)S(1)}, u32[]{:S(2)}, u32[]{:S(2)}) async-start(bf16[128,2,2048]{2,1,0:T(2,128)(2,1)} %reshape.466), calls=%async_computation | async-start | bytes 2097152 | tf_op jit(solution)/shard_map/all_to_all | solution.py:179
  22.4 0.1 reduce_sum.71
  22.5 0.0 copy-done.7
  22.5 0.2 reduce-window.8
  22.7 0.0 copy-done.2
  22.7 0.0 copy-done.5
  22.7 0.1 multiply_cosine_fusion.2
  22.8 0.1 fusion.43
  23.0 0.1 select_reduce_fusion.2
  23.1 0.1 maximum_bitcast_fusion.2
  23.1 0.1 fusion.29
  23.2 0.2 fusion.36
  23.4 0.1 fusion.27
  23.5 0.0 copy-done.1
  23.5 0.0 copy-done.4
  23.6 0.3 multiply_bitcast_fusion
  23.9 5.4 %fusion.23 = (bf16[2048,64]{1,0:T(8,128)(2,1)S(1)}, bf16[2048,64]{1,0:T(8,128)(2,1)}) fusion(f32[2048,1,128]{2,0,1:T(8,128)S(1)} %multiply_bitcast_fusion, f32[64]{0:T(128)S(1)} %multiply_exponential_fusion, f32[2048]{0:T(1024)S(1)} %subtract_convert_fusion.1), kind=kLoop, calls=%fused_computation.31 | loop fusion | flops 1179648 | bytes 1581312 | tf_op jit(solution)/shard_map/concatenate | solution.py:22
  29.3 24.4 %all-to-all-done = bf16[128,2,2048]{2,1,0:T(2,128)(2,1)S(1)} async-done(((bf16[128,2,2048]{2,1,0:T(2,128)(2,1)}), bf16[128,2,2048]{2,1,0:T(2,128)(2,1)S(1)}, u32[]{:S(2)}, u32[]{:S(2)}) %all-to-all-start) | async-done | bytes 1048608 | tf_op jit(solution)/shard_map/all_to_all | solution.py:179
  53.8 1.2 %reshape.467.x_ref = bf16[256,2048]{1,0:T(8,128)(2,1)} reshape(bf16[128,2,2048]{2,1,0:T(2,128)(2,1)S(1)} %all-to-all-done) | data formatting | bytes 2097152 | tf_op jit(solution)/shard_map/reshape | solution.py:182
  55.0 5.4 %shard_map.140 = bf16[4,256,512]{2,1,0:T(8,128)(2,1)} custom-call(bf16[256,2048]{1,0:T(8,128)(2,1)} %reshape.467.x_ref, bf16[2048,256]{1,0:T(8,128)(2,1)} %bitcast.78, bf16[2048,256]{1,0:T(8,128)(2,1)} %bitcast.79, bf16[256,2048]{1,0:T(8,128)(2,1)} %bitcast.80), custom_call_target="tpu_custom_call" | custom-call | tf_op jit(solution)/shard_map/pallas_call | solution.py:115
  60.4 4.4 %all-to-all-start.1 = ((bf16[4,256,512]{2,1,0:T(8,128)(2,1)}), bf16[4,256,512]{2,1,0:T(8,128)(2,1)S(1)}, u32[]{:S(2)}, u32[]{:S(2)}) async-start(bf16[4,256,512]{2,1,0:T(8,128)(2,1)} %shard_map.140), calls=%async_computation.1 | async-start | bytes 2097152 | tf_op jit(solution)/shard_map/all_to_all | solution.py:184
  64.8 0.0 copy-done.3
  64.8 1.6 %fusion.48 = (f32[8,16]{1,0:T(8,128)S(1)}, f32[8,1,16,2048]{3,2,0,1:T(8,128)S(1)}) fusion(bf16[8,16,64]{2,1,0:T(8,128)(2,1)S(1)} %get-tuple-element.7, bf16[8,16,64]{2,1,0:T(8,128)(2,1)S(1)} %get-tuple-element.6, bf16[2048,64]{1,0:T(8,128)(2,1)} %get-tuple-element.5, bf16[2048,64]{1,0:T(8,128)(2,1)S(1)} %get-tuple-element.4, pred[8,2048]{1,0:T(8,128)(4,1)S(1)} %fusion.27), kind=kOutput, calls=%fused_computation.94 | convolution fusion | flops 69009280 | bytes 1622528 | tf_op jit(solution)/shard_map/rgqd,cgd->rgqc/dot_general | solution.py:56
  66.4 0.0 copy-start.6
  66.5 11.9 %all-to-all-done.1 = bf16[4,256,512]{2,1,0:T(8,128)(2,1)S(1)} async-done(((bf16[4,256,512]{2,1,0:T(8,128)(2,1)}), bf16[4,256,512]{2,1,0:T(8,128)(2,1)S(1)}, u32[]{:S(2)}, u32[]{:S(2)}) %all-to-all-start.1) | async-done | bytes 1048608 | tf_op jit(solution)/shard_map/all_to_all | solution.py:184
  78.4 0.2 reduce_sum.75
  78.6 0.8 reduce_sum.76
  79.4 7.6 %all-to-all-start.2 = ((bf16[128,2,512]{2,1,0:T(2,128)(2,1)}), bf16[128,2,512]{2,1,0:T(2,128)(2,1)S(1)}, u32[]{:S(2)}, u32[]{:S(2)}) async-start(bf16[128,2,512]{2,1,0:T(2,128)(2,1)} %reduce_sum.76), calls=%async_computation.2 | async-start | bytes 524288 | tf_op jit(solution)/shard_map/all_to_all | solution.py:187
  87.1 0.1 copy.24
  87.2 0.1 select_reduce_fusion.1
  87.3 0.3 fusion.14
  87.6 14.2 %all-to-all-done.2 = bf16[128,2,512]{2,1,0:T(2,128)(2,1)S(1)} async-done(((bf16[128,2,512]{2,1,0:T(2,128)(2,1)}), bf16[128,2,512]{2,1,0:T(2,128)(2,1)S(1)}, u32[]{:S(2)}, u32[]{:S(2)}) %all-to-all-start.2) | async-done | bytes 262176 | tf_op jit(solution)/shard_map/all_to_all | solution.py:187
  101.8 0.1 reshape.481
  101.9 0.9 convolution_convert_fusion.1
  102.8 3.3 %all-to-all-start.3 = ((bf16[4,16,512]{2,1,0:T(8,128)(2,1)}), bf16[4,16,512]{2,1,0:T(8,128)(2,1)S(1)}, u32[]{:S(2)}, u32[]{:S(2)}) async-start(bf16[4,16,512]{2,1,0:T(8,128)(2,1)} %convolution_convert_fusion.1), calls=%async_computation.3 | async-start | bytes 131072 | tf_op jit(solution)/shard_map/all_to_all | solution.py:202
  106.1 0.4 fusion.9
  106.5 0.6 copy.36
  107.1 4.6 %all-to-all-done.3 = bf16[4,16,512]{2,1,0:T(8,128)(2,1)S(1)} async-done(((bf16[4,16,512]{2,1,0:T(8,128)(2,1)}), bf16[4,16,512]{2,1,0:T(8,128)(2,1)S(1)}, u32[]{:S(2)}, u32[]{:S(2)}) %all-to-all-start.3) | async-done | bytes 65568 | tf_op jit(solution)/shard_map/all_to_all | solution.py:202
  111.7 0.6 copy.28
  (21 shorter events, 0.1 us)
Async XLA Ops:
  0.6 105.5 %copy-start = (bf16[2048,128]{1,0:T(8,128)(2,1)S(1)}, bf16[2048,128]{1,0:T(8,128)(2,1)}, u32[]{:S(2)}) copy-start(bf16[2048,128]{1,0:T(8,128)(2,1)} %param.22) | copy-start | bytes 1572868
  4.8 17.6 %copy-start.7 = (s32[8]{0:T(128)S(1)}, s32[8]{0:T(128)}, u32[]{:S(2)}) copy-start(s32[8]{0:T(128)} %param.25) | copy-start | bytes 100
  4.8 17.8 %copy-start.2 = (bf16[8,2048]{1,0:T(8,128)(2,1)S(1)}, bf16[8,2048]{1,0:T(8,128)(2,1)}, u32[]{:S(2)}) copy-start(bf16[8,2048]{1,0:T(8,128)(2,1)} %param.19) | copy-start | bytes 98308
  4.8 17.9 %copy-start.5 = (bf16[8,128]{1,0:T(8,128)(2,1)S(1)}, bf16[8,128]{1,0:T(8,128)(2,1)}, u32[]{:S(2)}) copy-start(bf16[8,128]{1,0:T(8,128)(2,1)} %param.23) | copy-start | bytes 6148
  4.8 18.7 %copy-start.1 = (bf16[2048,128]{1,0:T(8,128)(2,1)S(1)}, bf16[2048,128]{1,0:T(8,128)(2,1)}, u32[]{:S(2)}) copy-start(bf16[2048,128]{1,0:T(8,128)(2,1)} %param.20) | copy-start | bytes 1572868
  4.8 18.7 %copy-start.4 = (f32[1,2048]{1,0:T(1,128)S(1)}, f32[1,2048]{1,0:T(1,128)}, u32[]{:S(2)}) copy-start(f32[1,2048]{1,0:T(1,128)} %param.21) | copy-start | bytes 24580
  4.9 48.9 %all-to-all-start = ((bf16[128,2,2048]{2,1,0:T(2,128)(2,1)}), bf16[128,2,2048]{2,1,0:T(2,128)(2,1)S(1)}, u32[]{:S(2)}, u32[]{:S(2)}) async-start(bf16[128,2,2048]{2,1,0:T(2,128)(2,1)} %reshape.466), calls=%async_computation | async-start | bytes 2097152 | tf_op jit(solution)/shard_map/all_to_all | solution.py:179
  60.4 4.4 %copy-start.3 = (s32[16,8]{0,1:T(8,128)S(1)}, s32[16,8]{0,1:T(8,128)}, u32[]{:S(2)}) copy-start(s32[16,8]{0,1:T(8,128)} %param.15) | copy-start | bytes 1540
  60.4 18.0 %all-to-all-start.1 = ((bf16[4,256,512]{2,1,0:T(8,128)(2,1)}), bf16[4,256,512]{2,1,0:T(8,128)(2,1)S(1)}, u32[]{:S(2)}, u32[]{:S(2)}) async-start(bf16[4,256,512]{2,1,0:T(8,128)(2,1)} %shard_map.140), calls=%async_computation.1 | async-start | bytes 2097152 | tf_op jit(solution)/shard_map/all_to_all | solution.py:184
  66.4 20.6 %copy-start.6 = (bf16[8,128]{1,0:T(8,128)(2,1)S(1)}, bf16[8,128]{1,0:T(8,128)(2,1)}, u32[]{:S(2)}) copy-start(bf16[8,128]{1,0:T(8,128)(2,1)} %param.24) | copy-start | bytes 6148
  79.4 22.4 %all-to-all-start.2 = ((bf16[128,2,512]{2,1,0:T(2,128)(2,1)}), bf16[128,2,512]{2,1,0:T(2,128)(2,1)S(1)}, u32[]{:S(2)}, u32[]{:S(2)}) async-start(bf16[128,2,512]{2,1,0:T(2,128)(2,1)} %reduce_sum.76), calls=%async_computation.2 | async-start | bytes 524288 | tf_op jit(solution)/shard_map/all_to_all | solution.py:187
  102.8 8.9 %all-to-all-start.3 = ((bf16[4,16,512]{2,1,0:T(8,128)(2,1)}), bf16[4,16,512]{2,1,0:T(8,128)(2,1)S(1)}, u32[]{:S(2)}, u32[]{:S(2)}) async-start(bf16[4,16,512]{2,1,0:T(8,128)(2,1)} %convolution_convert_fusion.1), calls=%async_computation.3 | async-start | bytes 131072 | tf_op jit(solution)/shard_map/all_to_all | solution.py:202

commit v9 on v5

--- a/solution.py
+++ b/solution.py
@@ -131,8 +131,11 @@
     outgoing = outgoing.reshape(experts, capacity, model_width)
     arrived = lax.all_to_all(outgoing, "dp", split_axis=0, concat_axis=0, tiled=True)
     slots = dp_size * capacity
-    gate_act = jnp.einsum("ecd,dh->ech", arrived, w_gate[0], preferred_element_type=jnp.float32)
-    up_act = jnp.einsum("ecd,dh->ech", arrived, w_up[0], preferred_element_type=jnp.float32)
+    hidden_width = w_gate.shape[2]
+    gate_up_w = jnp.concatenate([w_gate[0], w_up[0]], axis=1)
+    gate_up = jnp.einsum("ecd,dh->ech", arrived, gate_up_w, preferred_element_type=jnp.float32)
+    gate_act = gate_up[..., :hidden_width]
+    up_act = gate_up[..., hidden_width:]
     hidden_act = (jax.nn.silu(gate_act) * up_act).astype(jnp.bfloat16).reshape(slots, -1)
     down_w = w_down[0].reshape(w_down.shape[1], tp_size, slice_width)
     partial_value = jnp.einsum("sh,hcd->csd", hidden_act, down_w, preferred_element_type=jnp.float32)

time: 112 us -> 110 us (0.982)
  matrix products: 9.33 us -> 7.5 us
  waiting for transfers between devices: 52.6 us -> 53.9 us
    dot_general x2 -> x1, matrix products: 3.98 us -> 2.3 us  [on_device(): jnp.einsum('ecd,dh->ech', arrived, gate_up_w, preferred_element_type=jnp....]
    all_to_all x1, waiting for transfers between devices: 22 us -> 23.2 us  [on_device(): lax.all_to_all(outgoing, 'dp', split_axis=0, concat_axis=0, tiled=True)]
  transfers between devices with their start and end apart: 4 -> 4, of which waited for: 4 -> 4; matrix products, arithmetic and copies ran while one was open for 11% -> 10% of each run, Pallas kernels for 0% -> 0%
where the time goes in v9:
time: 110 us
  waiting for transfers between devices  53.9 us (49%)
  starting transfers between devices  33.3 us (30%)
  other arithmetic  7.75 us (7%)
  matrix products  7.5 us (7%)
  local copies, waits for them, and re-layouts  6.45 us (6%)
    all_to_all x1, waiting for transfers between devices, on_device(): lax.all_to_all(outgoing, 'dp', split_axis=0, concat_axis=0, tiled=True)  23.2 us
    all_to_all x1, starting transfers between devices, on_device(): lax.all_to_all(outgoing, 'dp', split_axis=0, concat_axis=0, tiled=True)  18 us
    all_to_all x1, waiting for transfers between devices, on_device(): lax.all_to_all(expert_out, 'dp', split_axis=0, concat_axis=0, tiled=True)  14.2 us
    all_to_all x1, waiting for transfers between devices, on_device(): lax.all_to_all(partial_value, 'tp', split_axis=0, concat_axis=0, tiled=True)  11.9 us
    all_to_all x1, starting transfers between devices, on_device(): lax.all_to_all(expert_out, 'dp', split_axis=0, concat_axis=0, tiled=True)  7.62 us
    concatenate x4, other arithmetic, rotate(): jnp.concatenate([front_half * cosine - back_half * sine_part, back_half *...  5.72 us
    all_to_all x1, waiting for transfers between devices, on_device(): lax.all_to_all(spread, 'tp', split_axis=1, concat_axis=1, tiled=True)  4.58 us
    all_to_all x1, starting transfers between devices, on_device(): lax.all_to_all(partial_value, 'tp', split_axis=0, concat_axis=0, tiled=True)  4.42 us
  transfers between devices with their start and end apart: 4, of which 4 were waited for; matrix products, arithmetic and copies ran while one was open for 10% of the time, Pallas kernels for 0%

profile of v9, /device:TPU:8, one launch (start us, length us, event | category | flops | bytes accessed | tf_op | source)
XLA Modules:
  0.0 109.9 jit_solution(3870151631322848324)
XLA Ops:
  0.6 0.0 copy-start
  0.6 0.8 copy.39
  1.5 0.1 eq.26
  1.5 0.2 convert_reduce_fusion
  1.7 0.1 fusion.31
  1.9 0.1 select_reduce_fusion
  2.0 1.3 %convolution_convert_fusion = bf16[256,2048]{1,0:T(8,128)(2,1)S(1)} fusion(bf16[16,2048]{1,0:T(8,128)(2,1)} %param.13, s32[256]{0:T(256)S(1)} %broadcast_select_fusion), kind=kOutput, calls=%fused_computation | convolution fusion | flops 17305600 | bytes 1115136 | tf_op jit(solution)/shard_map/dot_general | solution.py:130
  3.3 1.5 %reshape.467 = bf16[128,2,2048]{2,1,0:T(2,128)(2,1)} reshape(bf16[256,2048]{1,0:T(8,128)(2,1)S(1)} %convolution_convert_fusion) | data formatting | bytes 2097152 | tf_op jit(solution)/shard_map/reshape | solution.py:131
  4.8 18.0 %all-to-all-start = ((bf16[128,2,2048]{2,1,0:T(2,128)(2,1)}), bf16[128,2,2048]{2,1,0:T(2,128)(2,1)}, u32[]{:S(2)}, u32[]{:S(2)}) async-start(bf16[128,2,2048]{2,1,0:T(2,128)(2,1)} %reshape.467), calls=%async_computation | async-start | bytes 2097152 | tf_op jit(solution)/shard_map/all_to_all | solution.py:132
  22.8 0.1 reduce_sum.69
  22.9 0.0 copy-start.3
  22.9 0.0 copy-start.8
  23.0 0.0 copy-start.5
  23.0 0.8 reshape_squeeze.3
  23.8 0.2 reduce-window.8
  24.0 0.1 multiply_cosine_fusion.2
  24.1 0.1 fusion.49
  24.3 0.1 select_reduce_fusion.2
  24.4 0.1 maximum_bitcast_fusion.4
  24.4 0.1 fusion.36
  24.5 0.2 fusion.42
  24.7 0.1 fusion.34
  24.9 0.3 multiply_bitcast_fusion
  25.2 5.4 %fusion.29 = (bf16[2048,64]{1,0:T(8,128)(2,1)S(1)}, bf16[2048,64]{1,0:T(8,128)(2,1)}) fusion(f32[2048,1,128]{2,0,1:T(8,128)S(1)} %multiply_bitcast_fusion, f32[64]{0:T(128)S(1)} %multiply_exponential_fusion, f32[2048]{0:T(1024)S(1)} %subtract_convert_fusion.1), kind=kLoop, calls=%fused_computation.39 | loop fusion | flops 1179648 | bytes 1581312 | tf_op jit(solution)/shard_map/concatenate | solution.py:20
  30.6 23.2 %all-to-all-done = bf16[128,2,2048]{2,1,0:T(2,128)(2,1)} async-done(((bf16[128,2,2048]{2,1,0:T(2,128)(2,1)}), bf16[128,2,2048]{2,1,0:T(2,128)(2,1)}, u32[]{:S(2)}, u32[]{:S(2)}) %all-to-all-start) | async-done | bytes 1048608 | tf_op jit(solution)/shard_map/all_to_all | solution.py:132
  53.8 2.3 %fusion.2 = f32[128,2,512]{2,0,1:T(8,128)S(1)} fusion(bf16[2048,256]{1,0:T(8,128)(2,1)S(1)} %bitcast.93, bf16[2048,256]{1,0:T(8,128)(2,1)} %bitcast.94, bf16[128,2,2048]{2,1,0:T(2,128)(2,1)} %all-to-all-done), kind=kOutput, calls=%fused_computation.5 | convolution fusion | flops 541065216 | bytes 3670016 | tf_op jit(solution)/shard_map/ecd,dh->ech/dot_general | solution.py:136
  56.1 0.1 fusion.30
  56.2 0.1 copy.43
  56.4 0.1 reshape.484
  56.4 1.5 %fusion.9 = bf16[4,256,512]{2,1,0:T(8,128)(2,1)} fusion(bf16[256,256,1]{1,0,2:T(8,128)(2,1)S(1)} %reshape.484, bf16[256,4,512]{2,1,0:T(4,128)(2,1)S(1)} %reshape_squeeze.3), kind=kOutput, calls=%fused_computation.15 | convolution fusion | flops 268959744 | bytes 2228224 | tf_op jit(solution)/shard_map/sh,hcd->csd/dot_general | solution.py:141
  58.0 4.4 %all-to-all-start.1 = ((bf16[4,256,512]{2,1,0:T(8,128)(2,1)}), bf16[4,256,512]{2,1,0:T(8,128)(2,1)S(1)}, u32[]{:S(2)}, u32[]{:S(2)}) async-start(bf16[4,256,512]{2,1,0:T(8,128)(2,1)} %fusion.9), calls=%async_computation.1 | async-start | bytes 2097152 | tf_op jit(solution)/shard_map/all_to_all | solution.py:143
  62.4 1.6 %fusion.55 = (f32[8,16]{1,0:T(8,128)S(1)}, f32[8,1,16,2048]{3,2,0,1:T(8,128)S(1)}) fusion(bf16[8,16,64]{2,1,0:T(8,128)(2,1)S(1)} %get-tuple-element.7, bf16[8,16,64]{2,1,0:T(8,128)(2,1)S(1)} %get-tuple-element.6, bf16[2048,64]{1,0:T(8,128)(2,1)} %get-tuple-element.5, bf16[2048,64]{1,0:T(8,128)(2,1)S(1)} %get-tuple-element.4, pred[8,2048]{1,0:T(8,128)(4,1)S(1)} %fusion.34), kind=kOutput, calls=%fused_computation.104 | convolution fusion | flops 69009280 | bytes 1622528 | tf_op jit(solution)/shard_map/rgqd,cgd->rgqc/dot_general | solution.py:54
  64.0 11.9 %all-to-all-done.1 = bf16[4,256,512]{2,1,0:T(8,128)(2,1)S(1)} async-done(((bf16[4,256,512]{2,1,0:T(8,128)(2,1)}), bf16[4,256,512]{2,1,0:T(8,128)(2,1)S(1)}, u32[]{:S(2)}, u32[]{:S(2)}) %all-to-all-start.1) | async-done | bytes 1048608 | tf_op jit(solution)/shard_map/all_to_all | solution.py:143
  76.0 0.2 reduce_sum.73
  76.2 0.8 reshape.469
  77.0 7.6 %all-to-all-start.2 = ((bf16[128,2,512]{2,1,0:T(2,128)(2,1)}), bf16[128,2,512]{2,1,0:T(2,128)(2,1)S(1)}, u32[]{:S(2)}, u32[]{:S(2)}) async-start(bf16[128,2,512]{2,1,0:T(2,128)(2,1)} %reshape.469), calls=%async_computation.2 | async-start | bytes 524288 | tf_op jit(solution)/shard_map/all_to_all | solution.py:146
  84.7 0.1 copy.41
  84.7 0.1 select_reduce_fusion.1
  84.9 0.3 fusion.20
  85.2 14.2 %all-to-all-done.2 = bf16[128,2,512]{2,1,0:T(2,128)(2,1)S(1)} async-done(((bf16[128,2,512]{2,1,0:T(2,128)(2,1)}), bf16[128,2,512]{2,1,0:T(2,128)(2,1)S(1)}, u32[]{:S(2)}, u32[]{:S(2)}) %all-to-all-start.2) | async-done | bytes 262176 | tf_op jit(solution)/shard_map/all_to_all | solution.py:146
  99.4 0.1 reshape.470
  99.5 0.2 convolution_convert_fusion.2
  99.7 0.7 broadcast_in_dim.53
  100.3 3.3 %all-to-all-start.3 = ((bf16[16,4,512]{2,0,1:T(8,128)(2,1)}), bf16[16,4,512]{2,0,1:T(8,128)(2,1)S(1)}, u32[]{:S(2)}, u32[]{:S(2)}) async-start(bf16[16,4,512]{2,0,1:T(8,128)(2,1)} %broadcast_in_dim.53), calls=%async_computation.3 | async-start | bytes 131072 | tf_op jit(solution)/shard_map/all_to_all | solution.py:160
  103.6 0.4 fusion.13
  104.0 0.6 copy.60
  104.6 4.6 %all-to-all-done.3 = bf16[16,4,512]{2,0,1:T(8,128)(2,1)S(1)} async-done(((bf16[16,4,512]{2,0,1:T(8,128)(2,1)}), bf16[16,4,512]{2,0,1:T(8,128)(2,1)S(1)}, u32[]{:S(2)}, u32[]{:S(2)}) %all-to-all-start.3) | async-done | bytes 65568 | tf_op jit(solution)/shard_map/all_to_all | solution.py:160
  109.2 0.6 copy.48
  (30 shorter events, 0.2 us)
Async XLA Ops:
  0.6 103.0 %copy-start = (bf16[2048,128]{1,0:T(8,128)(2,1)S(1)}, bf16[2048,128]{1,0:T(8,128)(2,1)}, u32[]{:S(2)}) copy-start(bf16[2048,128]{1,0:T(8,128)(2,1)} %param.22) | copy-start | bytes 1572868
  4.8 18.1 %copy-start.1 = (bf16[1,256,2048]{2,1,0:T(8,128)(2,1)S(1)}, bf16[1,256,2048]{2,1,0:T(8,128)(2,1)}, u32[]{:S(2)}) copy-start(bf16[1,256,2048]{2,1,0:T(8,128)(2,1)} %param.18) | copy-start | bytes 3145732
  4.8 49.0 %all-to-all-start = ((bf16[128,2,2048]{2,1,0:T(2,128)(2,1)}), bf16[128,2,2048]{2,1,0:T(2,128)(2,1)}, u32[]{:S(2)}, u32[]{:S(2)}) async-start(bf16[128,2,2048]{2,1,0:T(2,128)(2,1)} %reshape.467), calls=%async_computation | async-start | bytes 2097152 | tf_op jit(solution)/shard_map/all_to_all | solution.py:132
  22.9 0.9 copy-start.3
  22.9 0.9 copy-start.8
  22.9 1.1 copy-start.6
  22.9 1.9 %copy-start.2 = (bf16[2048,128]{1,0:T(8,128)(2,1)S(1)}, bf16[2048,128]{1,0:T(8,128)(2,1)}, u32[]{:S(2)}) copy-start(bf16[2048,128]{1,0:T(8,128)(2,1)} %param.20) | copy-start | bytes 1572868
  23.0 1.9 %copy-start.5 = (f32[1,2048]{1,0:T(1,128)S(1)}, f32[1,2048]{1,0:T(1,128)}, u32[]{:S(2)}) copy-start(f32[1,2048]{1,0:T(1,128)} %param.21) | copy-start | bytes 24580
  25.2 28.6 %copy-start.9 = (bf16[1,2048,256]{2,1,0:T(8,128)(2,1)S(1)}, bf16[1,2048,256]{2,1,0:T(8,128)(2,1)}, u32[]{:S(2)}) copy-start(bf16[1,2048,256]{2,1,0:T(8,128)(2,1)} %param.17) | copy-start | bytes 3145732
  58.0 4.4 %copy-start.4 = (s32[16,8]{0,1:T(8,128)S(1)}, s32[16,8]{0,1:T(8,128)}, u32[]{:S(2)}) copy-start(s32[16,8]{0,1:T(8,128)} %param.15) | copy-start | bytes 1540
  58.0 18.0 %all-to-all-start.1 = ((bf16[4,256,512]{2,1,0:T(8,128)(2,1)}), bf16[4,256,512]{2,1,0:T(8,128)(2,1)S(1)}, u32[]{:S(2)}, u32[]{:S(2)}) async-start(bf16[4,256,512]{2,1,0:T(8,128)(2,1)} %fusion.9), calls=%async_computation.1 | async-start | bytes 2097152 | tf_op jit(solution)/shard_map/all_to_all | solution.py:143
  64.0 20.7 %copy-start.7 = (bf16[8,128]{1,0:T(8,128)(2,1)S(1)}, bf16[8,128]{1,0:T(8,128)(2,1)}, u32[]{:S(2)}) copy-start(bf16[8,128]{1,0:T(8,128)(2,1)} %param.24) | copy-start | bytes 6148
  77.0 22.4 %all-to-all-start.2 = ((bf16[128,2,512]{2,1,0:T(2,128)(2,1)}), bf16[128,2,512]{2,1,0:T(2,128)(2,1)S(1)}, u32[]{:S(2)}, u32[]{:S(2)}) async-start(bf16[128,2,512]{2,1,0:T(2,128)(2,1)} %reshape.469), calls=%async_computation.2 | async-start | bytes 524288 | tf_op jit(solution)/shard_map/all_to_all | solution.py:146
  100.3 8.9 %all-to-all-start.3 = ((bf16[16,4,512]{2,0,1:T(8,128)(2,1)}), bf16[16,4,512]{2,0,1:T(8,128)(2,1)S(1)}, u32[]{:S(2)}, u32[]{:S(2)}) async-start(bf16[16,4,512]{2,0,1:T(8,128)(2,1)} %broadcast_in_dim.53), calls=%async_computation.3 | async-start | bytes 131072 | tf_op jit(solution)/shard_map/all_to_all | solution.py:160

commit v10 on v9

--- a/solution.py
+++ b/solution.py
@@ -114,18 +114,16 @@
     slice_width = model_width // tp_size
     experts = dp_size * w_gate.shape[0]
     capacity = min(token_count, max(2, token_count * top_count * 2 // experts))
-    flat_ids = routes.reshape(-1)
-    pair_count = flat_ids.shape[0]
-    pair_pos = jnp.arange(pair_count, dtype=jnp.int32)
-    same_before = (flat_ids[:, None] == flat_ids[None, :]) & (pair_pos[None, :] < pair_pos[:, None])
-    rank_ids = jnp.sum(same_before.astype(jnp.int32), axis=1)
-    slot_ids = flat_ids * capacity + rank_ids
+    expert_pos = jnp.arange(experts, dtype=jnp.int32)
+    token_pos = jnp.arange(token_count, dtype=jnp.int32)
+    chose = jnp.any(routes[:, :, None] == expert_pos[None, None, :], axis=1)
+    first_token = jnp.min(jnp.where(chose, token_pos[:, None], token_count), axis=0)
+    last_token = jnp.max(jnp.where(chose, token_pos[:, None], -1), axis=0)
+    second_token = jnp.where(last_token > first_token, last_token, token_count)
+    slot_token = jnp.stack([first_token, second_token], axis=1).reshape(-1)
+    rank_grid = (token_pos[:, None] != first_token[routes]).astype(jnp.int32)
+    slot_ids = (routes * capacity + rank_grid).reshape(-1)
     slot_pos = jnp.arange(experts * capacity, dtype=jnp.int32)
-    token_of_pair = pair_pos // top_count
-    token_pos = jnp.arange(token_count, dtype=jnp.int32)
-    slot_hit = slot_pos[:, None] == slot_ids[None, :]
-    slot_token = jnp.sum(jnp.where(slot_hit, token_of_pair[None, :], 0), axis=1)
-    slot_token = jnp.where(jnp.any(slot_hit, axis=1), slot_token, token_count)
     selector = (slot_token[:, None] == token_pos[None, :]).astype(hidden.dtype)
     outgoing = jnp.dot(selector, hidden, preferred_element_type=jnp.float32).astype(hidden.dtype)
     outgoing = outgoing.reshape(experts, capacity, model_width)

time: 110 us -> 110 us (level)
  local copies, waits for them, and re-layouts: 6.45 us -> 8.01 us
  waiting for transfers between devices: 53.9 us -> 52.5 us
    all_to_all x1, waiting for transfers between devices: 23.2 us -> 21.7 us  [on_device(): lax.all_to_all(outgoing, 'dp', split_axis=0, concat_axis=0, tiled=True)]
    gather x0 -> x2, local copies, waits for them, and re-layouts: none -> 1.31 us  [on_device(): rank_grid = (token_pos[:, None] != first_token[routes]).astype(jnp.int32)]
  transfers between devices with their start and end apart: 4 -> 4, of which waited for: 4 -> 4; matrix products, arithmetic and copies ran while one was open for 10% -> 11% of each run, Pallas kernels for 0% -> 0%
where the time goes in v10:
time: 110 us
  waiting for transfers between devices  52.5 us (48%)
  starting transfers between devices  33.3 us (30%)
  local copies, waits for them, and re-layouts  8.01 us (7%)
  other arithmetic  7.49 us (7%)
  matrix products  7.48 us (7%)
    all_to_all x1, waiting for transfers between devices, on_device(): lax.all_to_all(outgoing, 'dp', split_axis=0, concat_axis=0, tiled=True)  21.7 us
    all_to_all x1, starting transfers between devices, on_device(): lax.all_to_all(outgoing, 'dp', split_axis=0, concat_axis=0, tiled=True)  18 us
    all_to_all x1, waiting for transfers between devices, on_device(): lax.all_to_all(expert_out, 'dp', split_axis=0, concat_axis=0, tiled=True)  14.2 us
    all_to_all x1, waiting for transfers between devices, on_device(): lax.all_to_all(partial_value, 'tp', split_axis=0, concat_axis=0, tiled=True)  11.9 us
    all_to_all x1, starting transfers between devices, on_device(): lax.all_to_all(expert_out, 'dp', split_axis=0, concat_axis=0, tiled=True)  7.62 us
    concatenate x4, other arithmetic, rotate(): jnp.concatenate([front_half * cosine - back_half * sine_part, back_half *...  5.73 us
    all_to_all x1, waiting for transfers between devices, on_device(): lax.all_to_all(spread, 'tp', split_axis=1, concat_axis=1, tiled=True)  4.58 us
    all_to_all x1, starting transfers between devices, on_device(): lax.all_to_all(partial_value, 'tp', split_axis=0, concat_axis=0, tiled=True)  4.42 us
  transfers between devices with their start and end apart: 4, of which 4 were waited for; matrix products, arithmetic and copies ran while one was open for 11% of the time, Pallas kernels for 0%

profile of v10, /device:TPU:8, one launch (start us, length us, event | category | flops | bytes accessed | tf_op | source)
XLA Modules:
  0.0 109.7 jit_solution(13615023397241362008)
XLA Ops:
  0.6 0.0 copy-start
  0.6 0.8 copy.46
  1.5 0.1 fusion.32
  1.6 0.1 copy.50
  1.7 0.1 eq.47
  1.9 1.3 %convolution_convert_fusion = bf16[256,2048]{1,0:T(8,128)(2,1)S(1)} fusion(bf16[16,2048]{1,0:T(8,128)(2,1)} %param.13, s32[256]{0:T(256)S(1)} %eq.47), kind=kOutput, calls=%fused_computation.1 | convolution fusion | flops 17305600 | bytes 1115136 | tf_op jit(solution)/shard_map/dot_general | solution.py:128
  3.2 1.5 %reshape.449 = bf16[128,2,2048]{2,1,0:T(2,128)(2,1)} reshape(bf16[256,2048]{1,0:T(8,128)(2,1)S(1)} %convolution_convert_fusion) | data formatting | bytes 2097152 | tf_op jit(solution)/shard_map/reshape | solution.py:129
  4.7 18.0 %all-to-all-start = ((bf16[128,2,2048]{2,1,0:T(2,128)(2,1)}), bf16[128,2,2048]{2,1,0:T(2,128)(2,1)}, u32[]{:S(2)}, u32[]{:S(2)}) async-start(bf16[128,2,2048]{2,1,0:T(2,128)(2,1)} %reshape.449), calls=%async_computation | async-start | bytes 2097152 | tf_op jit(solution)/shard_map/all_to_all | solution.py:130
  22.7 0.1 copy.48
  22.8 0.1 reshape.467
  22.9 1.2 %gather_fusion = s32[128]{0:T(128)S(1)} fusion(s32[128]{0:T(128)S(1)} %get-tuple-element.3, s32[1024]{0:T(1024)S(1)} %pad_clamp_fusion), kind=kCustom, calls=%fused_computation | custom fusion | bytes 1536 | tf_op jit(solution)/shard_map/gather | solution.py:124
  24.1 0.1 reshape.466
  24.3 0.0 copy-start.7
  24.3 0.8 reshape_squeeze.3
  25.1 0.2 reduce-window.8
  25.3 0.1 multiply_cosine_fusion.2
  25.5 0.1 fusion.48
  25.6 0.1 select_reduce_fusion.1
  25.7 0.1 maximum_bitcast_fusion.4
  25.7 0.1 fusion.35
  25.8 0.2 fusion.41
  26.1 0.1 fusion.33
  26.2 0.3 multiply_bitcast_fusion
  26.5 5.5 %fusion.29 = (bf16[2048,64]{1,0:T(8,128)(2,1)S(1)}, bf16[2048,64]{1,0:T(8,128)(2,1)}) fusion(f32[2048,1,128]{2,0,1:T(8,128)S(1)} %multiply_bitcast_fusion, f32[64]{0:T(128)S(1)} %multiply_exponential_fusion, f32[2048]{0:T(1024)S(1)} %subtract_convert_fusion.1), kind=kLoop, calls=%fused_computation.40 | loop fusion | flops 1179648 | bytes 1581312 | tf_op jit(solution)/shard_map/concatenate | solution.py:20
  32.0 21.7 %all-to-all-done = bf16[128,2,2048]{2,1,0:T(2,128)(2,1)} async-done(((bf16[128,2,2048]{2,1,0:T(2,128)(2,1)}), bf16[128,2,2048]{2,1,0:T(2,128)(2,1)}, u32[]{:S(2)}, u32[]{:S(2)}) %all-to-all-start) | async-done | bytes 1048608 | tf_op jit(solution)/shard_map/all_to_all | solution.py:130
  53.7 2.3 %fusion.2 = f32[128,2,512]{2,0,1:T(8,128)S(1)} fusion(bf16[2048,256]{1,0:T(8,128)(2,1)S(1)} %bitcast.98, bf16[2048,256]{1,0:T(8,128)(2,1)} %bitcast.99, bf16[128,2,2048]{2,1,0:T(2,128)(2,1)} %all-to-all-done), kind=kOutput, calls=%fused_computation.6 | convolution fusion | flops 541065216 | bytes 3670016 | tf_op jit(solution)/shard_map/ecd,dh->ech/dot_general | solution.py:134
  56.0 0.1 fusion.30
  56.1 0.1 copy.52
  56.2 0.1 reshape.476
  56.3 1.5 %fusion.9 = bf16[4,256,512]{2,1,0:T(8,128)(2,1)} fusion(bf16[256,256,1]{1,0,2:T(8,128)(2,1)S(1)} %reshape.476, bf16[256,4,512]{2,1,0:T(4,128)(2,1)S(1)} %reshape_squeeze.3), kind=kOutput, calls=%fused_computation.16 | convolution fusion | flops 268959744 | bytes 2228224 | tf_op jit(solution)/shard_map/sh,hcd->csd/dot_general | solution.py:139
  57.8 4.4 %all-to-all-start.1 = ((bf16[4,256,512]{2,1,0:T(8,128)(2,1)}), bf16[4,256,512]{2,1,0:T(8,128)(2,1)S(1)}, u32[]{:S(2)}, u32[]{:S(2)}) async-start(bf16[4,256,512]{2,1,0:T(8,128)(2,1)} %fusion.9), calls=%async_computation.1 | async-start | bytes 2097152 | tf_op jit(solution)/shard_map/all_to_all | solution.py:141
  62.3 1.6 %fusion.54 = (f32[8,16]{1,0:T(8,128)S(1)}, f32[8,1,16,2048]{3,2,0,1:T(8,128)S(1)}) fusion(bf16[8,16,64]{2,1,0:T(8,128)(2,1)S(1)} %get-tuple-element.9, bf16[8,16,64]{2,1,0:T(8,128)(2,1)S(1)} %get-tuple-element.8, bf16[2048,64]{1,0:T(8,128)(2,1)} %get-tuple-element.7, bf16[2048,64]{1,0:T(8,128)(2,1)S(1)} %get-tuple-element.6, pred[8,2048]{1,0:T(8,128)(4,1)S(1)} %fusion.33), kind=kOutput, calls=%fused_computation.102 | convolution fusion | flops 69009280 | bytes 1622528 | tf_op jit(solution)/shard_map/rgqd,cgd->rgqc/dot_general | solution.py:54
  63.9 11.9 %all-to-all-done.1 = bf16[4,256,512]{2,1,0:T(8,128)(2,1)S(1)} async-done(((bf16[4,256,512]{2,1,0:T(8,128)(2,1)}), bf16[4,256,512]{2,1,0:T(8,128)(2,1)S(1)}, u32[]{:S(2)}, u32[]{:S(2)}) %all-to-all-start.1) | async-done | bytes 1048608 | tf_op jit(solution)/shard_map/all_to_all | solution.py:141
  75.8 0.2 reduce_sum.50
  76.1 0.8 reshape.451
  76.9 7.6 %all-to-all-start.2 = ((bf16[128,2,512]{2,1,0:T(2,128)(2,1)}), bf16[128,2,512]{2,1,0:T(2,128)(2,1)S(1)}, u32[]{:S(2)}, u32[]{:S(2)}) async-start(bf16[128,2,512]{2,1,0:T(2,128)(2,1)} %reshape.451), calls=%async_computation.2 | async-start | bytes 524288 | tf_op jit(solution)/shard_map/all_to_all | solution.py:144
  84.5 0.1 copy.49
  84.6 0.1 select_reduce_fusion
  84.7 0.3 fusion.20
  85.0 14.2 %all-to-all-done.2 = bf16[128,2,512]{2,1,0:T(2,128)(2,1)S(1)} async-done(((bf16[128,2,512]{2,1,0:T(2,128)(2,1)}), bf16[128,2,512]{2,1,0:T(2,128)(2,1)S(1)}, u32[]{:S(2)}, u32[]{:S(2)}) %all-to-all-start.2) | async-done | bytes 262176 | tf_op jit(solution)/shard_map/all_to_all | solution.py:144
  99.2 0.1 reshape.452
  99.3 0.2 convolution_convert_fusion.2
  99.5 0.7 broadcast_in_dim.99
  100.2 3.3 %all-to-all-start.3 = ((bf16[16,4,512]{2,0,1:T(8,128)(2,1)}), bf16[16,4,512]{2,0,1:T(8,128)(2,1)S(1)}, u32[]{:S(2)}, u32[]{:S(2)}) async-start(bf16[16,4,512]{2,0,1:T(8,128)(2,1)} %broadcast_in_dim.99), calls=%async_computation.3 | async-start | bytes 131072 | tf_op jit(solution)/shard_map/all_to_all | solution.py:158
  103.5 0.4 fusion.13
  103.9 0.6 copy.69
  104.5 4.6 %all-to-all-done.3 = bf16[16,4,512]{2,0,1:T(8,128)(2,1)S(1)} async-done(((bf16[16,4,512]{2,0,1:T(8,128)(2,1)}), bf16[16,4,512]{2,0,1:T(8,128)(2,1)S(1)}, u32[]{:S(2)}, u32[]{:S(2)}) %all-to-all-start.3) | async-done | bytes 65568 | tf_op jit(solution)/shard_map/all_to_all | solution.py:158
  109.1 0.6 copy.57
  (37 shorter events, 0.2 us)
Async XLA Ops:
  0.6 102.9 %copy-start = (bf16[2048,128]{1,0:T(8,128)(2,1)S(1)}, bf16[2048,128]{1,0:T(8,128)(2,1)}, u32[]{:S(2)}) copy-start(bf16[2048,128]{1,0:T(8,128)(2,1)} %param.22) | copy-start | bytes 1572868
  4.7 18.0 %copy-start.4 = (s32[16,8]{0,1:T(8,128)S(1)}, s32[16,8]{0,1:T(8,128)}, u32[]{:S(2)}) copy-start(s32[16,8]{0,1:T(8,128)} %param.14) | copy-start | bytes 1540
  4.7 49.0 %all-to-all-start = ((bf16[128,2,2048]{2,1,0:T(2,128)(2,1)}), bf16[128,2,2048]{2,1,0:T(2,128)(2,1)}, u32[]{:S(2)}, u32[]{:S(2)}) async-start(bf16[128,2,2048]{2,1,0:T(2,128)(2,1)} %reshape.449), calls=%async_computation | async-start | bytes 2097152 | tf_op jit(solution)/shard_map/all_to_all | solution.py:130
  22.9 1.3 %copy-start.1 = (bf16[1,256,2048]{2,1,0:T(8,128)(2,1)S(1)}, bf16[1,256,2048]{2,1,0:T(8,128)(2,1)}, u32[]{:S(2)}) copy-start(bf16[1,256,2048]{2,1,0:T(8,128)(2,1)} %param.18) | copy-start | bytes 3145732
  24.2 0.9 copy-start.3
  24.2 0.9 copy-start.9
  24.3 1.1 copy-start.7
  24.3 1.9 %copy-start.2 = (bf16[2048,128]{1,0:T(8,128)(2,1)S(1)}, bf16[2048,128]{1,0:T(8,128)(2,1)}, u32[]{:S(2)}) copy-start(bf16[2048,128]{1,0:T(8,128)(2,1)} %param.20) | copy-start | bytes 1572868
  24.3 1.9 %copy-start.6 = (f32[1,2048]{1,0:T(1,128)S(1)}, f32[1,2048]{1,0:T(1,128)}, u32[]{:S(2)}) copy-start(f32[1,2048]{1,0:T(1,128)} %param.21) | copy-start | bytes 24580
  26.5 27.2 %copy-start.10 = (bf16[1,2048,256]{2,1,0:T(8,128)(2,1)S(1)}, bf16[1,2048,256]{2,1,0:T(8,128)(2,1)}, u32[]{:S(2)}) copy-start(bf16[1,2048,256]{2,1,0:T(8,128)(2,1)} %param.17) | copy-start | bytes 3145732
  57.8 4.4 %copy-start.5 = (s32[16,8]{0,1:T(8,128)S(1)}, s32[16,8]{0,1:T(8,128)}, u32[]{:S(2)}) copy-start(s32[16,8]{0,1:T(8,128)} %param.15) | copy-start | bytes 1540
  57.8 18.0 %all-to-all-start.1 = ((bf16[4,256,512]{2,1,0:T(8,128)(2,1)}), bf16[4,256,512]{2,1,0:T(8,128)(2,1)S(1)}, u32[]{:S(2)}, u32[]{:S(2)}) async-start(bf16[4,256,512]{2,1,0:T(8,128)(2,1)} %fusion.9), calls=%async_computation.1 | async-start | bytes 2097152 | tf_op jit(solution)/shard_map/all_to_all | solution.py:141
  63.9 20.7 %copy-start.8 = (bf16[8,128]{1,0:T(8,128)(2,1)S(1)}, bf16[8,128]{1,0:T(8,128)(2,1)}, u32[]{:S(2)}) copy-start(bf16[8,128]{1,0:T(8,128)(2,1)} %param.24) | copy-start | bytes 6148
  76.9 22.4 %all-to-all-start.2 = ((bf16[128,2,512]{2,1,0:T(2,128)(2,1)}), bf16[128,2,512]{2,1,0:T(2,128)(2,1)S(1)}, u32[]{:S(2)}, u32[]{:S(2)}) async-start(bf16[128,2,512]{2,1,0:T(2,128)(2,1)} %reshape.451), calls=%async_computation.2 | async-start | bytes 524288 | tf_op jit(solution)/shard_map/all_to_all | solution.py:144
  100.2 8.9 %all-to-all-start.3 = ((bf16[16,4,512]{2,0,1:T(8,128)(2,1)}), bf16[16,4,512]{2,0,1:T(8,128)(2,1)S(1)}, u32[]{:S(2)}, u32[]{:S(2)}) async-start(bf16[16,4,512]{2,0,1:T(8,128)(2,1)} %broadcast_in_dim.99), calls=%async_computation.3 | async-start | bytes 131072 | tf_op jit(solution)/shard_map/all_to_all | solution.py:158

commit v11 on v9

--- a/solution.py
+++ b/solution.py
@@ -150,15 +150,16 @@
     slot_weight = jnp.sum(
         jnp.where(slot_grid[:, :, None] == slot_pos[None, None, :], shares[:, :, None], 0.0), axis=1
     )
-    mix_cols = jnp.dot(
+    slot_weight = jnp.broadcast_to(slot_weight[None], (tp_size,) + slot_weight.shape)
+    spread = jnp.einsum(
+        "cts,sd->ctd",
         slot_weight,
         returned.reshape(experts * capacity, slice_width).astype(jnp.float32),
         precision=lax.Precision.HIGHEST,
         preferred_element_type=jnp.float32,
     ).astype(jnp.bfloat16)
-    spread = jnp.broadcast_to(mix_cols[:, None, :], (token_count, tp_size, slice_width))
-    expert_mix = lax.all_to_all(spread, "tp", split_axis=1, concat_axis=1, tiled=True)
-    expert_mix = expert_mix.reshape(token_count, model_width)
+    expert_mix = lax.all_to_all(spread, "tp", split_axis=0, concat_axis=0, tiled=True)
+    expert_mix = jnp.transpose(expert_mix, (1, 0, 2)).reshape(token_count, model_width)
     attended = attend_local(
         queries, key_codes, key_scales, cache_values, new_keys, new_values, lengths
     )

time: 110 us -> 110 us (level)
  no operation moved by 1% of the time
where the time goes in v11:
time: 110 us
  waiting for transfers between devices  53.9 us (49%)
  starting transfers between devices  33.3 us (30%)
  matrix products  8.18 us (7%)
  other arithmetic  7.75 us (7%)
  local copies, waits for them, and re-layouts  5.79 us (5%)
    all_to_all x1, waiting for transfers between devices, on_device(): lax.all_to_all(outgoing, 'dp', split_axis=0, concat_axis=0, tiled=True)  23.2 us
    all_to_all x1, starting transfers between devices, on_device(): lax.all_to_all(outgoing, 'dp', split_axis=0, concat_axis=0, tiled=True)  18 us
    all_to_all x1, waiting for transfers between devices, on_device(): lax.all_to_all(expert_out, 'dp', split_axis=0, concat_axis=0, tiled=True)  14.2 us
    all_to_all x1, waiting for transfers between devices, on_device(): lax.all_to_all(partial_value, 'tp', split_axis=0, concat_axis=0, tiled=True)  11.9 us
    all_to_all x1, starting transfers between devices, on_device(): lax.all_to_all(expert_out, 'dp', split_axis=0, concat_axis=0, tiled=True)  7.62 us
    concatenate x4, other arithmetic, rotate(): jnp.concatenate([front_half * cosine - back_half * sine_part, back_half *...  5.72 us
    all_to_all x1, waiting for transfers between devices, on_device(): lax.all_to_all(spread, 'tp', split_axis=0, concat_axis=0, tiled=True)  4.58 us
    all_to_all x1, starting transfers between devices, on_device(): lax.all_to_all(partial_value, 'tp', split_axis=0, concat_axis=0, tiled=True)  4.42 us
  transfers between devices with their start and end apart: 4, of which 4 were waited for; matrix products, arithmetic and copies ran while one was open for 10% of the time, Pallas kernels for 0%

profile of v11, /device:TPU:8, one launch (start us, length us, event | category | flops | bytes accessed | tf_op | source)
XLA Modules:
  0.0 109.9 jit_solution(6462670196019823642)
XLA Ops:
  0.6 0.0 copy-start
  0.6 0.8 copy.34
  1.5 0.1 eq.26
  1.5 0.2 convert_reduce_fusion
  1.7 0.1 fusion.31
  1.9 0.1 select_reduce_fusion
  2.0 1.3 %convolution_convert_fusion = bf16[256,2048]{1,0:T(8,128)(2,1)S(1)} fusion(bf16[16,2048]{1,0:T(8,128)(2,1)} %param.13, s32[256]{0:T(256)S(1)} %broadcast_select_fusion), kind=kOutput, calls=%fused_computation | convolution fusion | flops 17305600 | bytes 1115136 | tf_op jit(solution)/shard_map/dot_general | solution.py:130
  3.3 1.5 %reshape.467 = bf16[128,2,2048]{2,1,0:T(2,128)(2,1)} reshape(bf16[256,2048]{1,0:T(8,128)(2,1)S(1)} %convolution_convert_fusion) | data formatting | bytes 2097152 | tf_op jit(solution)/shard_map/reshape | solution.py:131
  4.8 18.0 %all-to-all-start = ((bf16[128,2,2048]{2,1,0:T(2,128)(2,1)}), bf16[128,2,2048]{2,1,0:T(2,128)(2,1)}, u32[]{:S(2)}, u32[]{:S(2)}) async-start(bf16[128,2,2048]{2,1,0:T(2,128)(2,1)} %reshape.467), calls=%async_computation | async-start | bytes 2097152 | tf_op jit(solution)/shard_map/all_to_all | solution.py:132
  22.8 0.1 reduce_sum.69
  22.9 0.0 copy-start.3
  22.9 0.0 copy-start.8
  23.0 0.0 copy-start.5
  23.0 0.8 reshape_squeeze.3
  23.8 0.2 reduce-window.8
  24.0 0.1 multiply_cosine_fusion.2
  24.1 0.1 fusion.50
  24.3 0.1 select_reduce_fusion.2
  24.4 0.1 maximum_bitcast_fusion.4
  24.4 0.1 fusion.36
  24.5 0.2 fusion.43
  24.7 0.1 fusion.34
  24.9 0.3 multiply_bitcast_fusion
  25.2 5.4 %fusion.29 = (bf16[2048,64]{1,0:T(8,128)(2,1)S(1)}, bf16[2048,64]{1,0:T(8,128)(2,1)}) fusion(f32[2048,1,128]{2,0,1:T(8,128)S(1)} %multiply_bitcast_fusion, f32[64]{0:T(128)S(1)} %multiply_exponential_fusion, f32[2048]{0:T(1024)S(1)} %subtract_convert_fusion.1), kind=kLoop, calls=%fused_computation.39 | loop fusion | flops 1179648 | bytes 1581312 | tf_op jit(solution)/shard_map/concatenate | solution.py:20
  30.6 23.2 %all-to-all-done = bf16[128,2,2048]{2,1,0:T(2,128)(2,1)} async-done(((bf16[128,2,2048]{2,1,0:T(2,128)(2,1)}), bf16[128,2,2048]{2,1,0:T(2,128)(2,1)}, u32[]{:S(2)}, u32[]{:S(2)}) %all-to-all-start) | async-done | bytes 1048608 | tf_op jit(solution)/shard_map/all_to_all | solution.py:132
  53.8 2.3 %fusion.2 = f32[128,2,512]{2,0,1:T(8,128)S(1)} fusion(bf16[2048,256]{1,0:T(8,128)(2,1)S(1)} %bitcast.93, bf16[2048,256]{1,0:T(8,128)(2,1)} %bitcast.94, bf16[128,2,2048]{2,1,0:T(2,128)(2,1)} %all-to-all-done), kind=kOutput, calls=%fused_computation.5 | convolution fusion | flops 541065216 | bytes 3670016 | tf_op jit(solution)/shard_map/ecd,dh->ech/dot_general | solution.py:136
  56.1 0.1 fusion.30
  56.2 0.1 copy.38
  56.4 0.1 reshape.484
  56.4 1.5 %fusion.9 = bf16[4,256,512]{2,1,0:T(8,128)(2,1)} fusion(bf16[256,256,1]{1,0,2:T(8,128)(2,1)S(1)} %reshape.484, bf16[256,4,512]{2,1,0:T(4,128)(2,1)S(1)} %reshape_squeeze.3), kind=kOutput, calls=%fused_computation.15 | convolution fusion | flops 268959744 | bytes 2228224 | tf_op jit(solution)/shard_map/sh,hcd->csd/dot_general | solution.py:141
  58.0 4.4 %all-to-all-start.1 = ((bf16[4,256,512]{2,1,0:T(8,128)(2,1)}), bf16[4,256,512]{2,1,0:T(8,128)(2,1)S(1)}, u32[]{:S(2)}, u32[]{:S(2)}) async-start(bf16[4,256,512]{2,1,0:T(8,128)(2,1)} %fusion.9), calls=%async_computation.1 | async-start | bytes 2097152 | tf_op jit(solution)/shard_map/all_to_all | solution.py:143
  62.4 1.6 %fusion.56 = (f32[8,16]{1,0:T(8,128)S(1)}, f32[8,1,16,2048]{3,2,0,1:T(8,128)S(1)}) fusion(bf16[8,16,64]{2,1,0:T(8,128)(2,1)S(1)} %get-tuple-element.7, bf16[8,16,64]{2,1,0:T(8,128)(2,1)S(1)} %get-tuple-element.6, bf16[2048,64]{1,0:T(8,128)(2,1)} %get-tuple-element.5, bf16[2048,64]{1,0:T(8,128)(2,1)S(1)} %get-tuple-element.4, pred[8,2048]{1,0:T(8,128)(4,1)S(1)} %fusion.34), kind=kOutput, calls=%fused_computation.105 | convolution fusion | flops 69009280 | bytes 1622528 | tf_op jit(solution)/shard_map/rgqd,cgd->rgqc/dot_general | solution.py:54
  64.0 0.0 copy-start.7
  64.0 11.9 %all-to-all-done.1 = bf16[4,256,512]{2,1,0:T(8,128)(2,1)S(1)} async-done(((bf16[4,256,512]{2,1,0:T(8,128)(2,1)}), bf16[4,256,512]{2,1,0:T(8,128)(2,1)S(1)}, u32[]{:S(2)}, u32[]{:S(2)}) %all-to-all-start.1) | async-done | bytes 1048608 | tf_op jit(solution)/shard_map/all_to_all | solution.py:143
  76.0 0.2 reduce_sum.73
  76.2 0.8 reshape.469
  77.0 7.6 %all-to-all-start.2 = ((bf16[128,2,512]{2,1,0:T(2,128)(2,1)}), bf16[128,2,512]{2,1,0:T(2,128)(2,1)S(1)}, u32[]{:S(2)}, u32[]{:S(2)}) async-start(bf16[128,2,512]{2,1,0:T(2,128)(2,1)} %reshape.469), calls=%async_computation.2 | async-start | bytes 524288 | tf_op jit(solution)/shard_map/all_to_all | solution.py:146
  84.7 0.1 copy.36
  84.7 0.1 select_reduce_fusion.1
  84.9 0.3 fusion.20
  85.2 14.2 %all-to-all-done.2 = bf16[128,2,512]{2,1,0:T(2,128)(2,1)S(1)} async-done(((bf16[128,2,512]{2,1,0:T(2,128)(2,1)}), bf16[128,2,512]{2,1,0:T(2,128)(2,1)S(1)}, u32[]{:S(2)}, u32[]{:S(2)}) %all-to-all-start.2) | async-done | bytes 262176 | tf_op jit(solution)/shard_map/all_to_all | solution.py:146
  99.4 0.1 reshape.485
  99.5 0.9 convolution_convert_fusion.2
  100.4 3.3 %all-to-all-start.3 = ((bf16[4,16,512]{2,1,0:T(8,128)(2,1)}), bf16[4,16,512]{2,1,0:T(8,128)(2,1)S(1)}, u32[]{:S(2)}, u32[]{:S(2)}) async-start(bf16[4,16,512]{2,1,0:T(8,128)(2,1)} %convolution_convert_fusion.2), calls=%async_computation.3 | async-start | bytes 131072 | tf_op jit(solution)/shard_map/all_to_all | solution.py:161
  103.7 0.4 fusion.13
  104.1 0.6 copy.55
  104.7 4.6 %all-to-all-done.3 = bf16[4,16,512]{2,1,0:T(8,128)(2,1)S(1)} async-done(((bf16[4,16,512]{2,1,0:T(8,128)(2,1)}), bf16[4,16,512]{2,1,0:T(8,128)(2,1)S(1)}, u32[]{:S(2)}, u32[]{:S(2)}) %all-to-all-start.3) | async-done | bytes 65568 | tf_op jit(solution)/shard_map/all_to_all | solution.py:161
  109.3 0.6 copy.43
  (29 shorter events, 0.1 us)
Async XLA Ops:
  0.6 103.0 %copy-start = (bf16[2048,128]{1,0:T(8,128)(2,1)S(1)}, bf16[2048,128]{1,0:T(8,128)(2,1)}, u32[]{:S(2)}) copy-start(bf16[2048,128]{1,0:T(8,128)(2,1)} %param.22) | copy-start | bytes 1572868
  4.8 18.1 %copy-start.1 = (bf16[1,256,2048]{2,1,0:T(8,128)(2,1)S(1)}, bf16[1,256,2048]{2,1,0:T(8,128)(2,1)}, u32[]{:S(2)}) copy-start(bf16[1,256,2048]{2,1,0:T(8,128)(2,1)} %param.18) | copy-start | bytes 3145732
  4.8 49.0 %all-to-all-start = ((bf16[128,2,2048]{2,1,0:T(2,128)(2,1)}), bf16[128,2,2048]{2,1,0:T(2,128)(2,1)}, u32[]{:S(2)}, u32[]{:S(2)}) async-start(bf16[128,2,2048]{2,1,0:T(2,128)(2,1)} %reshape.467), calls=%async_computation | async-start | bytes 2097152 | tf_op jit(solution)/shard_map/all_to_all | solution.py:132
  22.9 0.9 copy-start.3
  22.9 0.9 copy-start.8
  22.9 1.1 copy-start.6
  22.9 1.9 %copy-start.2 = (bf16[2048,128]{1,0:T(8,128)(2,1)S(1)}, bf16[2048,128]{1,0:T(8,128)(2,1)}, u32[]{:S(2)}) copy-start(bf16[2048,128]{1,0:T(8,128)(2,1)} %param.20) | copy-start | bytes 1572868
  23.0 1.9 %copy-start.5 = (f32[1,2048]{1,0:T(1,128)S(1)}, f32[1,2048]{1,0:T(1,128)}, u32[]{:S(2)}) copy-start(f32[1,2048]{1,0:T(1,128)} %param.21) | copy-start | bytes 24580
  25.2 28.6 %copy-start.9 = (bf16[1,2048,256]{2,1,0:T(8,128)(2,1)S(1)}, bf16[1,2048,256]{2,1,0:T(8,128)(2,1)}, u32[]{:S(2)}) copy-start(bf16[1,2048,256]{2,1,0:T(8,128)(2,1)} %param.17) | copy-start | bytes 3145732
  58.0 4.4 %copy-start.4 = (s32[16,8]{0,1:T(8,128)S(1)}, s32[16,8]{0,1:T(8,128)}, u32[]{:S(2)}) copy-start(s32[16,8]{0,1:T(8,128)} %param.15) | copy-start | bytes 1540
  58.0 18.0 %all-to-all-start.1 = ((bf16[4,256,512]{2,1,0:T(8,128)(2,1)}), bf16[4,256,512]{2,1,0:T(8,128)(2,1)S(1)}, u32[]{:S(2)}, u32[]{:S(2)}) async-start(bf16[4,256,512]{2,1,0:T(8,128)(2,1)} %fusion.9), calls=%async_computation.1 | async-start | bytes 2097152 | tf_op jit(solution)/shard_map/all_to_all | solution.py:143
  64.0 20.7 %copy-start.7 = (bf16[8,128]{1,0:T(8,128)(2,1)S(1)}, bf16[8,128]{1,0:T(8,128)(2,1)}, u32[]{:S(2)}) copy-start(bf16[8,128]{1,0:T(8,128)(2,1)} %param.24) | copy-start | bytes 6148
  77.0 22.4 %all-to-all-start.2 = ((bf16[128,2,512]{2,1,0:T(2,128)(2,1)}), bf16[128,2,512]{2,1,0:T(2,128)(2,1)S(1)}, u32[]{:S(2)}, u32[]{:S(2)}) async-start(bf16[128,2,512]{2,1,0:T(2,128)(2,1)} %reshape.469), calls=%async_computation.2 | async-start | bytes 524288 | tf_op jit(solution)/shard_map/all_to_all | solution.py:146
  100.4 8.9 %all-to-all-start.3 = ((bf16[4,16,512]{2,1,0:T(8,128)(2,1)}), bf16[4,16,512]{2,1,0:T(8,128)(2,1)S(1)}, u32[]{:S(2)}, u32[]{:S(2)}) async-start(bf16[4,16,512]{2,1,0:T(8,128)(2,1)} %convolution_convert_fusion.2), calls=%async_computation.3 | async-start | bytes 131072 | tf_op jit(solution)/shard_map/all_to_all | solution.py:161

commit v12 on v9

--- a/solution.py
+++ b/solution.py
@@ -132,7 +132,7 @@
     arrived = lax.all_to_all(outgoing, "dp", split_axis=0, concat_axis=0, tiled=True)
     slots = dp_size * capacity
     hidden_width = w_gate.shape[2]
-    gate_up_w = jnp.concatenate([w_gate[0], w_up[0]], axis=1)
+    gate_up_w = lax.optimization_barrier(jnp.concatenate([w_gate[0], w_up[0]], axis=1))
     gate_up = jnp.einsum("ecd,dh->ech", arrived, gate_up_w, preferred_element_type=jnp.float32)
     gate_act = gate_up[..., :hidden_width]
     up_act = gate_up[..., hidden_width:]

time: 110 us -> 111 us (level)
  other arithmetic: 7.75 us -> 10.6 us
  waiting for transfers between devices: 53.9 us -> 51.1 us
    concatenate x0 -> x1, other arithmetic: none -> 2.83 us  [on_device(): jnp.concatenate([w_gate[0], w_up[0]], axis=1)]
    all_to_all x1, waiting for transfers between devices: 23.2 us -> 20.4 us  [on_device(): lax.all_to_all(outgoing, 'dp', split_axis=0, concat_axis=0, tiled=True)]
  transfers between devices with their start and end apart: 4 -> 4, of which waited for: 4 -> 4; matrix products, arithmetic and copies ran while one was open for 10% -> 12% of each run, Pallas kernels for 0% -> 0%
where the time goes in v12:
time: 111 us; the launch traced here: 110 us
  waiting for transfers between devices  51.1 us (46%)
  starting transfers between devices  33.2 us (30%)
  other arithmetic  10.6 us (10%)
  matrix products  7.84 us (7%)
  local copies, waits for them, and re-layouts  6.43 us (6%)
    all_to_all x1, waiting for transfers between devices, on_device(): lax.all_to_all(outgoing, 'dp', split_axis=0, concat_axis=0, tiled=True)  20.4 us
    all_to_all x1, starting transfers between devices, on_device(): lax.all_to_all(outgoing, 'dp', split_axis=0, concat_axis=0, tiled=True)  18 us
    all_to_all x1, waiting for transfers between devices, on_device(): lax.all_to_all(expert_out, 'dp', split_axis=0, concat_axis=0, tiled=True)  14.2 us
    all_to_all x1, waiting for transfers between devices, on_device(): lax.all_to_all(partial_value, 'tp', split_axis=0, concat_axis=0, tiled=True)  11.9 us
    all_to_all x1, starting transfers between devices, on_device(): lax.all_to_all(expert_out, 'dp', split_axis=0, concat_axis=0, tiled=True)  7.62 us
    concatenate x4, other arithmetic, rotate(): jnp.concatenate([front_half * cosine - back_half * sine_part, back_half *...  5.73 us
    all_to_all x1, waiting for transfers between devices, on_device(): lax.all_to_all(spread, 'tp', split_axis=1, concat_axis=1, tiled=True)  4.59 us
    all_to_all x1, starting transfers between devices, on_device(): lax.all_to_all(partial_value, 'tp', split_axis=0, concat_axis=0, tiled=True)  4.3 us
  transfers between devices with their start and end apart: 4, of which 4 were waited for; matrix products, arithmetic and copies ran while one was open for 12% of the time, Pallas kernels for 0%

profile of v12, /device:TPU:8, one launch (start us, length us, event | category | flops | bytes accessed | tf_op | source)
XLA Modules:
  0.0 110.1 jit_solution(5751429369752679320)
XLA Ops:
  0.6 0.0 copy-start
  0.6 0.8 copy.39
  1.5 0.1 eq.26
  1.5 0.2 convert_reduce_fusion
  1.7 0.1 fusion.30
  1.9 0.1 select_reduce_fusion
  2.0 1.3 %convolution_convert_fusion = bf16[256,2048]{1,0:T(8,128)(2,1)S(1)} fusion(bf16[16,2048]{1,0:T(8,128)(2,1)} %param.13, s32[256]{0:T(256)S(1)} %broadcast_select_fusion), kind=kOutput, calls=%fused_computation | convolution fusion | flops 17305600 | bytes 1115136 | tf_op jit(solution)/shard_map/dot_general | solution.py:130
  3.3 0.0 copy-start.4
  3.3 0.0 copy-start.7
  3.3 1.5 %reshape.467 = bf16[128,2,2048]{2,1,0:T(2,128)(2,1)} reshape(bf16[256,2048]{1,0:T(8,128)(2,1)S(1)} %convolution_convert_fusion) | data formatting | bytes 2097152 | tf_op jit(solution)/shard_map/reshape | solution.py:131
  4.9 18.0 %all-to-all-start = ((bf16[128,2,2048]{2,1,0:T(2,128)(2,1)}), bf16[128,2,2048]{2,1,0:T(2,128)(2,1)}, u32[]{:S(2)}, u32[]{:S(2)}) async-start(bf16[128,2,2048]{2,1,0:T(2,128)(2,1)} %reshape.467), calls=%async_computation | async-start | bytes 2097152 | tf_op jit(solution)/shard_map/all_to_all | solution.py:132
  22.9 0.1 reduce_sum.69
  22.9 0.2 reduce-window.8
  23.2 0.1 multiply_cosine_fusion.2
  23.3 0.1 fusion.48
  23.4 2.8 %pad_maximum_fusion = bf16[2048,512]{1,0:T(8,128)(2,1)} fusion(bf16[2048,256]{1,0:T(8,128)(2,1)S(1)} %bitcast.83, bf16[2048,256]{1,0:T(8,128)(2,1)} %bitcast.84), kind=kLoop, calls=%fused_computation.4 | loop fusion | flops 4194304 | bytes 4194304 | tf_op jit(solution)/shard_map/concatenate | solution.py:135
  26.3 0.8 reshape_squeeze.3
  27.1 0.1 select_reduce_fusion.2
  27.2 0.1 maximum_bitcast_fusion.2
  27.2 0.1 fusion.35
  27.3 0.2 fusion.41
  27.5 0.1 fusion.33
  27.7 0.3 multiply_bitcast_fusion
  28.0 5.5 %fusion.28 = (bf16[2048,64]{1,0:T(8,128)(2,1)S(1)}, bf16[2048,64]{1,0:T(8,128)(2,1)}) fusion(f32[2048,1,128]{2,0,1:T(8,128)S(1)} %multiply_bitcast_fusion, f32[64]{0:T(128)S(1)} %multiply_exponential_fusion, f32[2048]{0:T(1024)S(1)} %subtract_convert_fusion.1), kind=kLoop, calls=%fused_computation.38 | loop fusion | flops 1179648 | bytes 1581312 | tf_op jit(solution)/shard_map/concatenate | solution.py:20
  33.5 20.4 %all-to-all-done = bf16[128,2,2048]{2,1,0:T(2,128)(2,1)} async-done(((bf16[128,2,2048]{2,1,0:T(2,128)(2,1)}), bf16[128,2,2048]{2,1,0:T(2,128)(2,1)}, u32[]{:S(2)}, u32[]{:S(2)}) %all-to-all-start) | async-done | bytes 1048608 | tf_op jit(solution)/shard_map/all_to_all | solution.py:132
  53.9 2.6 %fusion.2 = f32[128,2,512]{2,0,1:T(8,128)S(1)} fusion(bf16[2048,512]{1,0:T(8,128)(2,1)} %pad_maximum_fusion, bf16[128,2,2048]{2,1,0:T(2,128)(2,1)} %all-to-all-done), kind=kOutput, calls=%fused_computation.5 | convolution fusion | flops 536870912 | bytes 3670016 | tf_op jit(solution)/shard_map/ecd,dh->ech/dot_general | solution.py:136
  56.5 0.1 fusion.29
  56.6 0.1 copy.43
  56.7 0.1 reshape.484
  56.8 1.5 %fusion.8 = bf16[4,256,512]{2,1,0:T(8,128)(2,1)} fusion(bf16[256,256,1]{1,0,2:T(8,128)(2,1)S(1)} %reshape.484, bf16[256,4,512]{2,1,0:T(4,128)(2,1)S(1)} %reshape_squeeze.3), kind=kOutput, calls=%fused_computation.14 | convolution fusion | flops 268959744 | bytes 2228224 | tf_op jit(solution)/shard_map/sh,hcd->csd/dot_general | solution.py:141
  58.4 4.3 %all-to-all-start.1 = ((bf16[4,256,512]{2,1,0:T(8,128)(2,1)}), bf16[4,256,512]{2,1,0:T(8,128)(2,1)S(1)}, u32[]{:S(2)}, u32[]{:S(2)}) async-start(bf16[4,256,512]{2,1,0:T(8,128)(2,1)} %fusion.8), calls=%async_computation.1 | async-start | bytes 2097152 | tf_op jit(solution)/shard_map/all_to_all | solution.py:143
  62.7 1.6 %fusion.53 = (f32[8,16]{1,0:T(8,128)S(1)}, f32[8,1,16,2048]{3,2,0,1:T(8,128)S(1)}) fusion(bf16[8,16,64]{2,1,0:T(8,128)(2,1)S(1)} %get-tuple-element.7, bf16[8,16,64]{2,1,0:T(8,128)(2,1)S(1)} %get-tuple-element.6, bf16[2048,64]{1,0:T(8,128)(2,1)} %get-tuple-element.5, bf16[2048,64]{1,0:T(8,128)(2,1)S(1)} %get-tuple-element.4, pred[8,2048]{1,0:T(8,128)(4,1)S(1)} %fusion.33), kind=kOutput, calls=%fused_computation.102 | convolution fusion | flops 69009280 | bytes 1622528 | tf_op jit(solution)/shard_map/rgqd,cgd->rgqc/dot_general | solution.py:54
  64.3 11.9 %all-to-all-done.1 = bf16[4,256,512]{2,1,0:T(8,128)(2,1)S(1)} async-done(((bf16[4,256,512]{2,1,0:T(8,128)(2,1)}), bf16[4,256,512]{2,1,0:T(8,128)(2,1)S(1)}, u32[]{:S(2)}, u32[]{:S(2)}) %all-to-all-start.1) | async-done | bytes 1048608 | tf_op jit(solution)/shard_map/all_to_all | solution.py:143
  76.2 0.2 reduce_sum.73
  76.5 0.8 reshape.469
  77.3 7.6 %all-to-all-start.2 = ((bf16[128,2,512]{2,1,0:T(2,128)(2,1)}), bf16[128,2,512]{2,1,0:T(2,128)(2,1)S(1)}, u32[]{:S(2)}, u32[]{:S(2)}) async-start(bf16[128,2,512]{2,1,0:T(2,128)(2,1)} %reshape.469), calls=%async_computation.2 | async-start | bytes 524288 | tf_op jit(solution)/shard_map/all_to_all | solution.py:146
  84.9 0.1 copy.41
  85.0 0.1 select_reduce_fusion.1
  85.1 0.3 fusion.19
  85.4 14.2 %all-to-all-done.2 = bf16[128,2,512]{2,1,0:T(2,128)(2,1)S(1)} async-done(((bf16[128,2,512]{2,1,0:T(2,128)(2,1)}), bf16[128,2,512]{2,1,0:T(2,128)(2,1)S(1)}, u32[]{:S(2)}, u32[]{:S(2)}) %all-to-all-start.2) | async-done | bytes 262176 | tf_op jit(solution)/shard_map/all_to_all | solution.py:146
  99.6 0.1 reshape.470
  99.7 0.2 convolution_convert_fusion.2
  99.9 0.7 broadcast_in_dim.53
  100.6 3.3 %all-to-all-start.3 = ((bf16[16,4,512]{2,0,1:T(8,128)(2,1)}), bf16[16,4,512]{2,0,1:T(8,128)(2,1)S(1)}, u32[]{:S(2)}, u32[]{:S(2)}) async-start(bf16[16,4,512]{2,0,1:T(8,128)(2,1)} %broadcast_in_dim.53), calls=%async_computation.3 | async-start | bytes 131072 | tf_op jit(solution)/shard_map/all_to_all | solution.py:160
  103.9 0.4 fusion.12
  104.3 0.6 copy.60
  104.9 4.6 %all-to-all-done.3 = bf16[16,4,512]{2,0,1:T(8,128)(2,1)S(1)} async-done(((bf16[16,4,512]{2,0,1:T(8,128)(2,1)}), bf16[16,4,512]{2,0,1:T(8,128)(2,1)S(1)}, u32[]{:S(2)}, u32[]{:S(2)}) %all-to-all-start.3) | async-done | bytes 65568 | tf_op jit(solution)/shard_map/all_to_all | solution.py:160
  109.5 0.6 copy.48
  (31 shorter events, 0.2 us)
Async XLA Ops:
  0.6 103.3 %copy-start = (bf16[2048,128]{1,0:T(8,128)(2,1)S(1)}, bf16[2048,128]{1,0:T(8,128)(2,1)}, u32[]{:S(2)}) copy-start(bf16[2048,128]{1,0:T(8,128)(2,1)} %param.22) | copy-start | bytes 1572868
  3.3 19.6 %copy-start.9 = (s32[8]{0:T(128)S(1)}, s32[8]{0:T(128)}, u32[]{:S(2)}) copy-start(s32[8]{0:T(128)} %param.25) | copy-start | bytes 100
  3.3 19.8 %copy-start.4 = (bf16[8,2048]{1,0:T(8,128)(2,1)S(1)}, bf16[8,2048]{1,0:T(8,128)(2,1)}, u32[]{:S(2)}) copy-start(bf16[8,2048]{1,0:T(8,128)(2,1)} %param.19) | copy-start | bytes 98308
  3.3 19.8 %copy-start.7 = (bf16[8,128]{1,0:T(8,128)(2,1)S(1)}, bf16[8,128]{1,0:T(8,128)(2,1)}, u32[]{:S(2)}) copy-start(bf16[8,128]{1,0:T(8,128)(2,1)} %param.23) | copy-start | bytes 6148
  4.9 18.6 %copy-start.2 = (bf16[1,2048,256]{2,1,0:T(8,128)(2,1)S(1)}, bf16[1,2048,256]{2,1,0:T(8,128)(2,1)}, u32[]{:S(2)}) copy-start(bf16[1,2048,256]{2,1,0:T(8,128)(2,1)} %param.17) | copy-start | bytes 3145732
  4.9 49.0 %all-to-all-start = ((bf16[128,2,2048]{2,1,0:T(2,128)(2,1)}), bf16[128,2,2048]{2,1,0:T(2,128)(2,1)}, u32[]{:S(2)}, u32[]{:S(2)}) async-start(bf16[128,2,2048]{2,1,0:T(2,128)(2,1)} %reshape.467), calls=%async_computation | async-start | bytes 2097152 | tf_op jit(solution)/shard_map/all_to_all | solution.py:132
  23.4 2.8 %copy-start.1 = (bf16[1,256,2048]{2,1,0:T(8,128)(2,1)S(1)}, bf16[1,256,2048]{2,1,0:T(8,128)(2,1)}, u32[]{:S(2)}) copy-start(bf16[1,256,2048]{2,1,0:T(8,128)(2,1)} %param.18) | copy-start | bytes 3145732
  26.3 1.4 %copy-start.3 = (bf16[2048,128]{1,0:T(8,128)(2,1)S(1)}, bf16[2048,128]{1,0:T(8,128)(2,1)}, u32[]{:S(2)}) copy-start(bf16[2048,128]{1,0:T(8,128)(2,1)} %param.20) | copy-start | bytes 1572868
  26.3 1.4 %copy-start.6 = (f32[1,2048]{1,0:T(1,128)S(1)}, f32[1,2048]{1,0:T(1,128)}, u32[]{:S(2)}) copy-start(f32[1,2048]{1,0:T(1,128)} %param.21) | copy-start | bytes 24580
  56.8 5.8 %copy-start.5 = (s32[16,8]{0,1:T(8,128)S(1)}, s32[16,8]{0,1:T(8,128)}, u32[]{:S(2)}) copy-start(s32[16,8]{0,1:T(8,128)} %param.15) | copy-start | bytes 1540
  58.4 17.9 %all-to-all-start.1 = ((bf16[4,256,512]{2,1,0:T(8,128)(2,1)}), bf16[4,256,512]{2,1,0:T(8,128)(2,1)S(1)}, u32[]{:S(2)}, u32[]{:S(2)}) async-start(bf16[4,256,512]{2,1,0:T(8,128)(2,1)} %fusion.8), calls=%async_computation.1 | async-start | bytes 2097152 | tf_op jit(solution)/shard_map/all_to_all | solution.py:143
  62.7 22.2 %copy-start.8 = (bf16[8,128]{1,0:T(8,128)(2,1)S(1)}, bf16[8,128]{1,0:T(8,128)(2,1)}, u32[]{:S(2)}) copy-start(bf16[8,128]{1,0:T(8,128)(2,1)} %param.24) | copy-start | bytes 6148
  77.3 22.4 %all-to-all-start.2 = ((bf16[128,2,512]{2,1,0:T(2,128)(2,1)}), bf16[128,2,512]{2,1,0:T(2,128)(2,1)S(1)}, u32[]{:S(2)}, u32[]{:S(2)}) async-start(bf16[128,2,512]{2,1,0:T(2,128)(2,1)} %reshape.469), calls=%async_computation.2 | async-start | bytes 524288 | tf_op jit(solution)/shard_map/all_to_all | solution.py:146
  100.6 8.9 %all-to-all-start.3 = ((bf16[16,4,512]{2,0,1:T(8,128)(2,1)}), bf16[16,4,512]{2,0,1:T(8,128)(2,1)S(1)}, u32[]{:S(2)}, u32[]{:S(2)}) async-start(bf16[16,4,512]{2,0,1:T(8,128)(2,1)} %broadcast_in_dim.53), calls=%async_computation.3 | async-start | bytes 131072 | tf_op jit(solution)/shard_map/all_to_all | solution.py:160

commit v13 on v9

--- a/solution.py
+++ b/solution.py
@@ -127,7 +127,7 @@
     slot_token = jnp.sum(jnp.where(slot_hit, token_of_pair[None, :], 0), axis=1)
     slot_token = jnp.where(jnp.any(slot_hit, axis=1), slot_token, token_count)
     selector = (slot_token[:, None] == token_pos[None, :]).astype(hidden.dtype)
-    outgoing = jnp.dot(selector, hidden, preferred_element_type=jnp.float32).astype(hidden.dtype)
+    outgoing = jnp.dot(selector, hidden, preferred_element_type=hidden.dtype)
     outgoing = outgoing.reshape(experts, capacity, model_width)
     arrived = lax.all_to_all(outgoing, "dp", split_axis=0, concat_axis=0, tiled=True)
     slots = dp_size * capacity

time: 110 us -> 110 us (level)
  no operation moved by 1% of the time
where the time goes in v13:
time: 110 us
  waiting for transfers between devices  53.9 us (49%)
  starting transfers between devices  33.3 us (30%)
  other arithmetic  7.75 us (7%)
  matrix products  7.5 us (7%)
  local copies, waits for them, and re-layouts  6.45 us (6%)
    all_to_all x1, waiting for transfers between devices, on_device(): lax.all_to_all(outgoing, 'dp', split_axis=0, concat_axis=0, tiled=True)  23.2 us
    all_to_all x1, starting transfers between devices, on_device(): lax.all_to_all(outgoing, 'dp', split_axis=0, concat_axis=0, tiled=True)  18 us
    all_to_all x1, waiting for transfers between devices, on_device(): lax.all_to_all(expert_out, 'dp', split_axis=0, concat_axis=0, tiled=True)  14.2 us
    all_to_all x1, waiting for transfers between devices, on_device(): lax.all_to_all(partial_value, 'tp', split_axis=0, concat_axis=0, tiled=True)  11.9 us
    all_to_all x1, starting transfers between devices, on_device(): lax.all_to_all(expert_out, 'dp', split_axis=0, concat_axis=0, tiled=True)  7.62 us
    concatenate x4, other arithmetic, rotate(): jnp.concatenate([front_half * cosine - back_half * sine_part, back_half *...  5.72 us
    all_to_all x1, waiting for transfers between devices, on_device(): lax.all_to_all(spread, 'tp', split_axis=1, concat_axis=1, tiled=True)  4.58 us
    all_to_all x1, starting transfers between devices, on_device(): lax.all_to_all(partial_value, 'tp', split_axis=0, concat_axis=0, tiled=True)  4.42 us
  transfers between devices with their start and end apart: 4, of which 4 were waited for; matrix products, arithmetic and copies ran while one was open for 10% of the time, Pallas kernels for 0%

profile of v13, /device:TPU:8, one launch (start us, length us, event | category | flops | bytes accessed | tf_op | source)
XLA Modules:
  0.0 109.9 jit_solution(3870151631322848324)
XLA Ops:
  0.6 0.0 copy-start
  0.6 0.8 copy.39
  1.5 0.1 eq.26
  1.5 0.2 convert_reduce_fusion
  1.7 0.1 fusion.31
  1.9 0.1 select_reduce_fusion
  2.0 1.3 %fusion.32 = bf16[256,2048]{1,0:T(8,128)(2,1)S(1)} fusion(bf16[16,2048]{1,0:T(8,128)(2,1)} %param.13, s32[256]{0:T(256)S(1)} %broadcast_select_fusion), kind=kOutput, calls=%fused_computation.47 | convolution fusion | flops 16781312 | bytes 1115136 | tf_op jit(solution)/shard_map/dot_general | solution.py:130
  3.3 1.5 %reshape.467 = bf16[128,2,2048]{2,1,0:T(2,128)(2,1)} reshape(bf16[256,2048]{1,0:T(8,128)(2,1)S(1)} %fusion.32) | data formatting | bytes 2097152 | tf_op jit(solution)/shard_map/reshape | solution.py:131
  4.8 18.0 %all-to-all-start = ((bf16[128,2,2048]{2,1,0:T(2,128)(2,1)}), bf16[128,2,2048]{2,1,0:T(2,128)(2,1)}, u32[]{:S(2)}, u32[]{:S(2)}) async-start(bf16[128,2,2048]{2,1,0:T(2,128)(2,1)} %reshape.467), calls=%async_computation | async-start | bytes 2097152 | tf_op jit(solution)/shard_map/all_to_all | solution.py:132
  22.8 0.1 reduce_sum.69
  22.9 0.0 copy-start.3
  22.9 0.0 copy-start.2
  23.0 0.0 copy-start.5
  23.0 0.8 reshape_squeeze.3
  23.8 0.2 reduce-window.8
  24.0 0.1 multiply_cosine_fusion.2
  24.1 0.1 fusion.50
  24.3 0.1 select_reduce_fusion.2
  24.4 0.1 maximum_bitcast_fusion.4
  24.4 0.1 fusion.37
  24.5 0.2 fusion.43
  24.7 0.1 fusion.35
  24.9 0.3 multiply_bitcast_fusion
  25.2 5.4 %fusion.29 = (bf16[2048,64]{1,0:T(8,128)(2,1)S(1)}, bf16[2048,64]{1,0:T(8,128)(2,1)}) fusion(f32[2048,1,128]{2,0,1:T(8,128)S(1)} %multiply_bitcast_fusion, f32[64]{0:T(128)S(1)} %multiply_exponential_fusion, f32[2048]{0:T(1024)S(1)} %subtract_convert_fusion.1), kind=kLoop, calls=%fused_computation.38 | loop fusion | flops 1179648 | bytes 1581312 | tf_op jit(solution)/shard_map/concatenate | solution.py:20
  30.6 23.2 %all-to-all-done = bf16[128,2,2048]{2,1,0:T(2,128)(2,1)} async-done(((bf16[128,2,2048]{2,1,0:T(2,128)(2,1)}), bf16[128,2,2048]{2,1,0:T(2,128)(2,1)}, u32[]{:S(2)}, u32[]{:S(2)}) %all-to-all-start) | async-done | bytes 1048608 | tf_op jit(solution)/shard_map/all_to_all | solution.py:132
  53.8 2.3 %fusion.2 = f32[128,2,512]{2,0,1:T(8,128)S(1)} fusion(bf16[2048,256]{1,0:T(8,128)(2,1)S(1)} %bitcast.93, bf16[2048,256]{1,0:T(8,128)(2,1)} %bitcast.94, bf16[128,2,2048]{2,1,0:T(2,128)(2,1)} %all-to-all-done), kind=kOutput, calls=%fused_computation.4 | convolution fusion | flops 541065216 | bytes 3670016 | tf_op jit(solution)/shard_map/ecd,dh->ech/dot_general | solution.py:136
  56.1 0.1 fusion.30
  56.2 0.1 copy.43
  56.4 0.1 reshape.484
  56.4 1.5 %fusion.9 = bf16[4,256,512]{2,1,0:T(8,128)(2,1)} fusion(bf16[256,256,1]{1,0,2:T(8,128)(2,1)S(1)} %reshape.484, bf16[256,4,512]{2,1,0:T(4,128)(2,1)S(1)} %reshape_squeeze.3), kind=kOutput, calls=%fused_computation.14 | convolution fusion | flops 268959744 | bytes 2228224 | tf_op jit(solution)/shard_map/sh,hcd->csd/dot_general | solution.py:141
  58.0 4.4 %all-to-all-start.1 = ((bf16[4,256,512]{2,1,0:T(8,128)(2,1)}), bf16[4,256,512]{2,1,0:T(8,128)(2,1)S(1)}, u32[]{:S(2)}, u32[]{:S(2)}) async-start(bf16[4,256,512]{2,1,0:T(8,128)(2,1)} %fusion.9), calls=%async_computation.1 | async-start | bytes 2097152 | tf_op jit(solution)/shard_map/all_to_all | solution.py:143
  62.4 1.6 %fusion.56 = (f32[8,16]{1,0:T(8,128)S(1)}, f32[8,1,16,2048]{3,2,0,1:T(8,128)S(1)}) fusion(bf16[8,16,64]{2,1,0:T(8,128)(2,1)S(1)} %get-tuple-element.7, bf16[8,16,64]{2,1,0:T(8,128)(2,1)S(1)} %get-tuple-element.6, bf16[2048,64]{1,0:T(8,128)(2,1)} %get-tuple-element.5, bf16[2048,64]{1,0:T(8,128)(2,1)S(1)} %get-tuple-element.4, pred[8,2048]{1,0:T(8,128)(4,1)S(1)} %fusion.35), kind=kOutput, calls=%fused_computation.104 | convolution fusion | flops 69009280 | bytes 1622528 | tf_op jit(solution)/shard_map/rgqd,cgd->rgqc/dot_general | solution.py:54
  64.0 11.9 %all-to-all-done.1 = bf16[4,256,512]{2,1,0:T(8,128)(2,1)S(1)} async-done(((bf16[4,256,512]{2,1,0:T(8,128)(2,1)}), bf16[4,256,512]{2,1,0:T(8,128)(2,1)S(1)}, u32[]{:S(2)}, u32[]{:S(2)}) %all-to-all-start.1) | async-done | bytes 1048608 | tf_op jit(solution)/shard_map/all_to_all | solution.py:143
  76.0 0.2 reduce_sum.73
  76.2 0.8 reshape.469
  77.0 7.6 %all-to-all-start.2 = ((bf16[128,2,512]{2,1,0:T(2,128)(2,1)}), bf16[128,2,512]{2,1,0:T(2,128)(2,1)S(1)}, u32[]{:S(2)}, u32[]{:S(2)}) async-start(bf16[128,2,512]{2,1,0:T(2,128)(2,1)} %reshape.469), calls=%async_computation.2 | async-start | bytes 524288 | tf_op jit(solution)/shard_map/all_to_all | solution.py:146
  84.7 0.1 copy.41
  84.7 0.1 select_reduce_fusion.1
  84.9 0.3 fusion.20
  85.2 14.2 %all-to-all-done.2 = bf16[128,2,512]{2,1,0:T(2,128)(2,1)S(1)} async-done(((bf16[128,2,512]{2,1,0:T(2,128)(2,1)}), bf16[128,2,512]{2,1,0:T(2,128)(2,1)S(1)}, u32[]{:S(2)}, u32[]{:S(2)}) %all-to-all-start.2) | async-done | bytes 262176 | tf_op jit(solution)/shard_map/all_to_all | solution.py:146
  99.4 0.1 reshape.470
  99.5 0.2 convolution_convert_fusion.1
  99.7 0.7 broadcast_in_dim.53
  100.3 3.3 %all-to-all-start.3 = ((bf16[16,4,512]{2,0,1:T(8,128)(2,1)}), bf16[16,4,512]{2,0,1:T(8,128)(2,1)S(1)}, u32[]{:S(2)}, u32[]{:S(2)}) async-start(bf16[16,4,512]{2,0,1:T(8,128)(2,1)} %broadcast_in_dim.53), calls=%async_computation.3 | async-start | bytes 131072 | tf_op jit(solution)/shard_map/all_to_all | solution.py:160
  103.6 0.4 fusion.13
  104.0 0.6 copy.60
  104.6 4.6 %all-to-all-done.3 = bf16[16,4,512]{2,0,1:T(8,128)(2,1)S(1)} async-done(((bf16[16,4,512]{2,0,1:T(8,128)(2,1)}), bf16[16,4,512]{2,0,1:T(8,128)(2,1)S(1)}, u32[]{:S(2)}, u32[]{:S(2)}) %all-to-all-start.3) | async-done | bytes 65568 | tf_op jit(solution)/shard_map/all_to_all | solution.py:160
  109.2 0.6 copy.48
  (30 shorter events, 0.2 us)
Async XLA Ops:
  0.6 103.0 %copy-start = (bf16[2048,128]{1,0:T(8,128)(2,1)S(1)}, bf16[2048,128]{1,0:T(8,128)(2,1)}, u32[]{:S(2)}) copy-start(bf16[2048,128]{1,0:T(8,128)(2,1)} %param.22) | copy-start | bytes 1572868
  4.8 18.1 %copy-start.1 = (bf16[1,256,2048]{2,1,0:T(8,128)(2,1)S(1)}, bf16[1,256,2048]{2,1,0:T(8,128)(2,1)}, u32[]{:S(2)}) copy-start(bf16[1,256,2048]{2,1,0:T(8,128)(2,1)} %param.18) | copy-start | bytes 3145732
  4.8 49.0 %all-to-all-start = ((bf16[128,2,2048]{2,1,0:T(2,128)(2,1)}), bf16[128,2,2048]{2,1,0:T(2,128)(2,1)}, u32[]{:S(2)}, u32[]{:S(2)}) async-start(bf16[128,2,2048]{2,1,0:T(2,128)(2,1)} %reshape.467), calls=%async_computation | async-start | bytes 2097152 | tf_op jit(solution)/shard_map/all_to_all | solution.py:132
  22.9 0.9 copy-start.3
  22.9 0.9 copy-start.8
  22.9 1.1 copy-start.6
  22.9 1.9 %copy-start.2 = (bf16[2048,128]{1,0:T(8,128)(2,1)S(1)}, bf16[2048,128]{1,0:T(8,128)(2,1)}, u32[]{:S(2)}) copy-start(bf16[2048,128]{1,0:T(8,128)(2,1)} %param.20) | copy-start | bytes 1572868
  23.0 1.9 %copy-start.5 = (f32[1,2048]{1,0:T(1,128)S(1)}, f32[1,2048]{1,0:T(1,128)}, u32[]{:S(2)}) copy-start(f32[1,2048]{1,0:T(1,128)} %param.21) | copy-start | bytes 24580
  25.2 28.6 %copy-start.9 = (bf16[1,2048,256]{2,1,0:T(8,128)(2,1)S(1)}, bf16[1,2048,256]{2,1,0:T(8,128)(2,1)}, u32[]{:S(2)}) copy-start(bf16[1,2048,256]{2,1,0:T(8,128)(2,1)} %param.17) | copy-start | bytes 3145732
  58.0 4.4 %copy-start.4 = (s32[16,8]{0,1:T(8,128)S(1)}, s32[16,8]{0,1:T(8,128)}, u32[]{:S(2)}) copy-start(s32[16,8]{0,1:T(8,128)} %param.15) | copy-start | bytes 1540
  58.0 18.0 %all-to-all-start.1 = ((bf16[4,256,512]{2,1,0:T(8,128)(2,1)}), bf16[4,256,512]{2,1,0:T(8,128)(2,1)S(1)}, u32[]{:S(2)}, u32[]{:S(2)}) async-start(bf16[4,256,512]{2,1,0:T(8,128)(2,1)} %fusion.9), calls=%async_computation.1 | async-start | bytes 2097152 | tf_op jit(solution)/shard_map/all_to_all | solution.py:143
  64.0 20.7 %copy-start.7 = (bf16[8,128]{1,0:T(8,128)(2,1)S(1)}, bf16[8,128]{1,0:T(8,128)(2,1)}, u32[]{:S(2)}) copy-start(bf16[8,128]{1,0:T(8,128)(2,1)} %param.24) | copy-start | bytes 6148
  77.0 22.4 %all-to-all-start.2 = ((bf16[128,2,512]{2,1,0:T(2,128)(2,1)}), bf16[128,2,512]{2,1,0:T(2,128)(2,1)S(1)}, u32[]{:S(2)}, u32[]{:S(2)}) async-start(bf16[128,2,512]{2,1,0:T(2,128)(2,1)} %reshape.469), calls=%async_computation.2 | async-start | bytes 524288 | tf_op jit(solution)/shard_map/all_to_all | solution.py:146
  100.3 8.9 %all-to-all-start.3 = ((bf16[16,4,512]{2,0,1:T(8,128)(2,1)}), bf16[16,4,512]{2,0,1:T(8,128)(2,1)S(1)}, u32[]{:S(2)}, u32[]{:S(2)}) async-start(bf16[16,4,512]{2,0,1:T(8,128)(2,1)} %broadcast_in_dim.53), calls=%async_computation.3 | async-start | bytes 131072 | tf_op jit(solution)/shard_map/all_to_all | solution.py:160

commit v14 on v10

--- a/solution.py
+++ b/solution.py
@@ -148,15 +148,16 @@
     slot_weight = jnp.sum(
         jnp.where(slot_grid[:, :, None] == slot_pos[None, None, :], shares[:, :, None], 0.0), axis=1
     )
-    mix_cols = jnp.dot(
+    slot_weight = jnp.broadcast_to(slot_weight[None], (tp_size,) + slot_weight.shape)
+    spread = jnp.einsum(
+        "cts,sd->ctd",
         slot_weight,
         returned.reshape(experts * capacity, slice_width).astype(jnp.float32),
         precision=lax.Precision.HIGHEST,
         preferred_element_type=jnp.float32,
     ).astype(jnp.bfloat16)
-    spread = jnp.broadcast_to(mix_cols[:, None, :], (token_count, tp_size, slice_width))
-    expert_mix = lax.all_to_all(spread, "tp", split_axis=1, concat_axis=1, tiled=True)
-    expert_mix = expert_mix.reshape(token_count, model_width)
+    expert_mix = lax.all_to_all(spread, "tp", split_axis=0, concat_axis=0, tiled=True)
+    expert_mix = jnp.transpose(expert_mix, (1, 0, 2)).reshape(token_count, model_width)
     attended = attend_local(
         queries, key_codes, key_scales, cache_values, new_keys, new_values, lengths
     )

time: 110 us -> 110 us (level)
  no operation moved by 1% of the time
where the time goes in v14:
time: 110 us
  waiting for transfers between devices  52.5 us (48%)
  starting transfers between devices  33.3 us (30%)
  matrix products  8.18 us (7%)
  other arithmetic  7.48 us (7%)
  local copies, waits for them, and re-layouts  7.35 us (7%)
    all_to_all x1, waiting for transfers between devices, on_device(): lax.all_to_all(outgoing, 'dp', split_axis=0, concat_axis=0, tiled=True)  21.8 us
    all_to_all x1, starting transfers between devices, on_device(): lax.all_to_all(outgoing, 'dp', split_axis=0, concat_axis=0, tiled=True)  18 us
    all_to_all x1, waiting for transfers between devices, on_device(): lax.all_to_all(expert_out, 'dp', split_axis=0, concat_axis=0, tiled=True)  14.2 us
    all_to_all x1, waiting for transfers between devices, on_device(): lax.all_to_all(partial_value, 'tp', split_axis=0, concat_axis=0, tiled=True)  11.9 us
    all_to_all x1, starting transfers between devices, on_device(): lax.all_to_all(expert_out, 'dp', split_axis=0, concat_axis=0, tiled=True)  7.62 us
    concatenate x4, other arithmetic, rotate(): jnp.concatenate([front_half * cosine - back_half * sine_part, back_half *...  5.72 us
    all_to_all x1, waiting for transfers between devices, on_device(): lax.all_to_all(spread, 'tp', split_axis=0, concat_axis=0, tiled=True)  4.59 us
    all_to_all x1, starting transfers between devices, on_device(): lax.all_to_all(partial_value, 'tp', split_axis=0, concat_axis=0, tiled=True)  4.43 us
  transfers between devices with their start and end apart: 4, of which 4 were waited for; matrix products, arithmetic and copies ran while one was open for 11% of the time, Pallas kernels for 0%

profile of v14, /device:TPU:8, one launch (start us, length us, event | category | flops | bytes accessed | tf_op | source)
XLA Modules:
  0.0 109.8 jit_solution(16217854604739847754)
XLA Ops:
  0.6 0.0 copy-start
  0.6 0.8 copy.39
  1.5 0.1 fusion.32
  1.6 0.1 copy.43
  1.7 0.1 eq.47
  1.9 1.3 %convolution_convert_fusion = bf16[256,2048]{1,0:T(8,128)(2,1)S(1)} fusion(bf16[16,2048]{1,0:T(8,128)(2,1)} %param.13, s32[256]{0:T(256)S(1)} %eq.47), kind=kOutput, calls=%fused_computation.1 | convolution fusion | flops 17305600 | bytes 1115136 | tf_op jit(solution)/shard_map/dot_general | solution.py:128
  3.2 1.5 %reshape.449 = bf16[128,2,2048]{2,1,0:T(2,128)(2,1)} reshape(bf16[256,2048]{1,0:T(8,128)(2,1)S(1)} %convolution_convert_fusion) | data formatting | bytes 2097152 | tf_op jit(solution)/shard_map/reshape | solution.py:129
  4.7 18.0 %all-to-all-start = ((bf16[128,2,2048]{2,1,0:T(2,128)(2,1)}), bf16[128,2,2048]{2,1,0:T(2,128)(2,1)}, u32[]{:S(2)}, u32[]{:S(2)}) async-start(bf16[128,2,2048]{2,1,0:T(2,128)(2,1)} %reshape.449), calls=%async_computation | async-start | bytes 2097152 | tf_op jit(solution)/shard_map/all_to_all | solution.py:130
  22.7 0.8 reshape_squeeze.3
  23.5 0.1 copy.41
  23.6 0.1 reshape.467
  23.7 0.0 copy-start.7
  23.7 0.0 copy-start.2
  23.8 1.2 %gather_fusion = s32[128]{0:T(128)S(1)} fusion(s32[128]{0:T(128)S(1)} %get-tuple-element.2, s32[1024]{0:T(1024)S(1)} %pad_clamp_fusion), kind=kCustom, calls=%fused_computation | custom fusion | bytes 1536 | tf_op jit(solution)/shard_map/gather | solution.py:124
  25.0 0.1 reshape.466
  25.1 0.2 reduce-window.8
  25.3 0.1 multiply_cosine_fusion.2
  25.4 0.1 fusion.49
  25.6 0.1 select_reduce_fusion.1
  25.7 0.1 maximum_bitcast_fusion.4
  25.7 0.1 fusion.35
  25.8 0.2 fusion.42
  26.0 0.1 fusion.33
  26.2 0.3 multiply_bitcast_fusion
  26.5 5.4 %fusion.29 = (bf16[2048,64]{1,0:T(8,128)(2,1)S(1)}, bf16[2048,64]{1,0:T(8,128)(2,1)}) fusion(f32[2048,1,128]{2,0,1:T(8,128)S(1)} %multiply_bitcast_fusion, f32[64]{0:T(128)S(1)} %multiply_exponential_fusion, f32[2048]{0:T(1024)S(1)} %subtract_convert_fusion.1), kind=kLoop, calls=%fused_computation.40 | loop fusion | flops 1179648 | bytes 1581312 | tf_op jit(solution)/shard_map/concatenate | solution.py:20
  32.0 21.8 %all-to-all-done = bf16[128,2,2048]{2,1,0:T(2,128)(2,1)} async-done(((bf16[128,2,2048]{2,1,0:T(2,128)(2,1)}), bf16[128,2,2048]{2,1,0:T(2,128)(2,1)}, u32[]{:S(2)}, u32[]{:S(2)}) %all-to-all-start) | async-done | bytes 1048608 | tf_op jit(solution)/shard_map/all_to_all | solution.py:130
  53.7 2.3 %fusion.2 = f32[128,2,512]{2,0,1:T(8,128)S(1)} fusion(bf16[2048,256]{1,0:T(8,128)(2,1)S(1)} %bitcast.98, bf16[2048,256]{1,0:T(8,128)(2,1)} %bitcast.99, bf16[128,2,2048]{2,1,0:T(2,128)(2,1)} %all-to-all-done), kind=kOutput, calls=%fused_computation.6 | convolution fusion | flops 541065216 | bytes 3670016 | tf_op jit(solution)/shard_map/ecd,dh->ech/dot_general | solution.py:134
  56.0 0.1 fusion.30
  56.1 0.1 copy.45
  56.2 0.1 reshape.476
  56.3 1.5 %fusion.9 = bf16[4,256,512]{2,1,0:T(8,128)(2,1)} fusion(bf16[256,256,1]{1,0,2:T(8,128)(2,1)S(1)} %reshape.476, bf16[256,4,512]{2,1,0:T(4,128)(2,1)S(1)} %reshape_squeeze.3), kind=kOutput, calls=%fused_computation.16 | convolution fusion | flops 268959744 | bytes 2228224 | tf_op jit(solution)/shard_map/sh,hcd->csd/dot_general | solution.py:139
  57.9 4.4 %all-to-all-start.1 = ((bf16[4,256,512]{2,1,0:T(8,128)(2,1)}), bf16[4,256,512]{2,1,0:T(8,128)(2,1)S(1)}, u32[]{:S(2)}, u32[]{:S(2)}) async-start(bf16[4,256,512]{2,1,0:T(8,128)(2,1)} %fusion.9), calls=%async_computation.1 | async-start | bytes 2097152 | tf_op jit(solution)/shard_map/all_to_all | solution.py:141
  62.3 1.6 %fusion.55 = (f32[8,16]{1,0:T(8,128)S(1)}, f32[8,1,16,2048]{3,2,0,1:T(8,128)S(1)}) fusion(bf16[8,16,64]{2,1,0:T(8,128)(2,1)S(1)} %get-tuple-element.9, bf16[8,16,64]{2,1,0:T(8,128)(2,1)S(1)} %get-tuple-element.8, bf16[2048,64]{1,0:T(8,128)(2,1)} %get-tuple-element.7, bf16[2048,64]{1,0:T(8,128)(2,1)S(1)} %get-tuple-element.6, pred[8,2048]{1,0:T(8,128)(4,1)S(1)} %fusion.33), kind=kOutput, calls=%fused_computation.103 | convolution fusion | flops 69009280 | bytes 1622528 | tf_op jit(solution)/shard_map/rgqd,cgd->rgqc/dot_general | solution.py:54
  63.9 11.9 %all-to-all-done.1 = bf16[4,256,512]{2,1,0:T(8,128)(2,1)S(1)} async-done(((bf16[4,256,512]{2,1,0:T(8,128)(2,1)}), bf16[4,256,512]{2,1,0:T(8,128)(2,1)S(1)}, u32[]{:S(2)}, u32[]{:S(2)}) %all-to-all-start.1) | async-done | bytes 1048608 | tf_op jit(solution)/shard_map/all_to_all | solution.py:141
  75.9 0.2 reduce_sum.50
  76.1 0.8 reshape.451
  76.9 7.6 %all-to-all-start.2 = ((bf16[128,2,512]{2,1,0:T(2,128)(2,1)}), bf16[128,2,512]{2,1,0:T(2,128)(2,1)S(1)}, u32[]{:S(2)}, u32[]{:S(2)}) async-start(bf16[128,2,512]{2,1,0:T(2,128)(2,1)} %reshape.451), calls=%async_computation.2 | async-start | bytes 524288 | tf_op jit(solution)/shard_map/all_to_all | solution.py:144
  84.5 0.1 copy.42
  84.6 0.1 select_reduce_fusion
  84.7 0.3 fusion.20
  85.0 14.2 %all-to-all-done.2 = bf16[128,2,512]{2,1,0:T(2,128)(2,1)S(1)} async-done(((bf16[128,2,512]{2,1,0:T(2,128)(2,1)}), bf16[128,2,512]{2,1,0:T(2,128)(2,1)S(1)}, u32[]{:S(2)}, u32[]{:S(2)}) %all-to-all-start.2) | async-done | bytes 262176 | tf_op jit(solution)/shard_map/all_to_all | solution.py:144
  99.3 0.1 reshape.477
  99.4 0.9 convolution_convert_fusion.2
  100.3 3.3 %all-to-all-start.3 = ((bf16[4,16,512]{2,1,0:T(8,128)(2,1)}), bf16[4,16,512]{2,1,0:T(8,128)(2,1)S(1)}, u32[]{:S(2)}, u32[]{:S(2)}) async-start(bf16[4,16,512]{2,1,0:T(8,128)(2,1)} %convolution_convert_fusion.2), calls=%async_computation.3 | async-start | bytes 131072 | tf_op jit(solution)/shard_map/all_to_all | solution.py:159
  103.6 0.4 fusion.13
  103.9 0.6 copy.62
  104.6 4.6 %all-to-all-done.3 = bf16[4,16,512]{2,1,0:T(8,128)(2,1)S(1)} async-done(((bf16[4,16,512]{2,1,0:T(8,128)(2,1)}), bf16[4,16,512]{2,1,0:T(8,128)(2,1)S(1)}, u32[]{:S(2)}, u32[]{:S(2)}) %all-to-all-start.3) | async-done | bytes 65568 | tf_op jit(solution)/shard_map/all_to_all | solution.py:159
  109.1 0.6 copy.50
  (36 shorter events, 0.2 us)
Async XLA Ops:
  0.6 102.9 %copy-start = (bf16[2048,128]{1,0:T(8,128)(2,1)S(1)}, bf16[2048,128]{1,0:T(8,128)(2,1)}, u32[]{:S(2)}) copy-start(bf16[2048,128]{1,0:T(8,128)(2,1)} %param.22) | copy-start | bytes 1572868
  4.7 18.0 %copy-start.4 = (s32[16,8]{0,1:T(8,128)S(1)}, s32[16,8]{0,1:T(8,128)}, u32[]{:S(2)}) copy-start(s32[16,8]{0,1:T(8,128)} %param.14) | copy-start | bytes 1540
  4.7 18.0 %copy-start.1 = (bf16[1,256,2048]{2,1,0:T(8,128)(2,1)S(1)}, bf16[1,256,2048]{2,1,0:T(8,128)(2,1)}, u32[]{:S(2)}) copy-start(bf16[1,256,2048]{2,1,0:T(8,128)(2,1)} %param.18) | copy-start | bytes 3145732
  4.7 49.0 %all-to-all-start = ((bf16[128,2,2048]{2,1,0:T(2,128)(2,1)}), bf16[128,2,2048]{2,1,0:T(2,128)(2,1)}, u32[]{:S(2)}, u32[]{:S(2)}) async-start(bf16[128,2,2048]{2,1,0:T(2,128)(2,1)} %reshape.449), calls=%async_computation | async-start | bytes 2097152 | tf_op jit(solution)/shard_map/all_to_all | solution.py:130
  23.7 1.4 %copy-start.3 = (bf16[8,2048]{1,0:T(8,128)(2,1)S(1)}, bf16[8,2048]{1,0:T(8,128)(2,1)}, u32[]{:S(2)}) copy-start(bf16[8,2048]{1,0:T(8,128)(2,1)} %param.19) | copy-start | bytes 98308
  23.7 1.4 %copy-start.9 = (s32[8]{0:T(128)S(1)}, s32[8]{0:T(128)}, u32[]{:S(2)}) copy-start(s32[8]{0:T(128)} %param.25) | copy-start | bytes 100
  23.7 1.6 %copy-start.7 = (bf16[8,128]{1,0:T(8,128)(2,1)S(1)}, bf16[8,128]{1,0:T(8,128)(2,1)}, u32[]{:S(2)}) copy-start(bf16[8,128]{1,0:T(8,128)(2,1)} %param.23) | copy-start | bytes 6148
  23.7 2.4 %copy-start.2 = (bf16[2048,128]{1,0:T(8,128)(2,1)S(1)}, bf16[2048,128]{1,0:T(8,128)(2,1)}, u32[]{:S(2)}) copy-start(bf16[2048,128]{1,0:T(8,128)(2,1)} %param.20) | copy-start | bytes 1572868
  23.8 2.4 %copy-start.6 = (f32[1,2048]{1,0:T(1,128)S(1)}, f32[1,2048]{1,0:T(1,128)}, u32[]{:S(2)}) copy-start(f32[1,2048]{1,0:T(1,128)} %param.21) | copy-start | bytes 24580
  26.5 27.2 %copy-start.10 = (bf16[1,2048,256]{2,1,0:T(8,128)(2,1)S(1)}, bf16[1,2048,256]{2,1,0:T(8,128)(2,1)}, u32[]{:S(2)}) copy-start(bf16[1,2048,256]{2,1,0:T(8,128)(2,1)} %param.17) | copy-start | bytes 3145732
  57.9 4.4 %copy-start.5 = (s32[16,8]{0,1:T(8,128)S(1)}, s32[16,8]{0,1:T(8,128)}, u32[]{:S(2)}) copy-start(s32[16,8]{0,1:T(8,128)} %param.15) | copy-start | bytes 1540
  57.9 18.0 %all-to-all-start.1 = ((bf16[4,256,512]{2,1,0:T(8,128)(2,1)}), bf16[4,256,512]{2,1,0:T(8,128)(2,1)S(1)}, u32[]{:S(2)}, u32[]{:S(2)}) async-start(bf16[4,256,512]{2,1,0:T(8,128)(2,1)} %fusion.9), calls=%async_computation.1 | async-start | bytes 2097152 | tf_op jit(solution)/shard_map/all_to_all | solution.py:141
  63.9 20.7 %copy-start.8 = (bf16[8,128]{1,0:T(8,128)(2,1)S(1)}, bf16[8,128]{1,0:T(8,128)(2,1)}, u32[]{:S(2)}) copy-start(bf16[8,128]{1,0:T(8,128)(2,1)} %param.24) | copy-start | bytes 6148
  76.9 22.4 %all-to-all-start.2 = ((bf16[128,2,512]{2,1,0:T(2,128)(2,1)}), bf16[128,2,512]{2,1,0:T(2,128)(2,1)S(1)}, u32[]{:S(2)}, u32[]{:S(2)}) async-start(bf16[128,2,512]{2,1,0:T(2,128)(2,1)} %reshape.451), calls=%async_computation.2 | async-start | bytes 524288 | tf_op jit(solution)/shard_map/all_to_all | solution.py:144
  100.3 8.9 %all-to-all-start.3 = ((bf16[4,16,512]{2,1,0:T(8,128)(2,1)}), bf16[4,16,512]{2,1,0:T(8,128)(2,1)S(1)}, u32[]{:S(2)}, u32[]{:S(2)}) async-start(bf16[4,16,512]{2,1,0:T(8,128)(2,1)} %convolution_convert_fusion.2), calls=%async_computation.3 | async-start | bytes 131072 | tf_op jit(solution)/shard_map/all_to_all | solution.py:159
